TPU v7x, 128 devices: a whole 4x4x4 slice. The times are simulated.
128 devices in a mesh: sec: 2 (over y_hi), seq: 8 (over x, core), trk: 8 (over y_lo, z).
Axes of the slice: x: 4, y: 4 (y_hi: 2, y_lo: 2; y = y_hi * 2 + y_lo), z: 4, core: 2. Of those that a mesh axis runs over, the one named last changes fastest.
Arguments:
- tokens: bfloat16 [8, 512, 1536], P('sec', 'seq'), may hold values from -6 to 6
- norm_gain: bfloat16 [1536], replicated, may hold values from 0.25 to 1.75
- dilated_conv_weight: bfloat16 [1536, 3, 1536], P(None, None, 'trk'), may hold values from -0.09375 to 0.09375
- head_weight: bfloat16 [1536, 8, 20, 128], P(None, 'trk'), may hold values from -0.15625 to 0.15625
- targets: bfloat16 [8, 512, 8, 20, 128], P('sec', 'seq', 'trk'), may hold values from 0 to 2
- owner_tiles: int32 [8, 20], P('trk'), may hold values from -1 to 80, as said below
- species: int32 [8], P('sec'), may hold values from 0 to 1, as said below
Outputs:
- conv_grad: float32 [1536, 3, 1536], P(('sec', 'seq'), None, 'trk')
- head_grad: float32 [1536, 8, 20, 128], P(('sec', 'seq'), 'trk')
Inputs may be any that keep to these rules, and one draw needn't show every extreme that they name: `owner_tiles`: each of the 81 tiles (human tiles 0 to 59, then the mouse tiles) stands in exactly one slot of one owner; -1 marks an empty slot; in every draw one owner has all 20 slots filled. `species`: 0 is human, 1 is mouse; exactly half of the samples are mouse.
All inputs are finite; a program needn't handle non-finite values.
Results may differ from a plain program's by a relative error of at most 0.0023.
Values may be sent and summed in bfloat16 or wider, within the bound.
No kernel may reach another device: no remote copies, remote signals or barrier semaphores. Data moves between devices by JAX's collectives and lax.ppermute only.
A program may use at most 128 MiB of HBM per device.

v0:
```python
import math

import jax
import jax.numpy as jnp
from jax import lax
from jax.sharding import PartitionSpec as P

HTRACKS = 7611
MTRACKS = 2608
DILATION_BINS = 16
HTILES = 60


grad_clip = 0.1


def padded(cells, sides, width):
    for axis, dim in sides:
        count = lax.axis_size(axis)
        ends = count - 1
        head = lax.slice_in_dim(cells, 0, width, axis=dim)
        tail = lax.slice_in_dim(cells, cells.shape[dim] - width, cells.shape[dim], axis=dim)
        cells = jnp.concatenate(
            [
                lax.ppermute(tail, axis, [(i, (i + 1) % count) for i in range(ends)]),
                cells,
                lax.ppermute(head, axis, [((i + 1) % count, i) for i in range(ends)]),
            ],
            axis=dim,
        )
    return cells


def contracted_rows(left, right):
    return lax.dot_general(
        left, right, (((0,), (0,)), ((), ())), preferred_element_type=jnp.float32
    )


def body(tokens, norm_gain, dilated_conv_weight, head_weight, targets, owner_tiles, species):
    sample_count = tokens.shape[0]
    local_rows = tokens.shape[1]
    width_all = tokens.shape[2]
    tap_count = dilated_conv_weight.shape[1]
    out_share = dilated_conv_weight.shape[2]
    slot_count = head_weight.shape[2]
    lane_count = head_weight.shape[3]
    inputs = tokens.astype(jnp.float32)
    mean_sq = jnp.mean(inputs * inputs, axis=-1, keepdims=True)
    normed = inputs * lax.rsqrt(mean_sq + 1e-06) * norm_gain.astype(jnp.float32)
    hidden_state = jax.nn.gelu(normed).astype(jnp.bfloat16)
    padded_input = padded(hidden_state, (("seq", 1),), DILATION_BINS)
    convolution_output = jnp.zeros((sample_count, local_rows, out_share), jnp.float32)
    for kernel_tap_index in range(tap_count):
        convolution_output = convolution_output + jnp.dot(
            padded_input[
                :, kernel_tap_index * DILATION_BINS : kernel_tap_index * DILATION_BINS + local_rows
            ],
            dilated_conv_weight[:, kernel_tap_index, :],
            preferred_element_type=jnp.float32,
        )
    own_cols = lax.dynamic_slice_in_dim(inputs, lax.axis_index("trk") * out_share, out_share, 2)
    mixed_share = (own_cols + convolution_output).astype(jnp.bfloat16)
    mixed_all = lax.all_gather(mixed_share, "trk", axis=2, tiled=True)
    tiles_here = owner_tiles[0]
    is_mouse = tiles_here >= HTILES
    within = jnp.where(is_mouse, tiles_here - HTILES, tiles_here)
    track_limit = jnp.where(is_mouse, MTRACKS, HTRACKS).astype(jnp.int32)
    lane_ids = jnp.arange(lane_count, dtype=jnp.int32)
    lane_mask = (within[:, None] * lane_count + lane_ids[None, :] < track_limit[:, None]).astype(
        jnp.float32
    )
    grad_scale = 1.0 / math.sqrt(
        lax.axis_size("sec") * sample_count * lax.axis_size("seq") * local_rows
    )
    weights_here = head_weight[:, 0]
    delta_list = []
    back_list = []
    for sample_input in range(sample_count):
        active_int = ((tiles_here >= 0) & (is_mouse == (species[sample_input] == 1))).astype(
            jnp.int32
        )
        slot_order = jnp.argsort(1 - active_int, stable=True)
        live_count = jnp.sum(active_int)
        mixed_here = mixed_all[sample_input]
        target_here = targets[sample_input, :, 0]

        def slot_step(position, loop_state):
            deltas, back_sum = loop_state
            slot_index = slot_order[position]
            column_w = lax.dynamic_index_in_dim(weights_here, slot_index, 1, keepdims=False)
            logits = jnp.dot(mixed_here, column_w, preferred_element_type=jnp.float32)
            target_cols = lax.dynamic_index_in_dim(
                target_here, slot_index, 1, keepdims=False
            ).astype(jnp.float32)
            mask_row = lax.dynamic_index_in_dim(lane_mask, slot_index, 0, keepdims=False)
            delta_f = (
                grad_scale
                * (jax.nn.softplus(logits) - target_cols)
                * jax.nn.sigmoid(logits)
                * mask_row[None, :]
            )
            delta_b = delta_f.astype(jnp.bfloat16)
            deltas = lax.dynamic_update_index_in_dim(deltas, delta_b, slot_index, 1)
            back_sum = back_sum + lax.dot_general(
                delta_b, column_w, (((1,), (1,)), ((), ())), preferred_element_type=jnp.float32
            )
            return (deltas, back_sum)

        start_state = (
            jnp.zeros((local_rows, slot_count, lane_count), jnp.bfloat16),
            jnp.zeros((local_rows, width_all), jnp.float32),
        )
        deltas_one, back_one = lax.fori_loop(0, live_count, slot_step, start_state)
        delta_list.append(deltas_one)
        back_list.append(back_one)
    deltas = jnp.stack(delta_list)
    back_sum = jnp.stack(back_list)
    backward_portion = lax.psum_scatter(back_sum, "trk", scatter_dimension=2, tiled=True).astype(
        jnp.bfloat16
    )
    group_count = lax.axis_size("sec") * lax.axis_size("seq")
    share_rows = width_all // group_count
    per_tap = [
        lax.dot_general(
            padded_input[
                :, kernel_tap_index * DILATION_BINS : kernel_tap_index * DILATION_BINS + local_rows
            ],
            backward_portion,
            (((0, 1), (0, 1)), ((), ())),
            preferred_element_type=jnp.float32,
        )
        for kernel_tap_index in range(tap_count)
    ]
    conv_grad = lax.psum_scatter(
        jnp.stack(per_tap, axis=1), ("sec", "seq"), scatter_dimension=0, tiled=True
    )
    flat_mixed = mixed_all.reshape(sample_count * local_rows, width_all)
    flat_deltas = deltas.reshape(sample_count * local_rows, slot_count * lane_count)
    whole_sum = lax.psum(contracted_rows(flat_mixed, flat_deltas), ("sec", "seq"))
    total_sq = lax.psum(jnp.sum(whole_sum * whole_sum), "trk")
    grad_share = lax.dynamic_slice_in_dim(
        whole_sum, lax.axis_index(("sec", "seq")) * share_rows, share_rows, 0
    )
    entries = width_all * lax.axis_size("trk") * slot_count * lane_count
    factor = jnp.minimum(1.0, grad_clip * lax.rsqrt(total_sq / entries + 1e-06))
    head_grad = (grad_share * factor).reshape(share_rows, 1, slot_count, lane_count)
    return (conv_grad, head_grad)


def solution(mesh):
    return jax.shard_map(
        body,
        mesh=mesh,
        in_specs=(
            P("sec", "seq", None),
            P(),
            P(None, None, "trk"),
            P(None, "trk", None, None),
            P("sec", "seq", "trk", None, None),
            P("trk", None),
            P("sec"),
        ),
        out_specs=(P(("sec", "seq"), None, "trk"), P(("sec", "seq"), "trk", None, None)),
        check_vma=False,
    )
```

profile of v0, /device:TPU:0, one launch (start us, length us, event | category | flops | bytes accessed | tf_op | source)
XLA Modules:
  0.0 716.9 jit_solution(8282968039042155935)
XLA Ops:
  7.2 1.4 multiply_reduce_fusion.1
  9.4 1.8 fusion.63
  12.0 2.0 collective-permute-start
  14.0 1.3 collective-permute-start.1
  18.5 1.4 fusion.72
  21.7 1.7 sort.59
  23.4 1.7 sort.60
  25.1 1.7 sort.61
  26.7 1.7 sort.62
  28.5 1.6 fusion.70
  30.1 1.6 fusion.69
  31.8 33.5 %all_gather.3 = bf16[4,64,1536]{1,0,2:T(4,128)(2,1)S(1)} all-gather(bf16[4,64,192]{1,0,2:T(4,128)(2,1)S(1)} %copy.23), channel_id=1, replica_groups=mesh['sec'=2,'seq'=8,'trk'=8] {'trk'}, dimensions={2}, use_global_device_ids=true | all-gather | bytes 884736 | tf_op jit(solution)/shard_map/all_gather | solution.py:64
  67.2 34.5 %while.48 = (s32[]{:T(128)}, bf16[64,20,128]{2,0,1:T(8,128)(2,1)S(1)}, f32[64,1536]{1,0:T(8,128)S(1)}, s32[]{:T(128)}, s32[20]{0:T(128)S(1)}, /*index=5*/bf16[15...) while((s32[]{:T(128)}, ...), condition=%wide.region_4.5_spmd, body=%wide.region_3.4_spmd.sunk | while | flops 50552840 | bytes 1837781 | solution.py:114
  71.6 1.3 convolution_add_fusion.9
  77.2 1.3 convolution_add_fusion.9
  82.9 1.3 convolution_add_fusion.9
  88.5 1.3 convolution_add_fusion.9
  94.2 1.3 convolution_add_fusion.9
  99.9 1.3 convolution_add_fusion.9
  102.4 80.5 %while.51 = (s32[]{:T(128)}, bf16[64,20,128]{2,0,1:T(8,128)(2,1)S(1)}, f32[64,1536]{1,0:T(8,128)S(1)}, s32[]{:T(128)}, s32[20]{0:T(128)S(1)}, /*index=5*/bf16[15...) while((s32[]{:T(128)}, ...), condition=%wide.region_16.17_spmd, body=%wide.region_15.16_spmd.sunk | while | flops 50552840 | bytes 1837781 | solution.py:114
  106.9 1.3 convolution_add_fusion.12
  112.6 1.3 convolution_add_fusion.12
  118.3 1.3 convolution_add_fusion.12
  124.0 1.3 convolution_add_fusion.12
  129.7 1.3 convolution_add_fusion.12
  141.1 1.3 convolution_add_fusion.12
  158.2 1.3 convolution_add_fusion.12
  175.3 1.3 convolution_add_fusion.12
  183.7 80.3 %while.50 = (s32[]{:T(128)}, bf16[64,20,128]{2,0,1:T(8,128)(2,1)S(1)}, f32[64,1536]{1,0:T(8,128)S(1)}, s32[]{:T(128)}, s32[20]{0:T(128)S(1)}, /*index=5*/bf16[15...) while((s32[]{:T(128)}, ...), condition=%wide.region_12.13_spmd, body=%wide.region_11.12_spmd.sunk | while | flops 50552840 | bytes 1837781 | solution.py:114
  193.9 1.3 convolution_add_fusion.11
  205.2 1.3 convolution_add_fusion.11
  216.6 1.3 convolution_add_fusion.11
  228.0 1.3 convolution_add_fusion.11
  239.4 1.3 convolution_add_fusion.11
  250.8 1.3 convolution_add_fusion.11
  262.2 1.3 convolution_add_fusion.11
  264.9 80.4 %while.49 = (s32[]{:T(128)}, bf16[64,20,128]{2,0,1:T(8,128)(2,1)S(1)}, f32[64,1536]{1,0:T(8,128)S(1)}, s32[]{:T(128)}, s32[20]{0:T(128)S(1)}, /*index=5*/bf16[15...) while((s32[]{:T(128)}, ...), condition=%wide.region_8.9_spmd, body=%wide.region_7.8_spmd.sunk | while | flops 50552840 | bytes 1837781 | solution.py:114
  275.0 1.3 convolution_add_fusion.10
  280.7 1.3 convolution_add_fusion.10
  286.4 1.3 convolution_add_fusion.10
  292.1 1.3 convolution_add_fusion.10
  297.8 1.3 convolution_add_fusion.10
  303.5 1.3 convolution_add_fusion.10
  309.2 1.3 convolution_add_fusion.10
  314.9 1.3 convolution_add_fusion.10
  320.6 1.3 convolution_add_fusion.10
  326.3 1.3 convolution_add_fusion.10
  332.0 1.3 convolution_add_fusion.10
  337.7 1.3 convolution_add_fusion.10
  343.4 1.3 convolution_add_fusion.10
  345.3 1.3 pad_maximum_fusion.1
  346.6 4.1 copy.32
  350.7 4.2 reshape.71
  355.0 39.4 %reduce-scatter.7.cloned.1.call-done = f32[192,256]{1,0:T(8,128)} async-done(((f32[1536,256]{1,0:T(8,128)}), f32[192,256]{1,0:T(8,128)}) %reduce-scatter.7.cloned.1.call-update) | async-done | bytes 196624
  396.0 1.3 convolution_bitcast_fusion.4
  397.3 1.3 convolution_bitcast_fusion.6
  398.8 3.1 copy.36
  404.5 8.1 %fusion.64 = f32[1536,2560]{1,0:T(8,128)} fusion(bf16[256,1536]{1,0:T(8,128)(2,1)S(1)} %bitcast.262, bf16[32,8,20,128]{3,2,1,0:T(8,128)(2,1)S(1)} %bitcast.263), kind=kOutput, calls=%fused_computation.84 | convolution fusion | flops 2013265920 | bytes 17825792 | tf_op jit(solution)/shard_map/dot_general | solution.py:35
  412.6 67.1 %reduce-scatter.9.cloned.1.call-done = f32[96,576]{1,0:T(8,128)} async-done(((f32[1536,576]{1,0:T(8,128)}), f32[96,576]{1,0:T(8,128)}) %reduce-scatter.9.cloned.1.call-update) | async-done | bytes 221200
  480.8 194.9 %all-reduce.2.cloned.1.call-done = f32[1536,2560]{1,0:T(8,128)} async-done(((f32[1536,2560]{1,0:T(8,128)}), f32[1536,2560]{1,0:T(8,128)}) %all-reduce.2.cloned.1.call-update) | async-done | bytes 15728656 | tf_op jit(solution)/shard_map/psum | solution.py:140
  675.7 10.1 %multiply_reduce_fusion = f32[]{:T(128)} fusion(f32[1536,2560]{1,0:T(8,128)} %all-reduce.2.cloned.1.call-done), kind=kLoop, calls=%fused_computation.68 | loop fusion | flops 7864319 | bytes 15728644 | tf_op jit(solution)/shard_map/reduce_sum | solution.py:141
  686.7 19.5 %psum.15 = f32[]{:T(128)} all-reduce(f32[]{:T(128)} %multiply_reduce_fusion), channel_id=1, replica_groups=mesh['sec'=2,'seq'=8,'trk'=8] {'trk'}, use_global_device_ids=true, to_apply=%region_21.22 | all-reduce | flops 1 | bytes 8 | tf_op jit(solution)/shard_map/psum | solution.py:141
  706.9 1.3 dynamic-slice_multiply_fusion
  708.2 2.1 reshape.70
  (225 shorter events, 120.9 us)
Async XLA Ops:
  7.2 8.1 %copy-start.2 = (bf16[4,64,1536]{2,1,0:T(8,128)(2,1)S(1)}, bf16[4,64,1536]{2,1,0:T(8,128)(2,1)}, u32[]{:S(2)}) copy-start(bf16[4,64,1536]{2,1,0:T(8,128)(2,1)} %param.15) | copy-start | bytes 2359300
  7.2 387.2 %reduce-scatter.7.cloned.1.call-start = ((), (), s32[]{:S(2)}) async-start(), calls=%async_computation.3 | async-start | bytes 1769472
  11.2 4.3 copy-start.12
  12.0 18.1 %collective-permute-start = (bf16[4,16,1536]{2,1,0:T(8,128)(2,1)}, bf16[4,16,1536]{2,1,0:T(8,128)(2,1)}, u32[]{:S(2)}, u32[]{:S(2)}) collective-permute-start(bf16[4,16,1536]{2,1,0:T(8,128)(2,1)} %get-tuple-element.350), channel_id=1, source_target_pairs={{0,8},{8,16},{16,24},{24,32},{32,40},{40,48},{48,56},{1,9},{9,17},... | collective-permute-start | bytes 589832 | tf_op jit(solution)/shard_map/ppermute | solution.py:25
  14.0 14.5 %collective-permute-start.1 = (bf16[4,16,1536]{2,1,0:T(8,128)(2,1)}, bf16[4,16,1536]{2,1,0:T(8,128)(2,1)}, u32[]{:S(2)}, u32[]{:S(2)}) collective-permute-start(bf16[4,16,1536]{2,1,0:T(8,128)(2,1)} %get-tuple-element.351), channel_id=1, source_target_pairs={{8,0},{16,8},{24,16},{32,24},{40,32},{48,40},{56,48},{9,1},{17,9},... | collective-permute-start | bytes 589832 | tf_op jit(solution)/shard_map/ppermute | solution.py:27
  15.5 4.5 copy-start.11
  20.0 1.0 copy-start.13
  66.2 0.9 copy-start
  101.7 0.7 copy-start.5
  182.9 0.7 copy-start.7
  264.1 0.7 copy-start.9
  345.3 1.3 copy-start.3
  354.9 124.8 %reduce-scatter.9.cloned.1.call-start = ((), (), s32[]{:S(2)}) async-start(), calls=%async_computation.4 | async-start | bytes 4177920
  401.9 1.0 copy-start.4
  401.9 1.1 copy-start.6
  401.9 1.2 copy-start.8
  401.9 1.3 copy-start.10
  402.0 273.8 %all-reduce.2.cloned.1.call-start = ((), (), s32[]{:S(2)}) async-start(), calls=%async_computation.2 | async-start | bytes 31457280 | tf_op jit(solution)/shard_map/psum | solution.py:140
  403.4 1.1 copy-start.1
Sparse Core Ops, SparseCore 0:
  355.0 39.3 reduce-scatter.6
  402.1 77.5 reduce-scatter.8
  482.2 193.4 all-reduce.1
where the time goes:
time: 723 us; the launch traced here: 717 us
  waiting for transfers between devices  301 us (42%)
  matrix products  136 us (19%)
  loops' own time  127 us (18%)
  local copies, waits for them, and re-layouts  54.3 us (8%)
  blocking collectives  53 us (7%)
  other arithmetic  24.7 us (3%)
  between operations  17.2 us (2%)
    psum x1, waiting for transfers between devices, body(): lax.psum(contracted_rows(flat_mixed, flat_deltas), ('sec', 'seq'))  195 us
    another operation x4, loops' own time, body(): deltas_one, back_one = lax.fori_loop(0, live_count, slot_step, start_state)  127 us
    unnamed x5, waiting for transfers between devices  107 us
    dot_general x48, matrix products, slot_step(): lax.dot_general(delta_b, column_w, (((1,), (1,)), ((), ())), preferred_el...  60.8 us
    dot_general x48, matrix products, slot_step(): logits = jnp.dot(mixed_here, column_w, preferred_element_type=jnp.float32)  59.7 us
    all_gather x1, blocking collectives, body(): mixed_all = lax.all_gather(mixed_share, 'trk', axis=2, tiled=True)  33.5 us
    dynamic_slice x48, local copies, waits for them, and re-layouts, slot_step(): slot_index = slot_order[position]  28.2 us
    psum x1, blocking collectives, body(): total_sq = lax.psum(jnp.sum(whole_sum * whole_sum), 'trk')  19.5 us
  transfers between devices with their start and end apart: 5, of which 3 were waited for; matrix products, arithmetic and copies ran while one was open for 3% of the time, Pallas kernels for 0%

commit v1 on v0

--- a/solution.py
+++ b/solution.py
@@ -73,49 +73,26 @@
     grad_scale = 1.0 / math.sqrt(
         lax.axis_size("sec") * sample_count * lax.axis_size("seq") * local_rows
     )
-    weights_here = head_weight[:, 0]
-    delta_list = []
-    back_list = []
-    for sample_input in range(sample_count):
-        active_int = ((tiles_here >= 0) & (is_mouse == (species[sample_input] == 1))).astype(
-            jnp.int32
-        )
-        slot_order = jnp.argsort(1 - active_int, stable=True)
-        live_count = jnp.sum(active_int)
-        mixed_here = mixed_all[sample_input]
-        target_here = targets[sample_input, :, 0]
-
-        def slot_step(position, loop_state):
-            deltas, back_sum = loop_state
-            slot_index = slot_order[position]
-            column_w = lax.dynamic_index_in_dim(weights_here, slot_index, 1, keepdims=False)
-            logits = jnp.dot(mixed_here, column_w, preferred_element_type=jnp.float32)
-            target_cols = lax.dynamic_index_in_dim(
-                target_here, slot_index, 1, keepdims=False
-            ).astype(jnp.float32)
-            mask_row = lax.dynamic_index_in_dim(lane_mask, slot_index, 0, keepdims=False)
-            delta_f = (
-                grad_scale
-                * (jax.nn.softplus(logits) - target_cols)
-                * jax.nn.sigmoid(logits)
-                * mask_row[None, :]
-            )
-            delta_b = delta_f.astype(jnp.bfloat16)
-            deltas = lax.dynamic_update_index_in_dim(deltas, delta_b, slot_index, 1)
-            back_sum = back_sum + lax.dot_general(
-                delta_b, column_w, (((1,), (1,)), ((), ())), preferred_element_type=jnp.float32
-            )
-            return (deltas, back_sum)
-
-        start_state = (
-            jnp.zeros((local_rows, slot_count, lane_count), jnp.bfloat16),
-            jnp.zeros((local_rows, width_all), jnp.float32),
-        )
-        deltas_one, back_one = lax.fori_loop(0, live_count, slot_step, start_state)
-        delta_list.append(deltas_one)
-        back_list.append(back_one)
-    deltas = jnp.stack(delta_list)
-    back_sum = jnp.stack(back_list)
+    weights_here = head_weight[:, 0].reshape(width_all, slot_count * lane_count)
+    flat_mixed = mixed_all.reshape(sample_count * local_rows, width_all)
+    logits = jnp.dot(flat_mixed, weights_here, preferred_element_type=jnp.float32)
+    target_cols = targets[:, :, 0].reshape(sample_count * local_rows, slot_count * lane_count)
+    active = (tiles_here[None, :] >= 0) & (is_mouse[None, :] == (species[:, None] == 1))
+    live_mask = active.astype(jnp.float32)[:, :, None] * lane_mask[None, :, :]
+    live_rows = jnp.broadcast_to(
+        live_mask.reshape(sample_count, 1, slot_count * lane_count),
+        (sample_count, local_rows, slot_count * lane_count),
+    ).reshape(sample_count * local_rows, slot_count * lane_count)
+    delta_f = (
+        grad_scale
+        * (jax.nn.softplus(logits) - target_cols.astype(jnp.float32))
+        * jax.nn.sigmoid(logits)
+        * live_rows
+    )
+    flat_deltas = delta_f.astype(jnp.bfloat16)
+    back_sum = lax.dot_general(
+        flat_deltas, weights_here, (((1,), (1,)), ((), ())), preferred_element_type=jnp.float32
+    ).reshape(sample_count, local_rows, width_all)
     backward_portion = lax.psum_scatter(back_sum, "trk", scatter_dimension=2, tiled=True).astype(
         jnp.bfloat16
     )
@@ -135,13 +112,10 @@
     conv_grad = lax.psum_scatter(
         jnp.stack(per_tap, axis=1), ("sec", "seq"), scatter_dimension=0, tiled=True
     )
-    flat_mixed = mixed_all.reshape(sample_count * local_rows, width_all)
-    flat_deltas = deltas.reshape(sample_count * local_rows, slot_count * lane_count)
-    whole_sum = lax.psum(contracted_rows(flat_mixed, flat_deltas), ("sec", "seq"))
-    total_sq = lax.psum(jnp.sum(whole_sum * whole_sum), "trk")
-    grad_share = lax.dynamic_slice_in_dim(
-        whole_sum, lax.axis_index(("sec", "seq")) * share_rows, share_rows, 0
+    grad_share = lax.psum_scatter(
+        contracted_rows(flat_mixed, flat_deltas), ("sec", "seq"), scatter_dimension=0, tiled=True
     )
+    total_sq = lax.psum(jnp.sum(grad_share * grad_share), ("sec", "seq", "trk"))
     entries = width_all * lax.axis_size("trk") * slot_count * lane_count
     factor = jnp.minimum(1.0, grad_clip * lax.rsqrt(total_sq / entries + 1e-06))
     head_grad = (grad_share * factor).reshape(share_rows, 1, slot_count, lane_count)

time: 723 us -> 436 us (0.60)
  loops' own time: 127 us -> 0 us
  matrix products: 136 us -> 25.1 us
  waiting for transfers between devices: 301 us -> 252 us
  blocking collectives: 53 us -> 97.6 us
  local copies, waits for them, and re-layouts: 54.3 us -> 34.3 us
  other arithmetic: 24.7 us -> 7.97 us
    psum x1 -> x0, waiting for transfers between devices: 195 us -> none  [body(): lax.psum(contracted_rows(flat_mixed, flat_deltas), ('sec', 'seq'))]
    reduce_scatter x0 -> x1, waiting for transfers between devices: none -> 140 us  [body(): lax.psum_scatter(contracted_rows(flat_mixed, flat_deltas), ('sec', 'seq')...]
    another operation x4 -> x0, loops' own time: 127 us -> none  [body(): deltas_one, back_one = lax.fori_loop(0, live_count, slot_step, start_state)]
    dot_general x96 -> x2, matrix products: 121 us -> 13.9 us  [the longest x1 8.46 us: body(): jnp.dot(flat_mixed, weights_here, preferred_element_type=jnp.float32)]
    psum x1, blocking collectives: 19.5 us -> 63.9 us  [body(): total_sq = lax.psum(jnp.sum(grad_share * grad_share), ('sec', 'seq', 'trk'))]
    dynamic_slice x48 -> x0, local copies, waits for them, and re-layouts: 28.2 us -> none  [slot_step(): slot_index = slot_order[position]]
    reduce_sum x1, other arithmetic: 10.1 us -> 2.14 us  [body(): total_sq = lax.psum(jnp.sum(grad_share * grad_share), ('sec', 'seq', 'trk'))]
    unnamed x35 -> x25, local copies, waits for them, and re-layouts: 18.7 us -> 26.4 us
  transfers between devices with their start and end apart: 5 -> 5, of which waited for: 3 -> 3; matrix products, arithmetic and copies ran while one was open for 3% -> 6% of each run, Pallas kernels for 0% -> 0%
where the time goes in v1:
time: 436 us; the launch traced here: 435 us
  waiting for transfers between devices  252 us (58%)
  blocking collectives  97.6 us (22%)
  local copies, waits for them, and re-layouts  34.3 us (8%)
  matrix products  25.1 us (6%)
  between operations  14.7 us (3%)
  other arithmetic  7.97 us (2%)
    reduce_scatter x1, waiting for transfers between devices, body(): lax.psum_scatter(contracted_rows(flat_mixed, flat_deltas), ('sec', 'seq')...  140 us
    unnamed x5, waiting for transfers between devices  113 us
    psum x1, blocking collectives, body(): total_sq = lax.psum(jnp.sum(grad_share * grad_share), ('sec', 'seq', 'trk'))  63.9 us
    all_gather x1, blocking collectives, body(): mixed_all = lax.all_gather(mixed_share, 'trk', axis=2, tiled=True)  33.7 us
    unnamed x25, local copies, waits for them, and re-layouts  26.4 us
  transfers between devices with their start and end apart: 5, of which 3 were waited for; matrix products, arithmetic and copies ran while one was open for 6% of the time, Pallas kernels for 0%

profile of v1, /device:TPU:0, one launch (start us, length us, event | category | flops | bytes accessed | tf_op | source)
XLA Modules:
  0.0 434.8 jit_solution(13732311764783962784)
XLA Ops:
  7.2 0.0 copy-start.2
  7.2 0.0 copy-start.7
  7.2 0.0 reduce-scatter.10.cloned.1.call-start
  7.2 1.4 multiply_reduce_fusion
  8.7 0.7 convert_element_type.39
  9.4 1.8 fusion.12
  11.2 0.8 fusion.33
  12.0 1.3 collective-permute-start
  13.3 1.3 collective-permute-start.1
  14.6 0.0 copy-done.7
  14.6 0.0 copy-done.2
  14.6 0.2 convert_element_type.38
  14.8 0.7 broadcast_compare_fusion
  15.5 0.1 and_convert_fusion
  15.6 0.1 broadcast_bitcast_fusion
  15.6 3.8 copy.26
  19.5 10.6 %copy.25 = bf16[1536,1,20,128]{0,3,2,1:T(8,128)(2,1)} copy(bf16[1536,1,20,128]{3,0,2,1:T(8,128)(2,1)} %param.10) | data formatting | bytes 15728640 | tf_op args[3]
  30.1 0.0 copy-start.6
  30.1 0.1 broadcast_reduce_fusion
  30.2 0.6 bitcast_multiply_fusion
  30.9 1.4 fusion.18
  32.3 0.0 collective-permute-done.1
  32.3 0.0 copy-done.6
  32.3 0.4 fusion.16
  32.7 0.0 collective-permute-done
  32.7 0.4 fusion.15
  33.1 0.2 copy.23
  33.3 33.7 %all_gather.3 = bf16[4,64,1536]{1,0,2:T(4,128)(2,1)S(1)} all-gather(bf16[4,64,192]{1,0,2:T(4,128)(2,1)S(1)} %copy.23), channel_id=1, replica_groups=mesh['sec'=2,'seq'=8,'trk'=8] {'trk'}, dimensions={2}, use_global_device_ids=true | all-gather | bytes 884736 | tf_op jit(solution)/shard_map/all_gather | solution.py:64
  67.0 0.9 copy.24
  68.0 0.0 copy-start
  68.0 8.5 %fusion.4 = bf16[256,2560]{1,0:T(8,128)(2,1)S(1)} fusion(f32[32,8,20,128]{3,2,1,0:T(8,128)} %bitcast.78, f32[4,2560]{1,0:T(4,128)} %bitcast_multiply_fusion, bf16[256,1536]{1,0:T(8,128)(2,1)S(1)} %bitcast.79, bf16[1536,2560]{0,1:T(8,128)(2,1)} %bitcast.74), kind=kOutput, calls=%fused_computation.6 | convolution fusion | flops 2022440960 | bytes 12623872 | tf_op jit(solution)/shard_map/dot_general | solution.py:78
  76.5 0.0 copy-done
  76.5 0.0 copy-start.3
  76.5 1.2 copy-done.3
  77.6 5.4 %fusion.34 = f32[4,64,1536]{2,1,0:T(8,128)S(1)} fusion(bf16[4,64,2560]{2,1,0:T(8,128)(2,1)S(1)} %bitcast.81, bf16[1536,2560,1]{0,1,2:T(8,128)(2,1)} %bitcast.75), kind=kOutput, calls=%fused_computation.59 | convolution fusion | flops 2013265920 | bytes 10747904 | tf_op jit(solution)/shard_map/dot_general | solution.py:93
  83.1 2.7 copy.32
  85.8 4.2 reshape.148
  90.0 0.0 reduce-scatter.10.cloned.1.call-update
  90.0 0.0 reduce-scatter.12.cloned.1.call-start
  90.1 44.6 %reduce-scatter.10.cloned.1.call-done = f32[192,256]{1,0:T(8,128)} async-done(((f32[1536,256]{1,0:T(8,128)}), f32[192,256]{1,0:T(8,128)}) %reduce-scatter.10.cloned.1.call-update) | async-done | bytes 196624
  134.6 1.1 reshape.149
  135.7 0.1 copy.33
  135.9 0.4 convolution_bitcast_fusion.1
  136.2 0.4 convolution_bitcast_fusion
  136.6 0.4 convolution_bitcast_fusion.2
  136.9 0.2 pad_maximum_fusion
  137.2 3.1 copy.36
  140.3 0.0 copy-start.1
  140.3 0.0 copy-start.4
  140.3 0.0 reduce-scatter.12.cloned.1.call-update
  140.3 0.2 reduce-scatter.8.cloned.1.call-start
  140.6 0.9 copy-done.1
  141.4 0.4 copy-done.4
  141.9 8.0 %fusion.35 = f32[1536,2560]{1,0:T(8,128)} fusion(bf16[256,1536]{1,0:T(8,128)(2,1)S(1)} %bitcast.80, bf16[256,2560]{1,0:T(8,128)(2,1)S(1)} %copy-done.4), kind=kOutput, calls=%fused_computation.60 | convolution fusion | flops 2013265920 | bytes 17825792 | tf_op jit(solution)/shard_map/dot_general | solution.py:35
  149.8 0.0 reduce-scatter.8.cloned.1.call-update
  149.8 68.1 %reduce-scatter.12.cloned.1.call-done = f32[96,576]{1,0:T(8,128)} async-done(((f32[1536,576]{1,0:T(8,128)}), f32[96,576]{1,0:T(8,128)}) %reduce-scatter.12.cloned.1.call-update) | async-done | bytes 221200
  217.9 1.1 copy.37
  219.0 139.5 %reduce-scatter.8.cloned.1.call-done = f32[96,2560]{1,0:T(8,128)} async-done(((f32[1536,2560]{1,0:T(8,128)}), f32[96,2560]{1,0:T(8,128)}) %reduce-scatter.8.cloned.1.call-update) | async-done | bytes 983056 | tf_op jit(solution)/shard_map/reduce_scatter | solution.py:115
  358.5 2.1 multiply_reduce_fusion.1
  360.7 0.9 copy.28
  361.5 63.9 %psum.7 = f32[]{:T(128)} all-reduce(f32[]{:T(128)} %multiply_reduce_fusion.1), channel_id=1, replica_groups=mesh['sec'=2,'seq'=8,'trk'=8] {'sec','seq','trk'}, use_global_device_ids=true, to_apply=%region_5.6 | all-reduce | flops 1 | bytes 8 | tf_op jit(solution)/shard_map/psum | solution.py:118
  426.1 0.0 copy-done.5
  426.1 0.1 broadcast_multiply_fusion
  426.2 2.1 reshape.147
  (5 shorter events, 0.0 us)
Async XLA Ops:
  7.2 7.5 %copy-start.2 = (bf16[4,64,1536]{2,1,0:T(8,128)(2,1)S(1)}, bf16[4,64,1536]{2,1,0:T(8,128)(2,1)}, u32[]{:S(2)}) copy-start(bf16[4,64,1536]{2,1,0:T(8,128)(2,1)} %param.7) | copy-start | bytes 2359300
  7.2 7.4 %copy-start.7 = (s32[1,20]{1,0:T(1,128)S(1)}, s32[1,20]{1,0:T(1,128)}, u32[]{:S(2)}) copy-start(s32[1,20]{1,0:T(1,128)} %param.12) | copy-start | bytes 244
  7.2 127.5 %reduce-scatter.10.cloned.1.call-start = ((), (), s32[]{:S(2)}) async-start(), calls=%async_computation.4 | async-start | bytes 1769472
  12.0 20.7 %collective-permute-start = (bf16[4,16,1536]{2,1,0:T(8,128)(2,1)}, bf16[4,16,1536]{2,1,0:T(8,128)(2,1)S(1)}, u32[]{:S(2)}, u32[]{:S(2)}) collective-permute-start(bf16[4,16,1536]{2,1,0:T(8,128)(2,1)} %get-tuple-element.10), channel_id=1, source_target_pairs={{0,8},{8,16},{16,24},{24,32},{32,40},{40,48},{48,56},{1,9},{9,17},... | collective-permute-start | bytes 589832 | tf_op jit(solution)/shard_map/ppermute | solution.py:25
  13.3 19.0 %collective-permute-start.1 = (bf16[4,16,1536]{2,1,0:T(8,128)(2,1)}, bf16[4,16,1536]{2,1,0:T(8,128)(2,1)S(1)}, u32[]{:S(2)}, u32[]{:S(2)}) collective-permute-start(bf16[4,16,1536]{2,1,0:T(8,128)(2,1)} %get-tuple-element.11), channel_id=1, source_target_pairs={{8,0},{16,8},{24,16},{32,24},{40,32},{48,40},{56,48},{9,1},{17,9},... | collective-permute-start | bytes 589832 | tf_op jit(solution)/shard_map/ppermute | solution.py:27
  30.1 2.2 copy-start.6
  68.0 8.5 %copy-start = (bf16[4,64,1536]{2,1,0:T(8,128)(2,1)}, bf16[4,64,1536]{2,1,0:T(8,128)(2,1)S(1)}, u32[]{:S(2)}) copy-start(bf16[4,64,1536]{2,1,0:T(8,128)(2,1)S(1)} %copy.24) | copy-start | bytes 2359300
  76.5 1.2 copy-start.3
  90.0 127.9 %reduce-scatter.12.cloned.1.call-start = ((), (), s32[]{:S(2)}) async-start(), calls=%async_computation.5 | async-start | bytes 4177920
  140.3 1.1 copy-start.1
  140.3 1.6 copy-start.4
  140.3 218.2 %reduce-scatter.8.cloned.1.call-start = ((), (), s32[]{:S(2)}) async-start(), calls=%async_computation.3 | async-start | bytes 16711680 | tf_op jit(solution)/shard_map/reduce_scatter | solution.py:115
  358.5 67.6 %copy-start.5 = (f32[96,2560]{1,0:T(8,128)S(1)}, f32[96,2560]{1,0:T(8,128)}, u32[]{:S(2)}) copy-start(f32[96,2560]{1,0:T(8,128)} %reduce-scatter.8.cloned.1.call-done) | copy-start | bytes 2949124
Sparse Core Ops, SparseCore 0:
  90.1 44.4 reduce-scatter.9
  140.4 77.4 reduce-scatter.11
  222.3 136.1 reduce-scatter.7

commit v2 on v1

--- a/solution.py
+++ b/solution.py
@@ -61,7 +61,8 @@
         )
     own_cols = lax.dynamic_slice_in_dim(inputs, lax.axis_index("trk") * out_share, out_share, 2)
     mixed_share = (own_cols + convolution_output).astype(jnp.bfloat16)
-    mixed_all = lax.all_gather(mixed_share, "trk", axis=2, tiled=True)
+    mixed_parts = lax.all_gather(mixed_share, "trk", axis=0, tiled=False)
+    mixed_all = jnp.transpose(mixed_parts, (1, 2, 0, 3)).reshape(sample_count, local_rows, width_all)
     tiles_here = owner_tiles[0]
     is_mouse = tiles_here >= HTILES
     within = jnp.where(is_mouse, tiles_here - HTILES, tiles_here)
@@ -98,24 +99,30 @@
     )
     group_count = lax.axis_size("sec") * lax.axis_size("seq")
     share_rows = width_all // group_count
+    hidden_parts = lax.all_to_all(
+        padded_input.reshape(sample_count, local_rows + 2 * DILATION_BINS, group_count, share_rows),
+        ("sec", "seq"),
+        2,
+        0,
+        tiled=False,
+    )
+    back_parts = lax.all_gather(backward_portion, ("sec", "seq"), axis=0, tiled=False)
     per_tap = [
         lax.dot_general(
-            padded_input[
-                :, kernel_tap_index * DILATION_BINS : kernel_tap_index * DILATION_BINS + local_rows
-            ],
-            backward_portion,
-            (((0, 1), (0, 1)), ((), ())),
+            hidden_parts[
+                :, :, kernel_tap_index * DILATION_BINS : kernel_tap_index * DILATION_BINS + local_rows
+            ].reshape(group_count, sample_count, local_rows, share_rows),
+            back_parts,
+            (((0, 1, 2), (0, 1, 2)), ((), ())),
             preferred_element_type=jnp.float32,
         )
         for kernel_tap_index in range(tap_count)
     ]
-    conv_grad = lax.psum_scatter(
-        jnp.stack(per_tap, axis=1), ("sec", "seq"), scatter_dimension=0, tiled=True
-    )
+    conv_grad = jnp.stack(per_tap, axis=1)
     grad_share = lax.psum_scatter(
         contracted_rows(flat_mixed, flat_deltas), ("sec", "seq"), scatter_dimension=0, tiled=True
     )
-    total_sq = lax.psum(jnp.sum(grad_share * grad_share), ("sec", "seq", "trk"))
+    total_sq = lax.psum(lax.psum(lax.psum(jnp.sum(grad_share * grad_share), "trk"), "seq"), "sec")
     entries = width_all * lax.axis_size("trk") * slot_count * lane_count
     factor = jnp.minimum(1.0, grad_clip * lax.rsqrt(total_sq / entries + 1e-06))
     head_grad = (grad_share * factor).reshape(share_rows, 1, slot_count, lane_count)

time: 436 us -> 389 us (0.89)
  waiting for transfers between devices: 252 us -> 192 us
  matrix products: 25.1 us -> 32.5 us
  blocking collectives: 97.6 us -> 104 us
    unnamed x5 -> x4, waiting for transfers between devices: 113 us -> 45 us
    all_to_all x0 -> x1, blocking collectives: none -> 31.7 us  [body(): lax.all_to_all(padded_input.reshape(sample_count, local_rows + 2 * DILATI...]
    psum x1 -> x3, blocking collectives: 63.9 us -> 39.7 us  [the longest x1 19.6 us: body(): lax.psum(jnp.sum(grad_share * grad_share), 'trk')]
    all_gather x0 -> x1, waiting for transfers between devices: none -> 10.9 us  [body(): lax.all_gather(backward_portion, ('sec', 'seq'), axis=0, tiled=False)]
    dot_general x3, matrix products: 1.07 us -> 5.98 us  [body(): lax.dot_general(hidden_parts[:, :, kernel_tap_index * DILATION_BINS:kerne...]
    unnamed x25 -> x28, local copies, waits for them, and re-layouts: 26.4 us -> 21.8 us
    another operation x0 -> x3, local copies, waits for them, and re-layouts: none -> 4.48 us  [the longest x1 2.72 us: body(): flat_mixed = mixed_all.reshape(sample_count * local_rows, width_all)]
  transfers between devices with their start and end apart: 5 -> 5, of which waited for: 3 -> 3; matrix products, arithmetic and copies ran while one was open for 6% -> 8% of each run, Pallas kernels for 0% -> 0%
where the time goes in v2:
time: 389 us; the launch traced here: 388 us
  waiting for transfers between devices  192 us (49%)
  blocking collectives  104 us (27%)
  local copies, waits for them, and re-layouts  33 us (8%)
  matrix products  32.5 us (8%)
  between operations  14.7 us (4%)
  other arithmetic  9.92 us (3%)
    reduce_scatter x1, waiting for transfers between devices, body(): lax.psum_scatter(contracted_rows(flat_mixed, flat_deltas), ('sec', 'seq')...  136 us
    unnamed x4, waiting for transfers between devices  45 us
    all_gather x1, blocking collectives, body(): mixed_parts = lax.all_gather(mixed_share, 'trk', axis=0, tiled=False)  32.2 us
    all_to_all x1, blocking collectives, body(): lax.all_to_all(padded_input.reshape(sample_count, local_rows + 2 * DILATI...  31.7 us
    unnamed x28, local copies, waits for them, and re-layouts  21.8 us
    psum x1, blocking collectives, body(): lax.psum(jnp.sum(grad_share * grad_share), 'trk')  19.6 us
    psum x1, blocking collectives, body(): lax.psum(lax.psum(jnp.sum(grad_share * grad_share), 'trk'), 'seq')  13.1 us
    all_gather x1, waiting for transfers between devices, body(): lax.all_gather(backward_portion, ('sec', 'seq'), axis=0, tiled=False)  10.9 us
  transfers between devices with their start and end apart: 5, of which 3 were waited for; matrix products, arithmetic and copies ran while one was open for 8% of the time, Pallas kernels for 0%

profile of v2, /device:TPU:0, one launch (start us, length us, event | category | flops | bytes accessed | tf_op | source)
XLA Modules:
  0.0 388.1 jit_solution(2021800040342712282)
XLA Ops:
  7.2 0.0 copy-start.2
  7.2 0.0 copy-start.9
  7.2 0.0 reduce-scatter.7.cloned.1.call-start
  7.2 1.4 multiply_reduce_fusion
  8.7 0.7 convert_element_type.39
  9.4 1.8 fusion.12
  11.2 0.0 copy-start.5
  11.2 0.9 copy-done.5
  12.1 0.8 fusion.33
  12.9 1.3 collective-permute-start
  14.2 1.3 collective-permute-start.1
  15.5 0.0 copy-done.9
  15.5 0.0 copy-done.2
  15.5 1.4 convert_element_type.38
  16.9 0.0 copy-done.10
  16.9 0.1 and_convert_fusion
  17.0 0.7 broadcast_bitcast_fusion
  17.7 2.1 copy.21
  19.8 10.6 %copy.20 = bf16[1536,1,20,128]{0,3,2,1:T(8,128)(2,1)} copy(bf16[1536,1,20,128]{3,0,2,1:T(8,128)(2,1)} %param.10) | data formatting | bytes 15728640 | tf_op args[3]
  30.4 0.1 broadcast_reduce_fusion
  30.6 1.5 bitcast_multiply_fusion
  32.1 1.7 fusion.23
  33.8 0.0 collective-permute-done.1
  33.8 0.0 copy-done.6
  33.8 1.4 fusion.19
  35.2 0.0 collective-permute-done
  35.2 1.6 fusion.15
  36.8 32.2 %all-gather = bf16[32,64,192]{2,1,0:T(8,128)(2,1)S(1)} all-gather(bf16[4,64,192]{2,1,0:T(8,128)(2,1)S(1)} %fusion.15), channel_id=2, replica_groups=mesh['sec'=2,'seq'=8,'trk'=8] {'trk'}, dimensions={0}, use_global_device_ids=true | all-gather | bytes 884736 | tf_op jit(solution)/shard_map/all_gather | solution.py:64
  69.0 1.7 copy.36
  70.7 2.7 reshape_reshape.3
  73.4 7.3 %fusion.4 = bf16[256,2560]{1,0:T(8,128)(2,1)S(1)} fusion(f32[32,8,20,128]{3,2,1,0:T(8,128)S(1)} %bitcast.99, f32[4,2560]{1,0:T(4,128)} %bitcast_multiply_fusion, bf16[256,1536]{1,0:T(8,128)(2,1)} %reshape_reshape.3, bf16[1536,2560]{0,1:T(8,128)(2,1)} %bitcast.90), kind=kOutput, calls=%fused_computation.5 | convolution fusion | flops 2022440960 | bytes 12623872 | tf_op jit(solution)/shard_map/dot_general | solution.py:79
  80.7 0.0 copy-start.3
  80.7 1.0 copy-done.3
  81.8 6.7 %fusion.34 = f32[4,64,1536]{2,1,0:T(8,128)} fusion(bf16[4,64,2560]{2,1,0:T(8,128)(2,1)S(1)} %bitcast.100, bf16[1536,2560,1]{0,1,2:T(8,128)(2,1)} %bitcast.91), kind=kOutput, calls=%fused_computation.61 | convolution fusion | flops 2013265920 | bytes 10747904 | tf_op jit(solution)/shard_map/dot_general | solution.py:94
  88.5 2.9 copy.29
  91.4 2.7 reshape.147
  94.0 0.0 reduce-scatter.7.cloned.1.call-update
  94.0 0.0 all-gather.4.cloned.1.call-start
  94.1 44.9 %reduce-scatter.7.cloned.1.call-done = f32[192,256]{1,0:T(8,128)} async-done(((f32[1536,256]{1,0:T(8,128)}), f32[192,256]{1,0:T(8,128)}) %reduce-scatter.7.cloned.1.call-update) | async-done | bytes 196624
  139.0 1.1 reshape.148
  140.1 0.8 copy.30
  140.9 0.0 all-gather.4.cloned.1.call-update
  140.9 0.2 reduce-scatter.5.cloned.1.call-start
  141.2 0.0 copy-done.1
  141.2 7.8 %fusion.35 = f32[1536,2560]{1,0:T(8,128)} fusion(bf16[256,1536]{1,0:T(8,128)(2,1)S(1)} %copy-done.1, bf16[256,2560]{1,0:T(8,128)(2,1)S(1)} %copy-done.4), kind=kOutput, calls=%fused_computation.62 | convolution fusion | flops 2013265920 | bytes 17825792 | tf_op jit(solution)/shard_map/dot_general | solution.py:35
  148.9 0.0 reduce-scatter.5.cloned.1.call-update
  149.0 1.1 copy-done.7
  150.1 0.1 pad_maximum_fusion
  150.2 1.4 broadcast_in_dim_reshape.3
  151.5 0.4 copy.18
  151.9 31.7 %all_to_all.15 = bf16[1,4,96,16,96]{4,2,1,0,3:T(8,128)(2,1)} all-to-all(bf16[1,4,96,16,96]{4,2,1,0,3:T(8,128)(2,1)S(1)} %copy.18), channel_id=1, replica_groups=mesh['sec'=2,'seq'=8,'trk'=8] {'sec','seq'}, dimensions={3} | all-to-all | bytes 2359296 | tf_op jit(solution)/shard_map/all_to_all | solution.py:102
  183.6 10.9 %all-gather.4.cloned.1.call-done = bf16[64,64,192]{2,1,0:T(8,128)(2,1)} async-done(((bf16[4,64,192]{2,1,0:T(8,128)(2,1)}), bf16[64,64,192]{2,1,0:T(8,128)(2,1)}) %all-gather.4.cloned.1.call-update) | async-done | bytes 1572880 | tf_op jit(solution)/shard_map/all_gather | solution.py:109
  194.5 2.5 convolution_bitcast_fusion
  197.0 135.7 %reduce-scatter.5.cloned.1.call-done = f32[96,2560]{1,0:T(8,128)} async-done(((f32[1536,2560]{1,0:T(8,128)}), f32[96,2560]{1,0:T(8,128)}) %reduce-scatter.5.cloned.1.call-update) | async-done | bytes 983056 | tf_op jit(solution)/shard_map/reduce_scatter | solution.py:122
  332.7 2.1 multiply_reduce_fusion.1
  334.7 1.7 convolution_bitcast_fusion.1
  336.4 19.6 %psum.21 = f32[]{:T(128)} all-reduce(f32[]{:T(128)} %multiply_reduce_fusion.1), channel_id=1, replica_groups=mesh['sec'=2,'seq'=8,'trk'=8] {'trk'}, use_global_device_ids=true, to_apply=%region_4.5 | all-reduce | flops 1 | bytes 8 | tf_op jit(solution)/shard_map/psum | solution.py:125
  356.0 1.8 convolution_bitcast_fusion.2
  357.8 13.1 %psum.22 = f32[]{:T(128)} all-reduce(f32[]{:T(128)} %psum.21), channel_id=1, replica_groups=mesh['sec'=2,'seq'=8,'trk'=8] {'seq'}, use_global_device_ids=true, to_apply=%region_5.6 | all-reduce | flops 1 | bytes 8 | tf_op jit(solution)/shard_map/psum | solution.py:125
  370.9 0.7 pad_maximum_fusion.5
  371.6 7.0 %psum.23 = f32[]{:T(128)} all-reduce(f32[]{:T(128)} %psum.22), channel_id=1, replica_groups=mesh['sec'=2,'seq'=8,'trk'=8] {'sec'}, use_global_device_ids=true, to_apply=%region_6.7 | all-reduce | flops 1 | bytes 8 | tf_op jit(solution)/shard_map/psum | solution.py:125
  379.3 0.0 copy-done.8
  379.3 0.1 broadcast_multiply_fusion
  379.4 2.1 reshape.146
  (14 shorter events, 0.0 us)
Async XLA Ops:
  7.2 8.3 %copy-start.2 = (bf16[4,64,1536]{2,1,0:T(8,128)(2,1)S(1)}, bf16[4,64,1536]{2,1,0:T(8,128)(2,1)}, u32[]{:S(2)}) copy-start(bf16[4,64,1536]{2,1,0:T(8,128)(2,1)} %param.7) | copy-start | bytes 2359300
  7.2 8.3 %copy-start.9 = (s32[1,20]{1,0:T(1,128)S(1)}, s32[1,20]{1,0:T(1,128)}, u32[]{:S(2)}) copy-start(s32[1,20]{1,0:T(1,128)} %param.12) | copy-start | bytes 244
  7.2 131.8 %reduce-scatter.7.cloned.1.call-start = ((), (), s32[]{:S(2)}) async-start(), calls=%async_computation.5 | async-start | bytes 1769472
  11.2 0.9 copy-start.5
  12.1 4.8 %copy-start.10 = (s32[4]{0:T(128)S(1)}, s32[4]{0:T(128)}, u32[]{:S(2)}) copy-start(s32[4]{0:T(128)} %param.13) | copy-start | bytes 52
  12.9 22.4 %collective-permute-start = (bf16[4,16,1536]{2,1,0:T(8,128)(2,1)}, bf16[4,16,1536]{2,1,0:T(8,128)(2,1)S(1)}, u32[]{:S(2)}, u32[]{:S(2)}) collective-permute-start(bf16[4,16,1536]{2,1,0:T(8,128)(2,1)} %get-tuple-element.8), channel_id=1, source_target_pairs={{0,8},{8,16},{16,24},{24,32},{32,40},{40,48},{48,56},{1,9},{9,17},... | collective-permute-start | bytes 589832 | tf_op jit(solution)/shard_map/ppermute | solution.py:25
  14.2 19.6 %collective-permute-start.1 = (bf16[4,16,1536]{2,1,0:T(8,128)(2,1)}, bf16[4,16,1536]{2,1,0:T(8,128)(2,1)S(1)}, u32[]{:S(2)}, u32[]{:S(2)}) collective-permute-start(bf16[4,16,1536]{2,1,0:T(8,128)(2,1)} %get-tuple-element.9), channel_id=1, source_target_pairs={{8,0},{16,8},{24,16},{32,24},{40,32},{48,40},{56,48},{9,1},{17,9},... | collective-permute-start | bytes 589832 | tf_op jit(solution)/shard_map/ppermute | solution.py:27
  30.4 3.3 copy-start.6
  80.7 1.1 copy-start.3
  94.0 47.1 %copy-start.1 = (bf16[256,1536]{1,0:T(8,128)(2,1)S(1)}, bf16[256,1536]{1,0:T(8,128)(2,1)}, u32[]{:S(2)}) copy-start(bf16[256,1536]{1,0:T(8,128)(2,1)} %reshape_reshape.3) | copy-start | bytes 2359300
  94.0 47.2 %copy-start.4 = (bf16[256,2560]{1,0:T(8,128)(2,1)S(1)}, bf16[256,2560]{1,0:T(8,128)(2,1)}, u32[]{:S(2)}) copy-start(bf16[256,2560]{1,0:T(8,128)(2,1)} %copy-done.3) | copy-start | bytes 3932164
  94.0 100.5 %all-gather.4.cloned.1.call-start = ((), (), s32[]{:S(2)}) async-start(), calls=%async_computation.4 | async-start | bytes 2228224 | tf_op jit(solution)/shard_map/all_gather | solution.py:109
  140.9 191.8 %reduce-scatter.5.cloned.1.call-start = ((), (), s32[]{:S(2)}) async-start(), calls=%async_computation.3 | async-start | bytes 16711680 | tf_op jit(solution)/shard_map/reduce_scatter | solution.py:122
  148.9 1.1 copy-start.7
  194.5 140.2 %copy-start = (bf16[64,64,192]{2,1,0:T(8,128)(2,1)S(1)}, bf16[64,64,192]{2,1,0:T(8,128)(2,1)}, u32[]{:S(2)}) copy-start(bf16[64,64,192]{2,1,0:T(8,128)(2,1)} %all-gather.4.cloned.1.call-done) | copy-start | bytes 4718596
  356.0 23.3 %copy-start.8 = (f32[96,2560]{1,0:T(8,128)S(1)}, f32[96,2560]{1,0:T(8,128)}, u32[]{:S(2)}) copy-start(f32[96,2560]{1,0:T(8,128)} %reduce-scatter.5.cloned.1.call-done) | copy-start | bytes 2949124
Sparse Core Ops, SparseCore 0:
  94.2 44.8 reduce-scatter.6
  142.0 52.4 all-gather.3
  198.9 133.7 reduce-scatter.4

commit v3 on v2

--- a/solution.py
+++ b/solution.py
@@ -91,12 +91,14 @@
         * live_rows
     )
     flat_deltas = delta_f.astype(jnp.bfloat16)
+    head_partial = contracted_rows(flat_mixed, flat_deltas)
+    deltas_for_back, head_partial = lax.optimization_barrier((flat_deltas, head_partial))
+    grad_share = lax.psum_scatter(head_partial, ("sec", "seq"), scatter_dimension=0, tiled=True)
     back_sum = lax.dot_general(
-        flat_deltas, weights_here, (((1,), (1,)), ((), ())), preferred_element_type=jnp.float32
-    ).reshape(sample_count, local_rows, width_all)
-    backward_portion = lax.psum_scatter(back_sum, "trk", scatter_dimension=2, tiled=True).astype(
-        jnp.bfloat16
-    )
+        deltas_for_back, weights_here, (((1,), (1,)), ((), ())), preferred_element_type=jnp.float32
+    ).reshape(sample_count, local_rows, lax.axis_size("trk"), out_share)
+    back_from_owners = lax.all_to_all(back_sum, "trk", 2, 0, tiled=False)
+    backward_portion = jnp.sum(back_from_owners, axis=0).astype(jnp.bfloat16)
     group_count = lax.axis_size("sec") * lax.axis_size("seq")
     share_rows = width_all // group_count
     hidden_parts = lax.all_to_all(
@@ -106,7 +108,15 @@
         0,
         tiled=False,
     )
-    back_parts = lax.all_gather(backward_portion, ("sec", "seq"), axis=0, tiled=False)
+    back_parts = lax.all_to_all(
+        jnp.broadcast_to(
+            backward_portion[:, :, None, :], (sample_count, local_rows, group_count, out_share)
+        ),
+        ("sec", "seq"),
+        2,
+        0,
+        tiled=False,
+    )
     per_tap = [
         lax.dot_general(
             hidden_parts[
@@ -119,9 +129,6 @@
         for kernel_tap_index in range(tap_count)
     ]
     conv_grad = jnp.stack(per_tap, axis=1)
-    grad_share = lax.psum_scatter(
-        contracted_rows(flat_mixed, flat_deltas), ("sec", "seq"), scatter_dimension=0, tiled=True
-    )
     total_sq = lax.psum(lax.psum(lax.psum(jnp.sum(grad_share * grad_share), "trk"), "seq"), "sec")
     entries = width_all * lax.axis_size("trk") * slot_count * lane_count
     factor = jnp.minimum(1.0, grad_clip * lax.rsqrt(total_sq / entries + 1e-06))

time: 389 us -> 342 us (0.88)
  waiting for transfers between devices: 192 us -> 92.1 us
  local copies, waits for them, and re-layouts: 33 us -> 70 us
  starting transfers between devices: 2.88 us -> 16.2 us
    reduce_scatter x1, waiting for transfers between devices: 136 us -> 37.1 us  [body(): lax.psum_scatter(head_partial, ('sec', 'seq'), scatter_dimension=0, tiled...]
    all_to_all x0 -> x2, waiting for transfers between devices: none -> 54.9 us  [the longest x1 31.2 us: body(): back_from_owners = lax.all_to_all(back_sum, 'trk', 2, 0, tiled=False)]
    unnamed x4 -> x1, waiting for transfers between devices: 45 us -> 0.02 us
    dot_general x0 -> x2, local copies, waits for them, and re-layouts: none -> 16.2 us  [body(): lax.dot_general(deltas_for_back, weights_here, (((1,), (1,)), ((), ())),...]
    unnamed x28 -> x29, local copies, waits for them, and re-layouts: 21.8 us -> 37.2 us
    all_to_all x0 -> x2, starting transfers between devices: none -> 11.9 us  [the longest x1 6.52 us: body(): lax.all_to_all(padded_input.reshape(sample_count, local_rows + 2 * DILATI...]
    all_gather x1 -> x0, waiting for transfers between devices: 10.9 us -> none  [body(): lax.all_gather(backward_portion, ('sec', 'seq'), axis=0, tiled=False)]
    another operation x2, local copies, waits for them, and re-layouts: 1.76 us -> 6.81 us  [body(): lax.all_to_all(padded_input.reshape(sample_count, local_rows + 2 * DILATI...]
  transfers between devices with their start and end apart: 5 -> 5, of which waited for: 3 -> 3; matrix products, arithmetic and copies ran while one was open for 8% -> 22% of each run, Pallas kernels for 0% -> 0%
where the time goes in v3:
time: 342 us; the launch traced here: 340 us
  blocking collectives  105 us (31%)
  waiting for transfers between devices  92.1 us (27%)
  local copies, waits for them, and re-layouts  70 us (20%)
  matrix products  29 us (8%)
  starting transfers between devices  16.2 us (5%)
  between operations  15 us (4%)
  other arithmetic  12.8 us (4%)
    unnamed x29, local copies, waits for them, and re-layouts  37.2 us
    reduce_scatter x1, waiting for transfers between devices, body(): lax.psum_scatter(head_partial, ('sec', 'seq'), scatter_dimension=0, tiled...  37.1 us
    all_to_all x1, blocking collectives, body(): lax.all_to_all(jnp.broadcast_to(backward_portion[:, :, None, :], (sample_...  33.8 us
    all_gather x1, blocking collectives, body(): mixed_parts = lax.all_gather(mixed_share, 'trk', axis=0, tiled=False)  31.7 us
    all_to_all x1, waiting for transfers between devices, body(): back_from_owners = lax.all_to_all(back_sum, 'trk', 2, 0, tiled=False)  31.2 us
    all_to_all x1, waiting for transfers between devices, body(): lax.all_to_all(padded_input.reshape(sample_count, local_rows + 2 * DILATI...  23.7 us
    psum x1, blocking collectives, body(): lax.psum(jnp.sum(grad_share * grad_share), 'trk')  19.6 us
    dot_general x2, local copies, waits for them, and re-layouts, body(): lax.dot_general(deltas_for_back, weights_here, (((1,), (1,)), ((), ())),...  16.2 us
  transfers between devices with their start and end apart: 5, of which 3 were waited for; matrix products, arithmetic and copies ran while one was open for 22% of the time, Pallas kernels for 0%

profile of v3, /device:TPU:0, one launch (start us, length us, event | category | flops | bytes accessed | tf_op | source)
XLA Modules:
  0.0 340.3 jit_solution(9353924760610838188)
XLA Ops:
  7.2 0.0 copy-start.4
  7.2 0.0 reduce-scatter.2.cloned.1.call-start
  7.2 0.8 convert_element_type.39
  8.0 1.4 multiply_reduce_fusion
  9.4 1.8 fusion.18
  11.2 0.0 copy-start.7
  11.2 0.0 copy-start.11
  11.2 0.0 copy-start.12
  11.2 0.8 fusion.48
  12.0 1.3 collective-permute-start.1
  13.3 3.0 collective-permute-start
  16.4 0.0 copy-done.4
  16.4 1.4 convert_element_type.38
  17.8 0.0 copy-done.11
  17.8 0.0 copy-done.12
  17.8 0.1 and_convert_fusion
  17.9 0.7 broadcast_bitcast_fusion
  18.6 10.6 %copy.20 = bf16[1536,1,20,128]{0,3,2,1:T(8,128)(2,1)} copy(bf16[1536,1,20,128]{3,0,2,1:T(8,128)(2,1)} %param.10) | data formatting | bytes 15728640 | tf_op args[3]
  29.2 2.1 copy.21
  31.3 0.0 copy-start.8
  31.3 0.1 broadcast_reduce_fusion
  31.5 1.5 bitcast_multiply_fusion
  33.0 1.7 fusion.38
  34.6 0.0 collective-permute-done.1
  34.7 1.4 fusion.34
  36.1 0.0 collective-permute-done
  36.1 1.6 fusion.21
  37.7 31.7 %all-gather = bf16[32,64,192]{2,1,0:T(8,128)(2,1)S(1)} all-gather(bf16[4,64,192]{2,1,0:T(8,128)(2,1)S(1)} %fusion.21), channel_id=2, replica_groups=mesh['sec'=2,'seq'=8,'trk'=8] {'trk'}, dimensions={0}, use_global_device_ids=true | all-gather | bytes 884736 | tf_op jit(solution)/shard_map/all_gather | solution.py:64
  69.5 1.7 copy.34
  71.1 2.7 reshape_reshape.3
  73.9 7.4 %fusion.4 = bf16[256,2560]{1,0:T(8,128)(2,1)S(1)} fusion(f32[32,8,20,128]{3,2,1,0:T(8,128)S(1)} %bitcast.111, f32[4,2560]{1,0:T(4,128)} %bitcast_multiply_fusion, bf16[256,1536]{1,0:T(8,128)(2,1)} %reshape_reshape.3, bf16[1536,2560]{0,1:T(8,128)(2,1)} %bitcast.107), kind=kOutput, calls=%fused_computation.5 | convolution fusion | flops 2022440960 | bytes 12623872 | tf_op jit(solution)/shard_map/dot_general | solution.py:79
  81.3 1.1 copy-done.5
  82.4 0.0 copy-done.3
  82.4 7.8 %fusion.49 = f32[1536,2560]{1,0:T(8,128)} fusion(bf16[256,1536]{1,0:T(8,128)(2,1)S(1)} %copy-done.3, bf16[256,2560]{1,0:T(8,128)(2,1)S(1)} %fusion.4), kind=kOutput, calls=%fused_computation.68 | convolution fusion | flops 2013265920 | bytes 17825792 | tf_op jit(solution)/shard_map/dot_general | solution.py:35
  90.2 0.0 reduce-scatter.2.cloned.1.call-update
  90.2 22.3 %copy.22 = bf16[1536,1,20,128]{3,2,0,1:T(8,128)(2,1)} copy(bf16[1536,1,20,128]{3,0,2,1:T(8,128)(2,1)} %param.10) | data formatting | bytes 15728640 | tf_op args[3]
  112.5 14.6 %reshape.151 = bf16[8,192,2560,1]{2,1,0,3:T(8,128)(2,1)} reshape(bf16[1536,1,20,128]{3,2,0,1:T(8,128)(2,1)} %copy.22) | data formatting | bytes 15728640 | tf_op jit(solution)/shard_map/dot_general | solution.py:97
  127.1 0.0 copy-done.6
  127.1 5.2 %convolution_bitcast_fusion = f32[1,4,64,8,192]{4,2,3,1,0:T(8,128)S(1)} fusion(bf16[4,64,2560,1]{2,1,3,0:T(8,128)(2,1)S(1)} %bitcast.112, bf16[8,192,2560,1]{2,1,0,3:T(8,128)(2,1)} %reshape.151), kind=kOutput, calls=%fused_computation.13 | convolution fusion | flops 2013265920 | bytes 10747904 | tf_op jit(solution)/shard_map/dot_general | solution.py:97
  132.3 1.5 copy.23
  133.9 5.4 %all-to-all-start.1 = ((f32[1,4,64,8,192]{4,2,1,0,3:T(8,128)}), f32[1,4,64,8,192]{4,2,1,0,3:T(8,128)S(1)}, u32[]{:S(2)}, u32[]{:S(2)}) async-start(f32[1,4,64,8,192]{4,2,1,0,3:T(8,128)} %copy.23), calls=%async_computation.1 | async-start | bytes 4194304 | tf_op jit(solution)/shard_map/all_to_all | solution.py:100
  139.3 1.2 pad_maximum_fusion
  140.4 3.8 %broadcast_in_dim_reshape.4 = bf16[1,4,96,16,96]{4,3,2,1,0:T(8,128)(2,1)} reshape(bf16[4,96,1536]{2,1,0:T(8,128)(2,1)} %pad_maximum_fusion) | data formatting | bytes 2359296 | tf_op jit(solution)/shard_map/broadcast_in_dim;reshape | solution.py:104
  144.2 3.0 copy.18
  147.2 31.2 %all-to-all-done.1 = f32[1,4,64,8,192]{4,2,1,0,3:T(8,128)S(1)} async-done(((f32[1,4,64,8,192]{4,2,1,0,3:T(8,128)}), f32[1,4,64,8,192]{4,2,1,0,3:T(8,128)S(1)}, u32[]{:S(2)}, u32[]{:S(2)}) %all-to-all-start.1) | async-done | bytes 1572896 | tf_op jit(solution)/shard_map/all_to_all | solution.py:100
  178.4 1.3 copy-done.2
  179.7 6.5 %all-to-all-start = ((bf16[1,4,96,16,96]{4,2,1,0,3:T(8,128)(2,1)}), bf16[1,4,96,16,96]{4,2,1,0,3:T(8,128)(2,1)S(1)}, u32[]{:S(2)}, u32[]{:S(2)}) async-start(bf16[1,4,96,16,96]{4,2,1,0,3:T(8,128)(2,1)} %copy.18), calls=%async_computation | async-start | bytes 3145728 | tf_op jit(solution)/shard_map/all_to_all | solution.py:104
  186.3 1.8 reduce_sum.28
  188.0 23.7 %all-to-all-done = bf16[1,4,96,16,96]{4,2,1,0,3:T(8,128)(2,1)S(1)} async-done(((bf16[1,4,96,16,96]{4,2,1,0,3:T(8,128)(2,1)}), bf16[1,4,96,16,96]{4,2,1,0,3:T(8,128)(2,1)S(1)}, u32[]{:S(2)}, u32[]{:S(2)}) %all-to-all-start) | async-done | bytes 1179680 | tf_op jit(solution)/shard_map/all_to_all | solution.py:104
  211.8 1.1 copy-done
  212.9 0.2 broadcast_in_dim_broadcast_in_dim.2
  213.2 0.0 copy-start.1
  213.2 33.8 %all_to_all.39 = bf16[1,4,64,16,192]{4,2,1,0,3:T(8,128)(2,1)S(1)} all-to-all(bf16[1,4,64,16,192]{4,2,1,0,3:T(8,128)(2,1)S(1)} %broadcast_in_dim_broadcast_in_dim.2), channel_id=1, replica_groups=mesh['sec'=2,'seq'=8,'trk'=8] {'sec','seq'}, dimensions={3} | all-to-all | bytes 3145728 | tf_op jit(solution)/shard_map/all_to_all | solution.py:111
  247.0 0.5 fusion.22
  247.5 37.1 %reduce-scatter.2.cloned.1.call-done = f32[96,2560]{1,0:T(8,128)} async-done(((f32[1536,2560]{1,0:T(8,128)}), f32[96,2560]{1,0:T(8,128)}) %reduce-scatter.2.cloned.1.call-update) | async-done | bytes 983056 | tf_op jit(solution)/shard_map/reduce_scatter | solution.py:96
  284.6 2.1 multiply_reduce_fusion.1
  286.6 1.7 fusion.25
  288.3 19.6 %psum.21 = f32[]{:T(128)} all-reduce(f32[]{:T(128)} %multiply_reduce_fusion.1), channel_id=1, replica_groups=mesh['sec'=2,'seq'=8,'trk'=8] {'trk'}, use_global_device_ids=true, to_apply=%region_4.5 | all-reduce | flops 1 | bytes 8 | tf_op jit(solution)/shard_map/psum | solution.py:132
  307.9 1.8 fusion.28
  309.7 13.1 %psum.22 = f32[]{:T(128)} all-reduce(f32[]{:T(128)} %psum.21), channel_id=1, replica_groups=mesh['sec'=2,'seq'=8,'trk'=8] {'seq'}, use_global_device_ids=true, to_apply=%region_5.6 | all-reduce | flops 1 | bytes 8 | tf_op jit(solution)/shard_map/psum | solution.py:132
  322.7 0.7 pad_maximum_fusion.5
  323.5 7.0 %psum.23 = f32[]{:T(128)} all-reduce(f32[]{:T(128)} %psum.22), channel_id=1, replica_groups=mesh['sec'=2,'seq'=8,'trk'=8] {'sec'}, use_global_device_ids=true, to_apply=%region_6.7 | all-reduce | flops 1 | bytes 8 | tf_op jit(solution)/shard_map/psum | solution.py:132
  331.2 0.1 broadcast_multiply_fusion
  331.3 2.1 reshape.156
  (17 shorter events, 0.1 us)
Async XLA Ops:
  7.2 9.2 %copy-start.4 = (bf16[4,64,1536]{2,1,0:T(8,128)(2,1)S(1)}, bf16[4,64,1536]{2,1,0:T(8,128)(2,1)}, u32[]{:S(2)}) copy-start(bf16[4,64,1536]{2,1,0:T(8,128)(2,1)} %param.7) | copy-start | bytes 2359300
  7.2 277.4 %reduce-scatter.2.cloned.1.call-start = ((), (), s32[]{:S(2)}) async-start(), calls=%async_computation.4 | async-start | bytes 16711680 | tf_op jit(solution)/shard_map/reduce_scatter | solution.py:96
  11.2 6.6 %copy-start.7 = (bf16[4,64,1536]{2,1,0:T(8,128)(2,1)}, bf16[4,64,1536]{2,1,0:T(8,128)(2,1)S(1)}, u32[]{:S(2)}) copy-start(bf16[4,64,1536]{2,1,0:T(8,128)(2,1)S(1)} %fusion.18) | copy-start | bytes 2359300
  11.2 6.6 %copy-start.11 = (s32[1,20]{1,0:T(1,128)S(1)}, s32[1,20]{1,0:T(1,128)}, u32[]{:S(2)}) copy-start(s32[1,20]{1,0:T(1,128)} %param.12) | copy-start | bytes 244
  11.2 6.6 %copy-start.12 = (s32[4]{0:T(128)S(1)}, s32[4]{0:T(128)}, u32[]{:S(2)}) copy-start(s32[4]{0:T(128)} %param.13) | copy-start | bytes 52
  12.0 22.6 %collective-permute-start.1 = (bf16[4,16,1536]{2,1,0:T(8,128)(2,1)}, bf16[4,16,1536]{2,1,0:T(8,128)(2,1)S(1)}, u32[]{:S(2)}, u32[]{:S(2)}) collective-permute-start(bf16[4,16,1536]{2,1,0:T(8,128)(2,1)} %get-tuple-element.13), channel_id=1, source_target_pairs={{8,0},{16,8},{24,16},{32,24},{40,32},{48,40},{56,48},{9,1},{17,9},... | collective-permute-start | bytes 589832 | tf_op jit(solution)/shard_map/ppermute | solution.py:27
  13.3 22.8 %collective-permute-start = (bf16[4,16,1536]{2,1,0:T(8,128)(2,1)}, bf16[4,16,1536]{2,1,0:T(8,128)(2,1)S(1)}, u32[]{:S(2)}, u32[]{:S(2)}) collective-permute-start(bf16[4,16,1536]{2,1,0:T(8,128)(2,1)} %get-tuple-element.12), channel_id=1, source_target_pairs={{0,8},{8,16},{16,24},{24,32},{32,40},{40,48},{48,56},{1,9},{9,17},... | collective-permute-start | bytes 589832 | tf_op jit(solution)/shard_map/ppermute | solution.py:25
  31.3 3.3 copy-start.8
  73.9 8.5 %copy-start.3 = (bf16[256,1536]{1,0:T(8,128)(2,1)S(1)}, bf16[256,1536]{1,0:T(8,128)(2,1)}, u32[]{:S(2)}) copy-start(bf16[256,1536]{1,0:T(8,128)(2,1)} %reshape_reshape.3) | copy-start | bytes 2359300
  81.3 1.1 copy-start.5
  112.5 14.6 %copy-start.6 = (bf16[256,2560]{1,0:T(8,128)(2,1)S(1)}, bf16[256,2560]{1,0:T(8,128)(2,1)}, u32[]{:S(2)}) copy-start(bf16[256,2560]{1,0:T(8,128)(2,1)} %copy-done.5) | copy-start | bytes 3932164
  133.9 5.4 %copy-start.9 = (bf16[4,64,1536]{2,1,0:T(8,128)(2,1)S(1)}, bf16[4,64,1536]{2,1,0:T(8,128)(2,1)}, u32[]{:S(2)}) copy-start(bf16[4,64,1536]{2,1,0:T(8,128)(2,1)} %copy-done.7) | copy-start | bytes 2359300
  133.9 44.5 %all-to-all-start.1 = ((f32[1,4,64,8,192]{4,2,1,0,3:T(8,128)}), f32[1,4,64,8,192]{4,2,1,0,3:T(8,128)S(1)}, u32[]{:S(2)}, u32[]{:S(2)}) async-start(f32[1,4,64,8,192]{4,2,1,0,3:T(8,128)} %copy.23), calls=%async_computation.1 | async-start | bytes 4194304 | tf_op jit(solution)/shard_map/all_to_all | solution.py:100
  178.4 1.3 copy-start.2
  179.7 32.0 %all-to-all-start = ((bf16[1,4,96,16,96]{4,2,1,0,3:T(8,128)(2,1)}), bf16[1,4,96,16,96]{4,2,1,0,3:T(8,128)(2,1)S(1)}, u32[]{:S(2)}, u32[]{:S(2)}) async-start(bf16[1,4,96,16,96]{4,2,1,0,3:T(8,128)(2,1)} %copy.18), calls=%async_computation | async-start | bytes 3145728 | tf_op jit(solution)/shard_map/all_to_all | solution.py:104
  211.8 1.1 copy-start
  213.2 33.8 %copy-start.1 = (bf16[1,4,96,16,96]{4,2,1,0,3:T(8,128)(2,1)S(1)}, bf16[1,4,96,16,96]{4,2,1,0,3:T(8,128)(2,1)}, u32[]{:S(2)}) copy-start(bf16[1,4,96,16,96]{4,2,1,0,3:T(8,128)(2,1)} %copy-done) | copy-start | bytes 3538948
  307.9 23.3 %copy-start.10 = (f32[96,2560]{1,0:T(8,128)S(1)}, f32[96,2560]{1,0:T(8,128)}, u32[]{:S(2)}) copy-start(f32[96,2560]{1,0:T(8,128)} %reduce-scatter.2.cloned.1.call-done) | copy-start | bytes 2949124
Sparse Core Ops, SparseCore 0:
  90.3 194.2 reduce-scatter.1

commit v4 on v2

--- a/solution.py
+++ b/solution.py
@@ -35,6 +35,41 @@
     return lax.dot_general(
         left, right, (((0,), (0,)), ((), ())), preferred_element_type=jnp.float32
     )
+
+
+def ring_scatter(partial):
+    rows_all, cols = partial.shape
+    sec_n = lax.axis_size("sec")
+    x_n = lax.axis_size("seq") // 2
+    share = rows_all // (sec_n * x_n * 2)
+    sec_i = lax.axis_index("sec")
+    x_i = lax.axis_index("seq") // 2
+    core_i = lax.axis_index("seq") % 2
+    blocks = partial.reshape(sec_n, x_n, 2, share, cols)
+    keep = lax.dynamic_index_in_dim(blocks, core_i, 2, keepdims=False)
+    give = lax.dynamic_index_in_dim(blocks, 1 - core_i, 2, keepdims=False)
+    core_pairs = [(2 * i + j, 2 * i + 1 - j) for i in range(x_n) for j in range(2)]
+    summed = keep + lax.ppermute(give, "seq", core_pairs)
+    half = cols // 2
+    ahead = summed[..., :half]
+    behind = summed[..., half:]
+    to_next = [(2 * i + j, 2 * ((i + 1) % x_n) + j) for i in range(x_n) for j in range(2)]
+    to_prev = [(2 * i + j, 2 * ((i - 1) % x_n) + j) for i in range(x_n) for j in range(2)]
+    send_a = lax.dynamic_index_in_dim(ahead, (x_i - 1) % x_n, 1, keepdims=False)
+    send_b = lax.dynamic_index_in_dim(behind, (x_i + 1) % x_n, 1, keepdims=False)
+    for step in range(x_n - 1):
+        got_a = lax.ppermute(send_a, "seq", to_next)
+        got_b = lax.ppermute(send_b, "seq", to_prev)
+        send_a = got_a + lax.dynamic_index_in_dim(ahead, (x_i - step - 2) % x_n, 1, keepdims=False)
+        send_b = got_b + lax.dynamic_index_in_dim(behind, (x_i + step + 2) % x_n, 1, keepdims=False)
+    reduced = jnp.concatenate([send_a, send_b], axis=-1)
+    total = lax.dynamic_index_in_dim(reduced, sec_i, 0, keepdims=False)
+    for shift in range(1, sec_n):
+        other = lax.dynamic_index_in_dim(reduced, (sec_i - shift) % sec_n, 0, keepdims=False)
+        total = total + lax.ppermute(
+            other, "sec", [(i, (i - shift) % sec_n) for i in range(sec_n)]
+        )
+    return total
 
 
 def body(tokens, norm_gain, dilated_conv_weight, head_weight, targets, owner_tiles, species):
@@ -91,10 +126,11 @@
         * live_rows
     )
     flat_deltas = delta_f.astype(jnp.bfloat16)
-    back_sum = lax.dot_general(
-        flat_deltas, weights_here, (((1,), (1,)), ((), ())), preferred_element_type=jnp.float32
-    ).reshape(sample_count, local_rows, width_all)
-    backward_portion = lax.psum_scatter(back_sum, "trk", scatter_dimension=2, tiled=True).astype(
+    head_partial = contracted_rows(flat_mixed, flat_deltas)
+    deltas_for_back, head_partial = lax.optimization_barrier((flat_deltas, head_partial))
+    grad_share = ring_scatter(head_partial)
+    back_t = jnp.dot(weights_here, deltas_for_back.T, preferred_element_type=jnp.float32)
+    backward_portion = lax.psum_scatter(back_t, "trk", scatter_dimension=0, tiled=True).astype(
         jnp.bfloat16
     )
     group_count = lax.axis_size("sec") * lax.axis_size("seq")
@@ -111,17 +147,14 @@
         lax.dot_general(
             hidden_parts[
                 :, :, kernel_tap_index * DILATION_BINS : kernel_tap_index * DILATION_BINS + local_rows
-            ].reshape(group_count, sample_count, local_rows, share_rows),
+            ].reshape(group_count, sample_count * local_rows, share_rows),
             back_parts,
-            (((0, 1, 2), (0, 1, 2)), ((), ())),
+            (((0, 1), (0, 2)), ((), ())),
             preferred_element_type=jnp.float32,
         )
         for kernel_tap_index in range(tap_count)
     ]
     conv_grad = jnp.stack(per_tap, axis=1)
-    grad_share = lax.psum_scatter(
-        contracted_rows(flat_mixed, flat_deltas), ("sec", "seq"), scatter_dimension=0, tiled=True
-    )
     total_sq = lax.psum(lax.psum(lax.psum(jnp.sum(grad_share * grad_share), "trk"), "seq"), "sec")
     entries = width_all * lax.axis_size("trk") * slot_count * lane_count
     factor = jnp.minimum(1.0, grad_clip * lax.rsqrt(total_sq / entries + 1e-06))

time: 389 us -> 291 us (0.75)
  waiting for transfers between devices: 192 us -> 79.7 us
  blocking collectives: 104 us -> 73 us
  other arithmetic: 9.92 us -> 31.6 us
  starting transfers between devices: 2.88 us -> 22.3 us
  local copies, waits for them, and re-layouts: 33 us -> 41.9 us
  matrix products: 32.5 us -> 26 us
    reduce_scatter x1, waiting for transfers between devices: 136 us -> 0.01 us  [body(): lax.psum_scatter(back_t, 'trk', scatter_dimension=0, tiled=True)]
    ppermute x0 -> x8, waiting for transfers between devices: none -> 76.4 us  [the longest x3 58 us: ring_scatter(): got_a = lax.ppermute(send_a, 'seq', to_next)]
    unnamed x4 -> x2, waiting for transfers between devices: 45 us -> 0.03 us
    all_to_all x1 -> x0, blocking collectives: 31.7 us -> none  [body(): lax.all_to_all(padded_input.reshape(sample_count, local_rows + 2 * DILATI...]
    add x0 -> x7, other arithmetic: none -> 18.3 us  [the longest x1 7.23 us: ring_scatter(): summed = keep + lax.ppermute(give, 'seq', core_pairs)]
    ppermute x0 -> x8, starting transfers between devices: none -> 13.5 us  [the longest x3 8.57 us: ring_scatter(): got_b = lax.ppermute(send_b, 'seq', to_prev)]
    all_gather x1, waiting for transfers between devices: 10.9 us -> 0.01 us  [body(): lax.all_gather(backward_portion, ('sec', 'seq'), axis=0, tiled=False)]
    squeeze x0 -> x3, local copies, waits for them, and re-layouts: none -> 6.3 us  [the longest x1 4.01 us: ring_scatter(): give = lax.dynamic_index_in_dim(blocks, 1 - core_i, 2, keepdims=False)]
  transfers between devices with their start and end apart: 5 -> 13, of which waited for: 3 -> 9; matrix products, arithmetic and copies ran while one was open for 8% -> 21% of each run, Pallas kernels for 0% -> 0%
where the time goes in v4:
time: 291 us; the launch traced here: 289 us
  waiting for transfers between devices  79.7 us (27%)
  blocking collectives  73 us (25%)
  local copies, waits for them, and re-layouts  41.9 us (14%)
  other arithmetic  31.6 us (11%)
  matrix products  26 us (9%)
  starting transfers between devices  22.3 us (8%)
  between operations  15 us (5%)
    ppermute x3, waiting for transfers between devices, ring_scatter(): got_a = lax.ppermute(send_a, 'seq', to_next)  58 us
    all_gather x1, blocking collectives, body(): mixed_parts = lax.all_gather(mixed_share, 'trk', axis=0, tiled=False)  31.7 us
    psum x1, blocking collectives, body(): lax.psum(jnp.sum(grad_share * grad_share), 'trk')  20.3 us
    unnamed x35, local copies, waits for them, and re-layouts  18.8 us
    psum x1, blocking collectives, body(): lax.psum(lax.psum(jnp.sum(grad_share * grad_share), 'trk'), 'seq')  13.8 us
    ppermute x1, waiting for transfers between devices, ring_scatter(): lax.ppermute(other, 'sec', [(i, (i - shift) % sec_n) for i in range(sec_n)])  10.8 us
    ppermute x3, starting transfers between devices, ring_scatter(): got_b = lax.ppermute(send_b, 'seq', to_prev)  8.57 us
    dot_general x1, matrix products, body(): jnp.dot(flat_mixed, weights_here, preferred_element_type=jnp.float32)  7.42 us
  transfers between devices with their start and end apart: 13, of which 9 were waited for; matrix products, arithmetic and copies ran while one was open for 21% of the time, Pallas kernels for 0%

profile of v4, /device:TPU:0, one launch (start us, length us, event | category | flops | bytes accessed | tf_op | source)
XLA Modules:
  0.0 289.4 jit_solution(13412641418798745092)
XLA Ops:
  7.2 0.8 convert_element_type.39
  8.0 1.4 multiply_reduce_fusion
  9.4 1.8 fusion.12
  11.2 0.8 fusion.38
  12.0 1.3 collective-permute-start.1
  13.3 3.0 %collective-permute-start = (bf16[4,16,1536]{2,1,0:T(8,128)(2,1)}, bf16[4,16,1536]{2,1,0:T(8,128)(2,1)S(1)}, u32[]{:S(2)}, u32[]{:S(2)}) collective-permute-start(bf16[4,16,1536]{2,1,0:T(8,128)(2,1)} %get-tuple-element.13), channel_id=1, source_target_pairs={{0,8},{8,16},{16,24},{24,32},{32,40},{40,48},{48,56},{1,9},{9,17},... | collective-permute-start | bytes 589832 | tf_op jit(solution)/shard_map/ppermute | solution.py:25
  16.4 1.4 convert_element_type.38
  17.8 2.1 copy.35
  20.0 0.7 broadcast_bitcast_fusion
  20.7 10.6 %copy.34 = bf16[1536,1,20,128]{0,3,2,1:T(8,128)(2,1)} copy(bf16[1536,1,20,128]{3,0,2,1:T(8,128)(2,1)} %param.10) | data formatting | bytes 15728640 | tf_op args[3]
  31.3 0.1 broadcast_reduce_fusion
  31.4 1.4 bitcast_multiply_fusion
  32.9 1.8 fusion.25
  34.7 1.4 fusion.21
  36.1 1.6 fusion.15
  37.7 31.7 %all-gather = bf16[32,64,192]{2,1,0:T(8,128)(2,1)S(1)} all-gather(bf16[4,64,192]{2,1,0:T(8,128)(2,1)S(1)} %fusion.15), channel_id=2, replica_groups=mesh['sec'=2,'seq'=8,'trk'=8] {'trk'}, dimensions={0}, use_global_device_ids=true | all-gather | bytes 884736 | tf_op jit(solution)/shard_map/all_gather | solution.py:99
  69.4 1.6 copy.50
  71.0 2.7 reshape_reshape.3
  73.7 7.4 %fusion.4 = bf16[256,2560]{1,0:T(8,128)(2,1)S(1)} fusion(f32[32,8,20,128]{3,2,1,0:T(8,128)S(1)} %bitcast.121, f32[4,2560]{1,0:T(4,128)} %bitcast_multiply_fusion, bf16[256,1536]{1,0:T(8,128)(2,1)} %reshape_reshape.3, bf16[1536,2560]{0,1:T(8,128)(2,1)} %bitcast.115), kind=kOutput, calls=%fused_computation.8 | convolution fusion | flops 2022440960 | bytes 12623872 | tf_op jit(solution)/shard_map/dot_general | solution.py:114
  81.2 2.2 fusion.39
  83.5 4.0 %dynamic-slice_bitcast_fusion = f32[2,4,96,2560]{3,2,1,0:T(8,128)} fusion(f32[2,4,2,96,2560]{4,3,2,1,0:T(8,128)S(1)} %bitcast.113, s32[]{:T(128)S(6)} %select_n.115), kind=kLoop, calls=%fused_computation.1 | loop fusion | bytes 15728644 | tf_op jit(solution)/shard_map/jit(dynamic_index_in_dim)/squeeze | solution.py:50
  87.5 4.0 %copy-done = f32[1536,2560]{1,0:T(8,128)} copy-done((f32[1536,2560]{1,0:T(8,128)}, f32[1536,2560]{1,0:T(8,128)S(1)}, u32[]{:S(2)}) %copy-start) | copy-done | bytes 15728664
  91.5 5.4 %convolution_bitcast_fusion = f32[1536,256]{0,1:T(8,128)S(1)} fusion(bf16[256,2560]{1,0:T(8,128)(2,1)S(1)} %copy-done.6, bf16[1536,2560]{0,1:T(8,128)(2,1)} %bitcast.116), kind=kOutput, calls=%fused_computation.3 | convolution fusion | flops 2013265920 | bytes 10747904 | tf_op jit(solution)/shard_map/dot_general | solution.py:132
  96.9 1.6 copy.43
  98.6 5.6 %collective-permute-done.2 = f32[2,4,96,2560]{3,2,1,0:T(8,128)} collective-permute-done((f32[2,4,96,2560]{3,2,1,0:T(8,128)}, f32[2,4,96,2560]{3,2,1,0:T(8,128)}, u32[]{:S(2)}, u32[]{:S(2)}) %collective-permute-start.2) | collective-permute-done | bytes 7864352 | tf_op jit(solution)/shard_map/ppermute | solution.py:52
  104.2 7.2 %bitcast_add_fusion = f32[2,4,96,2560]{3,2,1,0:T(8,128)S(1)} fusion(f32[2,4,96,2560]{3,2,1,0:T(8,128)} %collective-permute-done.2, f32[2,4,2,96,2560]{4,3,2,1,0:T(8,128)} %bitcast.114, s32[]{:T(128)S(6)} %select_n.114), kind=kLoop, calls=%fused_computation | loop fusion | flops 1966080 | bytes 23592964 | tf_op jit(solution)/shard_map/add | solution.py:52
  111.5 2.6 fusion.36
  114.1 1.9 copy-done.1
  116.0 1.5 collective-permute-start.3
  117.5 2.2 dynamic-slice_bitcast_fusion.1
  119.8 1.8 collective-permute-start.6
  121.5 19.6 %collective-permute-done.3 = f32[2,96,1280]{2,1,0:T(8,128)S(1)} collective-permute-done((f32[2,96,1280]{2,1,0:T(8,128)S(1)}, f32[2,96,1280]{2,1,0:T(8,128)S(1)}, u32[]{:S(2)}, u32[]{:S(2)}) %collective-permute-start.3) | collective-permute-done | bytes 983072 | tf_op jit(solution)/shard_map/ppermute | solution.py:61
  141.1 1.3 bitcast_add_fusion.6
  142.4 0.3 collective-permute-start.4
  142.7 0.9 collective-permute-done.6
  143.6 1.6 bitcast_add_fusion.3
  145.2 3.1 %collective-permute-start.7 = (f32[2,96,1280]{2,1,0:T(8,128)S(1)}, f32[2,96,1280]{2,1,0:T(8,128)}, u32[]{:S(2)}, u32[]{:S(2)}) collective-permute-start(f32[2,96,1280]{2,1,0:T(8,128)S(1)} %bitcast_add_fusion.3), channel_id=1, source_target_pairs={{0,48},{8,56},{16,0},{24,8},{32,16},{40,24},{48,32},{56,40},{1,49}... | collective-permute-start | bytes 2949128 | tf_op jit(solution)/shard_map/ppermute | solution.py:62
  148.3 1.6 convert_element_type.47
  149.9 17.7 %collective-permute-done.4 = f32[2,96,1280]{2,1,0:T(8,128)S(1)} collective-permute-done((f32[2,96,1280]{2,1,0:T(8,128)S(1)}, f32[2,96,1280]{2,1,0:T(8,128)S(1)}, u32[]{:S(2)}, u32[]{:S(2)}) %collective-permute-start.4) | collective-permute-done | bytes 983072 | tf_op jit(solution)/shard_map/ppermute | solution.py:61
  167.6 2.2 bitcast_add_fusion.5
  169.9 2.7 bitcast_add_fusion.2
  172.6 3.8 %collective-permute-start.8 = (f32[2,96,1280]{2,1,0:T(8,128)}, f32[2,96,1280]{2,1,0:T(8,128)}, u32[]{:S(2)}, u32[]{:S(2)}) collective-permute-start(f32[2,96,1280]{2,1,0:T(8,128)} %bitcast_add_fusion.2), channel_id=1, source_target_pairs={{0,48},{8,56},{16,0},{24,8},{32,16},{40,24},{48,32},{56,40},{1,49}... | collective-permute-start | bytes 2949128 | tf_op jit(solution)/shard_map/ppermute | solution.py:62
  176.3 0.1 pad_maximum_fusion
  176.4 1.4 broadcast_in_dim_reshape.3
  177.8 1.5 copy.32
  179.3 4.4 %all-to-all-start = ((bf16[1,4,96,16,96]{4,2,1,0,3:T(8,128)(2,1)}), bf16[1,4,96,16,96]{4,2,1,0,3:T(8,128)(2,1)S(1)}, u32[]{:S(2)}, u32[]{:S(2)}) async-start(bf16[1,4,96,16,96]{4,2,1,0,3:T(8,128)(2,1)} %copy.32), calls=%async_computation | async-start | bytes 3145728 | tf_op jit(solution)/shard_map/all_to_all | solution.py:138
  183.7 20.7 %collective-permute-done.5 = f32[2,96,1280]{2,1,0:T(8,128)} collective-permute-done((f32[2,96,1280]{2,1,0:T(8,128)}, f32[2,96,1280]{2,1,0:T(8,128)}, u32[]{:S(2)}, u32[]{:S(2)}) %collective-permute-start.5) | collective-permute-done | bytes 983072 | tf_op jit(solution)/shard_map/ppermute | solution.py:61
  204.4 1.6 bitcast_add_fusion.4
  206.0 1.1 collective-permute-done.8
  207.1 1.6 bitcast_add_fusion.1
  208.7 1.0 fusion.17
  209.8 3.1 %collective-permute-start.9 = (f32[96,2560]{1,0:T(8,128)}, f32[96,2560]{1,0:T(8,128)}, u32[]{:S(2)}, u32[]{:S(2)}) collective-permute-start(f32[96,2560]{1,0:T(8,128)} %fusion.17), channel_id=1, source_target_pairs={{0,64},{64,0},{1,65},{65,1},{2,66},{66,2},{3,67},{67,3},{4,68},{68... | collective-permute-start | bytes 2949128 | tf_op jit(solution)/shard_map/ppermute | solution.py:69
  212.8 3.2 %all-to-all-done = bf16[1,4,96,16,96]{4,2,1,0,3:T(8,128)(2,1)S(1)} async-done(((bf16[1,4,96,16,96]{4,2,1,0,3:T(8,128)(2,1)}), bf16[1,4,96,16,96]{4,2,1,0,3:T(8,128)(2,1)S(1)}, u32[]{:S(2)}, u32[]{:S(2)}) %all-to-all-start) | async-done | bytes 1179680 | tf_op jit(solution)/shard_map/all_to_all | solution.py:138
  216.1 1.8 fusion.37
  217.9 3.1 %convolution_bitcast_fusion.1 = f32[96,1,192]{2,0,1:T(8,128)} fusion(bf16[16,256,96]{2,1,0:T(8,128)(2,1)} %bitcast.126, bf16[16,192,256]{2,1,0:T(8,128)(2,1)} %bitcast.118), kind=kOutput, calls=%fused_computation.28 | convolution fusion | flops 150994944 | bytes 2433024 | tf_op jit(solution)/shard_map/dot_general | solution.py:147
  221.0 1.2 convolution_bitcast_fusion.2
  222.2 10.8 %collective-permute-done.9 = f32[96,2560]{1,0:T(8,128)} collective-permute-done((f32[96,2560]{1,0:T(8,128)}, f32[96,2560]{1,0:T(8,128)}, u32[]{:S(2)}, u32[]{:S(2)}) %collective-permute-start.9) | collective-permute-done | bytes 983072 | tf_op jit(solution)/shard_map/ppermute | solution.py:69
  232.9 3.0 %multiply_reduce_fusion.1 = (f32[]{:T(128)}, f32[96,2560]{1,0:T(8,128)}) fusion(f32[96,2560]{1,0:T(8,128)} %collective-permute-done.9, s32[]{:T(128)S(6)} %select_n.133, f32[2,96,1280]{2,1,0:T(8,128)S(1)} %bitcast_add_fusion.1, f32[2,96,1280]{2,1,0:T(8,128)S(1)} %bitcast_add_fusion.4), kind=kLoop, calls=%fused_computation.43 | loop fusion | flops 983039 | bytes 3932168 | tf_op jit(solution)/shard_map/reduce_sum | solution.py:158
  235.9 20.3 %psum.21 = f32[]{:T(128)} all-reduce(f32[]{:T(128)} %get-tuple-element.6), channel_id=1, replica_groups=mesh['sec'=2,'seq'=8,'trk'=8] {'trk'}, use_global_device_ids=true, to_apply=%region_3.4 | all-reduce | flops 1 | bytes 8 | tf_op jit(solution)/shard_map/psum | solution.py:158
  256.2 1.8 convolution_bitcast_fusion.3
  258.0 13.8 %psum.22 = f32[]{:T(128)} all-reduce(f32[]{:T(128)} %psum.21), channel_id=1, replica_groups=mesh['sec'=2,'seq'=8,'trk'=8] {'seq'}, use_global_device_ids=true, to_apply=%region_4.5 | all-reduce | flops 1 | bytes 8 | tf_op jit(solution)/shard_map/psum | solution.py:158
  271.8 0.7 pad_maximum_fusion.5
  272.6 7.1 %psum.23 = f32[]{:T(128)} all-reduce(f32[]{:T(128)} %psum.22), channel_id=1, replica_groups=mesh['sec'=2,'seq'=8,'trk'=8] {'sec'}, use_global_device_ids=true, to_apply=%region_5.6 | all-reduce | flops 1 | bytes 8 | tf_op jit(solution)/shard_map/psum | solution.py:158
  280.5 2.1 reshape.149
  (49 shorter events, 0.5 us)
Async XLA Ops:
  7.2 9.3 %copy-start.4 = (bf16[4,64,1536]{2,1,0:T(8,128)(2,1)S(1)}, bf16[4,64,1536]{2,1,0:T(8,128)(2,1)}, u32[]{:S(2)}) copy-start(bf16[4,64,1536]{2,1,0:T(8,128)(2,1)} %param.7) | copy-start | bytes 2359300
  7.2 9.2 %copy-start.14 = (s32[1,20]{1,0:T(1,128)S(1)}, s32[1,20]{1,0:T(1,128)}, u32[]{:S(2)}) copy-start(s32[1,20]{1,0:T(1,128)} %param.12) | copy-start | bytes 244
  7.2 141.1 %reduce-scatter.4.cloned.1.call-start = ((), (), s32[]{:S(2)}) async-start(), calls=%async_computation.3 | async-start | bytes 1769472 | tf_op jit(solution)/shard_map/reduce_scatter | solution.py:133
  11.2 6.6 %copy-start.7 = (bf16[4,64,1536]{2,1,0:T(8,128)(2,1)}, bf16[4,64,1536]{2,1,0:T(8,128)(2,1)S(1)}, u32[]{:S(2)}) copy-start(bf16[4,64,1536]{2,1,0:T(8,128)(2,1)S(1)} %fusion.12) | copy-start | bytes 2359300
  12.0 22.6 %collective-permute-start.1 = (bf16[4,16,1536]{2,1,0:T(8,128)(2,1)}, bf16[4,16,1536]{2,1,0:T(8,128)(2,1)S(1)}, u32[]{:S(2)}, u32[]{:S(2)}) collective-permute-start(bf16[4,16,1536]{2,1,0:T(8,128)(2,1)} %get-tuple-element.14), channel_id=1, source_target_pairs={{8,0},{16,8},{24,16},{32,24},{40,32},{48,40},{56,48},{9,1},{17,9},... | collective-permute-start | bytes 589832 | tf_op jit(solution)/shard_map/ppermute | solution.py:27
  13.3 22.8 %collective-permute-start = (bf16[4,16,1536]{2,1,0:T(8,128)(2,1)}, bf16[4,16,1536]{2,1,0:T(8,128)(2,1)S(1)}, u32[]{:S(2)}, u32[]{:S(2)}) collective-permute-start(bf16[4,16,1536]{2,1,0:T(8,128)(2,1)} %get-tuple-element.13), channel_id=1, source_target_pairs={{0,8},{8,16},{16,24},{24,32},{32,40},{40,48},{48,56},{1,9},{9,17},... | collective-permute-start | bytes 589832 | tf_op jit(solution)/shard_map/ppermute | solution.py:25
  17.8 2.1 copy-start.15
  32.9 1.8 copy-start.8
  73.7 7.4 %copy-start.3 = (bf16[256,1536]{1,0:T(8,128)(2,1)S(1)}, bf16[256,1536]{1,0:T(8,128)(2,1)}, u32[]{:S(2)}) copy-start(bf16[256,1536]{1,0:T(8,128)(2,1)} %reshape_reshape.3) | copy-start | bytes 2359300
  81.2 2.3 copy-start.5
  83.4 8.0 %copy-start = (f32[1536,2560]{1,0:T(8,128)}, f32[1536,2560]{1,0:T(8,128)S(1)}, u32[]{:S(2)}) copy-start(f32[1536,2560]{1,0:T(8,128)S(1)} %fusion.39) | copy-start | bytes 47185924
  83.4 8.0 %copy-start.6 = (bf16[256,2560]{1,0:T(8,128)(2,1)S(1)}, bf16[256,2560]{1,0:T(8,128)(2,1)}, u32[]{:S(2)}) copy-start(bf16[256,2560]{1,0:T(8,128)(2,1)} %copy-done.5) | copy-start | bytes 3932164
  91.5 12.8 %collective-permute-start.2 = (f32[2,4,96,2560]{3,2,1,0:T(8,128)}, f32[2,4,96,2560]{3,2,1,0:T(8,128)}, u32[]{:S(2)}, u32[]{:S(2)}) collective-permute-start(f32[2,4,96,2560]{3,2,1,0:T(8,128)} %dynamic-slice_bitcast_fusion), channel_id=1, source_target_pairs={{0,8},{8,0},{16,24},{24,16},{32,40},{40,32},{48,56},{56,48},{1,9},... | collective-permute-start | bytes 23592968 | tf_op jit(solution)/shard_map/ppermute | solution.py:52
  98.5 119.3 %all-gather.4.cloned.1.call-start = ((), (), s32[]{:S(2)}) async-start(), calls=%async_computation.2 | async-start | bytes 1671168 | tf_op jit(solution)/shard_map/all_gather | solution.py:145
  114.1 1.9 copy-start.1
  116.0 25.1 %collective-permute-start.3 = (f32[2,96,1280]{2,1,0:T(8,128)S(1)}, f32[2,96,1280]{2,1,0:T(8,128)S(1)}, u32[]{:S(2)}, u32[]{:S(2)}) collective-permute-start(f32[2,96,1280]{2,1,0:T(8,128)S(1)} %dynamic-slice_bitcast_fusion.2), channel_id=1, source_target_pairs={{0,16},{8,24},{16,32},{24,40},{32,48},{40,56},{48,0},{56,8},{1,17}... | collective-permute-start | bytes 2949128 | tf_op jit(solution)/shard_map/ppermute | solution.py:61
  119.8 23.8 %collective-permute-start.6 = (f32[2,96,1280]{2,1,0:T(8,128)}, f32[2,96,1280]{2,1,0:T(8,128)}, u32[]{:S(2)}, u32[]{:S(2)}) collective-permute-start(f32[2,96,1280]{2,1,0:T(8,128)} %dynamic-slice_bitcast_fusion.1), channel_id=1, source_target_pairs={{0,48},{8,56},{16,0},{24,8},{32,16},{40,24},{48,32},{56,40},{1,49}... | collective-permute-start | bytes 2949128 | tf_op jit(solution)/shard_map/ppermute | solution.py:62
  142.4 25.2 %collective-permute-start.4 = (f32[2,96,1280]{2,1,0:T(8,128)S(1)}, f32[2,96,1280]{2,1,0:T(8,128)S(1)}, u32[]{:S(2)}, u32[]{:S(2)}) collective-permute-start(f32[2,96,1280]{2,1,0:T(8,128)S(1)} %bitcast_add_fusion.6), channel_id=1, source_target_pairs={{0,16},{8,24},{16,32},{24,40},{32,48},{40,56},{48,0},{56,8},{1,17}... | collective-permute-start | bytes 2949128 | tf_op jit(solution)/shard_map/ppermute | solution.py:61
  145.2 24.7 %collective-permute-start.7 = (f32[2,96,1280]{2,1,0:T(8,128)S(1)}, f32[2,96,1280]{2,1,0:T(8,128)}, u32[]{:S(2)}, u32[]{:S(2)}) collective-permute-start(f32[2,96,1280]{2,1,0:T(8,128)S(1)} %bitcast_add_fusion.3), channel_id=1, source_target_pairs={{0,48},{8,56},{16,0},{24,8},{32,16},{40,24},{48,32},{56,40},{1,49}... | collective-permute-start | bytes 2949128 | tf_op jit(solution)/shard_map/ppermute | solution.py:62
  169.8 6.5 %copy-start.9 = (bf16[4,64,1536]{2,1,0:T(8,128)(2,1)S(1)}, bf16[4,64,1536]{2,1,0:T(8,128)(2,1)}, u32[]{:S(2)}) copy-start(bf16[4,64,1536]{2,1,0:T(8,128)(2,1)} %copy-done.7) | copy-start | bytes 2359300
  169.8 34.6 %collective-permute-start.5 = (f32[2,96,1280]{2,1,0:T(8,128)}, f32[2,96,1280]{2,1,0:T(8,128)}, u32[]{:S(2)}, u32[]{:S(2)}) collective-permute-start(f32[2,96,1280]{2,1,0:T(8,128)} %bitcast_add_fusion.5), channel_id=1, source_target_pairs={{0,16},{8,24},{16,32},{24,40},{32,48},{40,56},{48,0},{56,8},{1,17}... | collective-permute-start | bytes 2949128 | tf_op jit(solution)/shard_map/ppermute | solution.py:61
  172.6 34.6 %collective-permute-start.8 = (f32[2,96,1280]{2,1,0:T(8,128)}, f32[2,96,1280]{2,1,0:T(8,128)}, u32[]{:S(2)}, u32[]{:S(2)}) collective-permute-start(f32[2,96,1280]{2,1,0:T(8,128)} %bitcast_add_fusion.2), channel_id=1, source_target_pairs={{0,48},{8,56},{16,0},{24,8},{32,16},{40,24},{48,32},{56,40},{1,49}... | collective-permute-start | bytes 2949128 | tf_op jit(solution)/shard_map/ppermute | solution.py:62
  179.3 36.8 %all-to-all-start = ((bf16[1,4,96,16,96]{4,2,1,0,3:T(8,128)(2,1)}), bf16[1,4,96,16,96]{4,2,1,0,3:T(8,128)(2,1)S(1)}, u32[]{:S(2)}, u32[]{:S(2)}) async-start(bf16[1,4,96,16,96]{4,2,1,0,3:T(8,128)(2,1)} %copy.32), calls=%async_computation | async-start | bytes 3145728 | tf_op jit(solution)/shard_map/all_to_all | solution.py:138
  209.8 23.2 %collective-permute-start.9 = (f32[96,2560]{1,0:T(8,128)}, f32[96,2560]{1,0:T(8,128)}, u32[]{:S(2)}, u32[]{:S(2)}) collective-permute-start(f32[96,2560]{1,0:T(8,128)} %fusion.17), channel_id=1, source_target_pairs={{0,64},{64,0},{1,65},{65,1},{2,66},{66,2},{3,67},{67,3},{4,68},{68... | collective-permute-start | bytes 2949128 | tf_op jit(solution)/shard_map/ppermute | solution.py:69
  217.9 3.1 %copy-start.2 = (bf16[3072,256]{1,0:T(8,128)(2,1)S(1)}, bf16[3072,256]{1,0:T(8,128)(2,1)}, u32[]{:S(2)}) copy-start(bf16[3072,256]{1,0:T(8,128)(2,1)} %all-gather.4.cloned.1.call-done) | copy-start | bytes 4718596
  217.9 3.1 %copy-start.10 = (bf16[16,4,64,96]{3,2,1,0:T(8,128)(2,1)S(1)}, bf16[16,4,64,96]{3,2,1,0:T(8,128)(2,1)}, u32[]{:S(2)}) copy-start(bf16[16,4,64,96]{3,2,1,0:T(8,128)(2,1)} %get-tuple-element.12) | copy-start | bytes 2359300
  235.9 35.9 %copy-start.12 = (f32[96,1,192]{2,0,1:T(8,128)S(1)}, f32[96,1,192]{2,0,1:T(8,128)}, u32[]{:S(2)}) copy-start(f32[96,1,192]{2,0,1:T(8,128)} %convolution_bitcast_fusion.1) | copy-start | bytes 221188
  235.9 35.9 %copy-start.13 = (f32[96,1,192]{2,0,1:T(8,128)S(1)}, f32[96,1,192]{2,0,1:T(8,128)}, u32[]{:S(2)}) copy-start(f32[96,1,192]{2,0,1:T(8,128)} %convolution_bitcast_fusion.2) | copy-start | bytes 221188
  235.9 44.5 %copy-start.11 = (f32[96,2560]{1,0:T(8,128)S(1)}, f32[96,2560]{1,0:T(8,128)}, u32[]{:S(2)}) copy-start(f32[96,2560]{1,0:T(8,128)} %get-tuple-element.7) | copy-start | bytes 2949124
Sparse Core Ops, SparseCore 0:
  98.6 42.8 reduce-scatter.3
  150.0 46.3 all-gather.3

commit v5 on v4

--- a/solution.py
+++ b/solution.py
@@ -72,6 +72,16 @@
     return total
 
 
+def butterfly_sum(value):
+    for axis in ("seq", "trk", "sec"):
+        count = lax.axis_size(axis)
+        bit = 1
+        while bit < count:
+            value = value + lax.ppermute(value, axis, [(i, i ^ bit) for i in range(count)])
+            bit *= 2
+    return value
+
+
 def body(tokens, norm_gain, dilated_conv_weight, head_weight, targets, owner_tiles, species):
     sample_count = tokens.shape[0]
     local_rows = tokens.shape[1]
@@ -96,7 +106,13 @@
         )
     own_cols = lax.dynamic_slice_in_dim(inputs, lax.axis_index("trk") * out_share, out_share, 2)
     mixed_share = (own_cols + convolution_output).astype(jnp.bfloat16)
-    mixed_parts = lax.all_gather(mixed_share, "trk", axis=0, tiled=False)
+    trk_n = lax.axis_size("trk")
+    shifted = [mixed_share] + [
+        lax.ppermute(mixed_share, "trk", [(i, (i + k) % trk_n) for i in range(trk_n)])
+        for k in range(1, trk_n)
+    ]
+    order = (lax.axis_index("trk") - jnp.arange(trk_n)) % trk_n
+    mixed_parts = jnp.take(jnp.stack(shifted), order, axis=0)
     mixed_all = jnp.transpose(mixed_parts, (1, 2, 0, 3)).reshape(sample_count, local_rows, width_all)
     tiles_here = owner_tiles[0]
     is_mouse = tiles_here >= HTILES
@@ -155,7 +171,7 @@
         for kernel_tap_index in range(tap_count)
     ]
     conv_grad = jnp.stack(per_tap, axis=1)
-    total_sq = lax.psum(lax.psum(lax.psum(jnp.sum(grad_share * grad_share), "trk"), "seq"), "sec")
+    total_sq = butterfly_sum(jnp.sum(grad_share * grad_share))
     entries = width_all * lax.axis_size("trk") * slot_count * lane_count
     factor = jnp.minimum(1.0, grad_clip * lax.rsqrt(total_sq / entries + 1e-06))
     head_grad = (grad_share * factor).reshape(share_rows, 1, slot_count, lane_count)

time: 291 us -> 281 us (0.966)
  blocking collectives: 73 us -> 0 us
  starting transfers between devices: 22.3 us -> 58.6 us
  waiting for transfers between devices: 79.7 us -> 94.3 us
  local copies, waits for them, and re-layouts: 41.9 us -> 49 us
  between operations: 15 us -> 19.1 us
    psum x3 -> x0, blocking collectives: 41.2 us -> none  [the longest x1 20.3 us: body(): lax.psum(jnp.sum(grad_share * grad_share), 'trk')]
    ppermute x0 -> x14, starting transfers between devices: none -> 36.2 us  [the longest x7 22 us: butterfly_sum(): lax.ppermute(value, axis, [(i, i ^ bit) for i in range(count)])]
    all_gather x1 -> x0, blocking collectives: 31.7 us -> none  [body(): mixed_parts = lax.all_gather(mixed_share, 'trk', axis=0, tiled=False)]
    ppermute x0 -> x14, waiting for transfers between devices: none -> 10.9 us  [the longest x7 6.97 us: butterfly_sum(): lax.ppermute(value, axis, [(i, i ^ bit) for i in range(count)])]
    ppermute x1, waiting for transfers between devices: 10.8 us -> 17 us  [ring_scatter(): lax.ppermute(other, 'sec', [(i, (i - shift) % sec_n) for i in range(sec_n)])]
    ppermute x3, waiting for transfers between devices: 58 us -> 53.7 us  [ring_scatter(): got_a = lax.ppermute(send_a, 'seq', to_next)]
    unnamed x35, local copies, waits for them, and re-layouts: 18.8 us -> 22.9 us
    all_to_all x1, waiting for transfers between devices: 3.22 us -> 6.98 us  [body(): lax.all_to_all(padded_input.reshape(sample_count, local_rows + 2 * DILATI...]
  transfers between devices with their start and end apart: 13 -> 27, of which waited for: 9 -> 16; matrix products, arithmetic and copies ran while one was open for 21% -> 24% of each run, Pallas kernels for 0% -> 0%
where the time goes in v5:
time: 281 us; the launch traced here: 279 us
  waiting for transfers between devices  94.3 us (34%)
  starting transfers between devices  58.6 us (21%)
  local copies, waits for them, and re-layouts  49 us (17%)
  other arithmetic  34.1 us (12%)
  matrix products  24.1 us (9%)
  between operations  19.1 us (7%)
    ppermute x3, waiting for transfers between devices, ring_scatter(): got_a = lax.ppermute(send_a, 'seq', to_next)  53.7 us
    unnamed x35, local copies, waits for them, and re-layouts  22.9 us
    ppermute x7, starting transfers between devices, butterfly_sum(): lax.ppermute(value, axis, [(i, i ^ bit) for i in range(count)])  22 us
    ppermute x1, waiting for transfers between devices, ring_scatter(): lax.ppermute(other, 'sec', [(i, (i - shift) % sec_n) for i in range(sec_n)])  17 us
    ppermute x7, starting transfers between devices, body(): lax.ppermute(mixed_share, 'trk', [(i, (i + k) % trk_n) for i in range(trk...  14.2 us
    ppermute x3, starting transfers between devices, ring_scatter(): got_b = lax.ppermute(send_b, 'seq', to_prev)  10 us
    dot_general x1, matrix products, body(): jnp.dot(flat_mixed, weights_here, preferred_element_type=jnp.float32)  7.42 us
    add x1, other arithmetic, ring_scatter(): summed = keep + lax.ppermute(give, 'seq', core_pairs)  7.09 us
  transfers between devices with their start and end apart: 27, of which 16 were waited for; matrix products, arithmetic and copies ran while one was open for 24% of the time, Pallas kernels for 0%

profile of v5, /device:TPU:0, one launch (start us, length us, event | category | flops | bytes accessed | tf_op | source)
XLA Modules:
  0.0 279.2 jit_solution(13412768640120358258)
XLA Ops:
  8.0 1.4 multiply_reduce_fusion
  9.4 1.8 fusion.12
  12.0 1.3 collective-permute-start.1
  13.3 3.0 %collective-permute-start = (bf16[4,16,1536]{2,1,0:T(8,128)(2,1)}, bf16[4,16,1536]{2,1,0:T(8,128)(2,1)S(1)}, u32[]{:S(2)}, u32[]{:S(2)}) collective-permute-start(bf16[4,16,1536]{2,1,0:T(8,128)(2,1)} %get-tuple-element.13), channel_id=1, source_target_pairs={{0,8},{8,16},{16,24},{24,32},{32,40},{40,48},{48,56},{1,9},{9,17},... | collective-permute-start | bytes 589832 | tf_op jit(solution)/shard_map/ppermute | solution.py:25
  16.4 1.4 convert_element_type.38
  17.8 2.1 copy.35
  20.7 10.7 %copy.34 = bf16[1536,1,20,128]{0,3,2,1:T(8,128)(2,1)} copy(bf16[1536,1,20,128]{3,0,2,1:T(8,128)(2,1)} %param.10) | data formatting | bytes 15728640 | tf_op args[3]
  31.5 1.4 bitcast_multiply_fusion
  32.9 1.8 fusion.25
  34.7 1.4 fusion.21
  36.2 2.2 bitcast_dynamic-update-slice_fusion.7
  38.4 2.0 collective-permute-start.2
  40.5 3.7 %collective-permute-start.3 = (bf16[4,64,192]{2,1,0:T(8,128)(2,1)S(1)}, bf16[4,64,192]{2,1,0:T(8,128)(2,1)S(1)}, u32[]{:S(2)}, u32[]{:S(2)}) collective-permute-start(bf16[4,64,192]{2,1,0:T(8,128)(2,1)S(1)} %get-tuple-element.20), channel_id=1, source_target_pairs={{0,2},{1,3},{2,4},{3,5},{4,6},{5,7},{6,0},{7,1},{8,10},{9,11},{10,... | collective-permute-start | bytes 294920 | tf_op jit(solution)/shard_map/ppermute | solution.py:111
  44.1 2.0 collective-permute-start.4
  46.6 2.0 collective-permute-start.6
  48.6 3.0 %collective-permute-start.7 = (bf16[4,64,192]{2,1,0:T(8,128)(2,1)S(1)}, bf16[4,64,192]{2,1,0:T(8,128)(2,1)S(1)}, u32[]{:S(2)}, u32[]{:S(2)}) collective-permute-start(bf16[4,64,192]{2,1,0:T(8,128)(2,1)S(1)} %get-tuple-element.20), channel_id=1, source_target_pairs={{0,6},{1,7},{2,0},{3,1},{4,2},{5,3},{6,4},{7,5},{8,14},{9,15},{10,... | collective-permute-start | bytes 294920 | tf_op jit(solution)/shard_map/ppermute | solution.py:111
  57.6 2.9 %collective-permute-done.8 = bf16[4,64,192]{2,1,0:T(8,128)(2,1)S(1)} collective-permute-done((bf16[4,64,192]{2,1,0:T(8,128)(2,1)S(1)}, bf16[4,64,192]{2,1,0:T(8,128)(2,1)S(1)}, u32[]{:S(2)}, u32[]{:S(2)}) %collective-permute-start.8) | collective-permute-done | bytes 98336 | tf_op jit(solution)/shard_map/ppermute | solution.py:111
  61.2 2.8 %gather_fusion = bf16[8,4,64,192]{3,2,1,0:T(8,128)(2,1)} fusion(bf16[8,4,64,192]{3,2,1,0:T(8,128)(2,1)} %bitcast_dynamic-update-slice_fusion, s32[1024]{0:T(1024)S(1)} %pad_clamp_fusion), kind=kCustom, calls=%fused_computation | custom fusion | bytes 1572896 | tf_op jit(solution)/shard_map/jit(_take)/gather | solution.py:115
  64.0 1.4 select_bitcast_fusion
  65.4 1.6 copy.33
  66.9 2.7 reshape_reshape.3
  69.6 7.4 %fusion.4 = bf16[256,2560]{1,0:T(8,128)(2,1)S(1)} fusion(f32[32,8,20,128]{3,2,1,0:T(8,128)S(1)} %bitcast.139, f32[4,2560]{1,0:T(4,128)} %bitcast_multiply_fusion, bf16[256,1536]{1,0:T(8,128)(2,1)} %reshape_reshape.3, bf16[1536,2560]{0,1:T(8,128)(2,1)} %bitcast.133), kind=kOutput, calls=%fused_computation.9 | convolution fusion | flops 2022440960 | bytes 12623872 | tf_op jit(solution)/shard_map/dot_general | solution.py:130
  77.1 2.2 fusion.42
  79.4 4.0 %dynamic-slice_bitcast_fusion = f32[2,4,96,2560]{3,2,1,0:T(8,128)} fusion(f32[2,4,2,96,2560]{4,3,2,1,0:T(8,128)S(1)} %bitcast.131, s32[]{:T(128)S(6)} %select_n.162), kind=kLoop, calls=%fused_computation.2 | loop fusion | bytes 15728644 | tf_op jit(solution)/shard_map/jit(dynamic_index_in_dim)/squeeze | solution.py:50
  83.3 4.0 %copy-done = f32[1536,2560]{1,0:T(8,128)} copy-done((f32[1536,2560]{1,0:T(8,128)}, f32[1536,2560]{1,0:T(8,128)S(1)}, u32[]{:S(2)}) %copy-start) | copy-done | bytes 15728664
  87.4 5.4 %convolution_bitcast_fusion = f32[1536,256]{0,1:T(8,128)S(1)} fusion(bf16[256,2560]{1,0:T(8,128)(2,1)S(1)} %copy-done.6, bf16[1536,2560]{0,1:T(8,128)(2,1)} %bitcast.134), kind=kOutput, calls=%fused_computation.4 | convolution fusion | flops 2013265920 | bytes 10747904 | tf_op jit(solution)/shard_map/dot_general | solution.py:148
  92.8 1.6 copy.43
  94.7 5.4 %collective-permute-done.9 = f32[2,4,96,2560]{3,2,1,0:T(8,128)} collective-permute-done((f32[2,4,96,2560]{3,2,1,0:T(8,128)}, f32[2,4,96,2560]{3,2,1,0:T(8,128)}, u32[]{:S(2)}, u32[]{:S(2)}) %collective-permute-start.9) | collective-permute-done | bytes 7864352 | tf_op jit(solution)/shard_map/ppermute | solution.py:52
  100.1 7.1 %bitcast_add_fusion = f32[2,4,96,2560]{3,2,1,0:T(8,128)S(1)} fusion(f32[2,4,96,2560]{3,2,1,0:T(8,128)} %collective-permute-done.9, f32[2,4,2,96,2560]{4,3,2,1,0:T(8,128)} %bitcast.132, s32[]{:T(128)S(6)} %select_n.161), kind=kLoop, calls=%fused_computation.1 | loop fusion | flops 1966080 | bytes 23592964 | tf_op jit(solution)/shard_map/add | solution.py:52
  107.2 2.6 fusion.39
  109.8 1.9 copy-done.1
  111.8 1.5 collective-permute-start.10
  113.3 1.3 dynamic-slice_bitcast_fusion.1
  114.6 1.8 collective-permute-start.13
  116.5 20.4 %collective-permute-done.10 = f32[2,96,1280]{2,1,0:T(8,128)S(1)} collective-permute-done((f32[2,96,1280]{2,1,0:T(8,128)S(1)}, f32[2,96,1280]{2,1,0:T(8,128)S(1)}, u32[]{:S(2)}, u32[]{:S(2)}) %collective-permute-start.10) | collective-permute-done | bytes 983072 | tf_op jit(solution)/shard_map/ppermute | solution.py:61
  136.9 2.3 bitcast_add_fusion.6
  139.4 2.6 bitcast_add_fusion.3
  142.0 3.0 %collective-permute-start.14 = (f32[2,96,1280]{2,1,0:T(8,128)}, f32[2,96,1280]{2,1,0:T(8,128)}, u32[]{:S(2)}, u32[]{:S(2)}) collective-permute-start(f32[2,96,1280]{2,1,0:T(8,128)} %bitcast_add_fusion.3), channel_id=1, source_target_pairs={{0,48},{8,56},{16,0},{24,8},{32,16},{40,24},{48,32},{56,40},{1,49}... | collective-permute-start | bytes 2949128 | tf_op jit(solution)/shard_map/ppermute | solution.py:62
  144.9 1.6 convert_element_type.47
  146.6 1.4 broadcast_in_dim_reshape.3
  148.0 1.6 copy.32
  149.6 3.7 %all-to-all-start = ((bf16[1,4,96,16,96]{4,2,1,0,3:T(8,128)(2,1)}), bf16[1,4,96,16,96]{4,2,1,0,3:T(8,128)(2,1)S(1)}, u32[]{:S(2)}, u32[]{:S(2)}) async-start(bf16[1,4,96,16,96]{4,2,1,0,3:T(8,128)(2,1)} %copy.32), calls=%async_computation | async-start | bytes 3145728 | tf_op jit(solution)/shard_map/all_to_all | solution.py:154
  153.3 16.7 %collective-permute-done.11 = f32[2,96,1280]{2,1,0:T(8,128)} collective-permute-done((f32[2,96,1280]{2,1,0:T(8,128)}, f32[2,96,1280]{2,1,0:T(8,128)}, u32[]{:S(2)}, u32[]{:S(2)}) %collective-permute-start.11) | collective-permute-done | bytes 983072 | tf_op jit(solution)/shard_map/ppermute | solution.py:61
  170.0 2.5 bitcast_add_fusion.5
  172.5 2.6 bitcast_add_fusion.2
  175.1 5.2 %collective-permute-start.15 = (f32[2,96,1280]{2,1,0:T(8,128)}, f32[2,96,1280]{2,1,0:T(8,128)}, u32[]{:S(2)}, u32[]{:S(2)}) collective-permute-start(f32[2,96,1280]{2,1,0:T(8,128)} %bitcast_add_fusion.2), channel_id=1, source_target_pairs={{0,48},{8,56},{16,0},{24,8},{32,16},{40,24},{48,32},{56,40},{1,49}... | collective-permute-start | bytes 2949128 | tf_op jit(solution)/shard_map/ppermute | solution.py:62
  180.3 7.0 %all-to-all-done = bf16[1,4,96,16,96]{4,2,1,0,3:T(8,128)(2,1)S(1)} async-done(((bf16[1,4,96,16,96]{4,2,1,0,3:T(8,128)(2,1)}), bf16[1,4,96,16,96]{4,2,1,0,3:T(8,128)(2,1)S(1)}, u32[]{:S(2)}, u32[]{:S(2)}) %all-to-all-start) | async-done | bytes 1179680 | tf_op jit(solution)/shard_map/all_to_all | solution.py:154
  187.3 2.4 fusion.40
  189.6 16.6 %collective-permute-done.12 = f32[2,96,1280]{2,1,0:T(8,128)} collective-permute-done((f32[2,96,1280]{2,1,0:T(8,128)}, f32[2,96,1280]{2,1,0:T(8,128)}, u32[]{:S(2)}, u32[]{:S(2)}) %collective-permute-start.12) | collective-permute-done | bytes 983072 | tf_op jit(solution)/shard_map/ppermute | solution.py:61
  206.3 1.6 bitcast_add_fusion.4
  208.1 1.6 bitcast_add_fusion.1
  210.7 2.3 collective-permute-start.16
  213.0 2.5 convolution_bitcast_fusion.1
  217.4 17.0 %collective-permute-done.16 = f32[96,2560]{1,0:T(8,128)} collective-permute-done((f32[96,2560]{1,0:T(8,128)}, f32[96,2560]{1,0:T(8,128)}, u32[]{:S(2)}, u32[]{:S(2)}) %collective-permute-start.16) | collective-permute-done | bytes 983072 | tf_op jit(solution)/shard_map/ppermute | solution.py:69
  234.4 2.1 multiply_reduce_fusion.1
  236.5 1.4 collective-permute-done.17
  239.1 2.5 collective-permute-start.18
  243.5 4.4 %collective-permute-start.19 = (f32[]{:T(128)}, f32[]{:T(128)}, u32[]{:S(2)}, u32[]{:S(2)}) collective-permute-start(f32[]{:T(128)} %add.301), channel_id=1, source_target_pairs={{0,32},{8,40},{16,48},{24,56},{32,0},{40,8},{48,16},{56,24},{1,33}... | collective-permute-start | bytes 20 | tf_op jit(solution)/shard_map/ppermute | solution.py:80
  249.3 1.9 collective-permute-start.20
  251.2 1.9 collective-permute-done.20
  253.6 5.4 %collective-permute-start.21 = (f32[]{:T(128)}, f32[]{:T(128)}, u32[]{:S(2)}, u32[]{:S(2)}) collective-permute-start(f32[]{:T(128)} %add.303), channel_id=1, source_target_pairs={{0,2},{1,3},{2,0},{3,1},{4,6},{5,7},{6,4},{7,5},{8,10},{9,11},{10,... | collective-permute-start | bytes 20 | tf_op jit(solution)/shard_map/ppermute | solution.py:80
  260.0 3.1 %collective-permute-start.22 = (f32[]{:T(128)}, f32[]{:T(128)}, u32[]{:S(2)}, u32[]{:S(2)}) collective-permute-start(f32[]{:T(128)} %add.304), channel_id=1, source_target_pairs={{0,4},{1,5},{2,6},{3,7},{4,0},{5,1},{6,2},{7,3},{8,12},{9,13},{10,... | collective-permute-start | bytes 20 | tf_op jit(solution)/shard_map/ppermute | solution.py:80
  264.3 4.6 %collective-permute-start.23 = (f32[]{:T(128)}, f32[]{:T(128)}, u32[]{:S(2)}, u32[]{:S(2)}) collective-permute-start(f32[]{:T(128)} %add.305), channel_id=1, source_target_pairs={{0,64},{64,0},{1,65},{65,1},{2,66},{66,2},{3,67},{67,3},{4,68},{68... | collective-permute-start | bytes 20 | tf_op jit(solution)/shard_map/ppermute | solution.py:80
  270.3 2.1 reshape.203
  (79 shorter events, 17.4 us)
Async XLA Ops:
  7.2 9.3 %copy-start.4 = (bf16[4,64,1536]{2,1,0:T(8,128)(2,1)S(1)}, bf16[4,64,1536]{2,1,0:T(8,128)(2,1)}, u32[]{:S(2)}) copy-start(bf16[4,64,1536]{2,1,0:T(8,128)(2,1)} %param.7) | copy-start | bytes 2359300
  7.2 9.2 %copy-start.11 = (s32[1,20]{1,0:T(1,128)S(1)}, s32[1,20]{1,0:T(1,128)}, u32[]{:S(2)}) copy-start(s32[1,20]{1,0:T(1,128)} %param.12) | copy-start | bytes 244
  7.2 137.7 %reduce-scatter.4.cloned.1.call-start = ((), (), s32[]{:S(2)}) async-start(), calls=%async_computation.3 | async-start | bytes 1769472 | tf_op jit(solution)/shard_map/reduce_scatter | solution.py:149
  11.2 6.6 %copy-start.7 = (bf16[4,64,1536]{2,1,0:T(8,128)(2,1)}, bf16[4,64,1536]{2,1,0:T(8,128)(2,1)S(1)}, u32[]{:S(2)}) copy-start(bf16[4,64,1536]{2,1,0:T(8,128)(2,1)S(1)} %fusion.12) | copy-start | bytes 2359300
  12.0 22.7 %collective-permute-start.1 = (bf16[4,16,1536]{2,1,0:T(8,128)(2,1)}, bf16[4,16,1536]{2,1,0:T(8,128)(2,1)S(1)}, u32[]{:S(2)}, u32[]{:S(2)}) collective-permute-start(bf16[4,16,1536]{2,1,0:T(8,128)(2,1)} %get-tuple-element.14), channel_id=1, source_target_pairs={{8,0},{16,8},{24,16},{32,24},{40,32},{48,40},{56,48},{9,1},{17,9},... | collective-permute-start | bytes 589832 | tf_op jit(solution)/shard_map/ppermute | solution.py:27
  13.3 22.9 %collective-permute-start = (bf16[4,16,1536]{2,1,0:T(8,128)(2,1)}, bf16[4,16,1536]{2,1,0:T(8,128)(2,1)S(1)}, u32[]{:S(2)}, u32[]{:S(2)}) collective-permute-start(bf16[4,16,1536]{2,1,0:T(8,128)(2,1)} %get-tuple-element.13), channel_id=1, source_target_pairs={{0,8},{8,16},{16,24},{24,32},{32,40},{40,48},{48,56},{1,9},{9,17},... | collective-permute-start | bytes 589832 | tf_op jit(solution)/shard_map/ppermute | solution.py:25
  17.8 2.1 copy-start.12
  32.9 1.8 copy-start.8
  38.4 10.2 %collective-permute-start.2 = (bf16[4,64,192]{2,1,0:T(8,128)(2,1)S(1)}, bf16[4,64,192]{2,1,0:T(8,128)(2,1)S(1)}, u32[]{:S(2)}, u32[]{:S(2)}) collective-permute-start(bf16[4,64,192]{2,1,0:T(8,128)(2,1)S(1)} %get-tuple-element.20), channel_id=1, source_target_pairs={{0,1},{1,2},{2,3},{3,4},{4,5},{5,6},{6,7},{7,0},{8,9},{9,10},{10,1... | collective-permute-start | bytes 294920 | tf_op jit(solution)/shard_map/ppermute | solution.py:111
  40.5 11.8 %collective-permute-start.3 = (bf16[4,64,192]{2,1,0:T(8,128)(2,1)S(1)}, bf16[4,64,192]{2,1,0:T(8,128)(2,1)S(1)}, u32[]{:S(2)}, u32[]{:S(2)}) collective-permute-start(bf16[4,64,192]{2,1,0:T(8,128)(2,1)S(1)} %get-tuple-element.20), channel_id=1, source_target_pairs={{0,2},{1,3},{2,4},{3,5},{4,6},{5,7},{6,0},{7,1},{8,10},{9,11},{10,... | collective-permute-start | bytes 294920 | tf_op jit(solution)/shard_map/ppermute | solution.py:111
  44.1 9.8 %collective-permute-start.4 = (bf16[4,64,192]{2,1,0:T(8,128)(2,1)S(1)}, bf16[4,64,192]{2,1,0:T(8,128)(2,1)S(1)}, u32[]{:S(2)}, u32[]{:S(2)}) collective-permute-start(bf16[4,64,192]{2,1,0:T(8,128)(2,1)S(1)} %get-tuple-element.20), channel_id=1, source_target_pairs={{0,3},{1,4},{2,5},{3,6},{4,7},{5,0},{6,1},{7,2},{8,11},{9,12},{10,... | collective-permute-start | bytes 294920 | tf_op jit(solution)/shard_map/ppermute | solution.py:111
  46.1 8.5 %collective-permute-start.5 = (bf16[4,64,192]{2,1,0:T(8,128)(2,1)S(1)}, bf16[4,64,192]{2,1,0:T(8,128)(2,1)S(1)}, u32[]{:S(2)}, u32[]{:S(2)}) collective-permute-start(bf16[4,64,192]{2,1,0:T(8,128)(2,1)S(1)} %get-tuple-element.20), channel_id=1, source_target_pairs={{0,4},{1,5},{2,6},{3,7},{4,0},{5,1},{6,2},{7,3},{8,12},{9,13},{10,... | collective-permute-start | bytes 294920 | tf_op jit(solution)/shard_map/ppermute | solution.py:111
  46.6 9.7 %collective-permute-start.6 = (bf16[4,64,192]{2,1,0:T(8,128)(2,1)S(1)}, bf16[4,64,192]{2,1,0:T(8,128)(2,1)S(1)}, u32[]{:S(2)}, u32[]{:S(2)}) collective-permute-start(bf16[4,64,192]{2,1,0:T(8,128)(2,1)S(1)} %get-tuple-element.20), channel_id=1, source_target_pairs={{0,5},{1,6},{2,7},{3,0},{4,1},{5,2},{6,3},{7,4},{8,13},{9,14},{10,... | collective-permute-start | bytes 294920 | tf_op jit(solution)/shard_map/ppermute | solution.py:111
  48.6 8.4 %collective-permute-start.7 = (bf16[4,64,192]{2,1,0:T(8,128)(2,1)S(1)}, bf16[4,64,192]{2,1,0:T(8,128)(2,1)S(1)}, u32[]{:S(2)}, u32[]{:S(2)}) collective-permute-start(bf16[4,64,192]{2,1,0:T(8,128)(2,1)S(1)} %get-tuple-element.20), channel_id=1, source_target_pairs={{0,6},{1,7},{2,0},{3,1},{4,2},{5,3},{6,4},{7,5},{8,14},{9,15},{10,... | collective-permute-start | bytes 294920 | tf_op jit(solution)/shard_map/ppermute | solution.py:111
  52.2 8.3 %collective-permute-start.8 = (bf16[4,64,192]{2,1,0:T(8,128)(2,1)S(1)}, bf16[4,64,192]{2,1,0:T(8,128)(2,1)S(1)}, u32[]{:S(2)}, u32[]{:S(2)}) collective-permute-start(bf16[4,64,192]{2,1,0:T(8,128)(2,1)S(1)} %get-tuple-element.20), channel_id=1, source_target_pairs={{0,7},{1,0},{2,1},{3,2},{4,3},{5,4},{6,5},{7,6},{8,15},{9,8},{10,9... | collective-permute-start | bytes 294920 | tf_op jit(solution)/shard_map/ppermute | solution.py:111
  69.6 7.4 %copy-start.3 = (bf16[256,1536]{1,0:T(8,128)(2,1)S(1)}, bf16[256,1536]{1,0:T(8,128)(2,1)}, u32[]{:S(2)}) copy-start(bf16[256,1536]{1,0:T(8,128)(2,1)} %reshape_reshape.3) | copy-start | bytes 2359300
  77.1 2.3 copy-start.5
  79.3 8.0 %copy-start = (f32[1536,2560]{1,0:T(8,128)}, f32[1536,2560]{1,0:T(8,128)S(1)}, u32[]{:S(2)}) copy-start(f32[1536,2560]{1,0:T(8,128)S(1)} %fusion.42) | copy-start | bytes 47185924
  79.3 8.0 %copy-start.6 = (bf16[256,2560]{1,0:T(8,128)(2,1)S(1)}, bf16[256,2560]{1,0:T(8,128)(2,1)}, u32[]{:S(2)}) copy-start(bf16[256,2560]{1,0:T(8,128)(2,1)} %copy-done.5) | copy-start | bytes 3932164
  87.4 12.8 %collective-permute-start.9 = (f32[2,4,96,2560]{3,2,1,0:T(8,128)}, f32[2,4,96,2560]{3,2,1,0:T(8,128)}, u32[]{:S(2)}, u32[]{:S(2)}) collective-permute-start(f32[2,4,96,2560]{3,2,1,0:T(8,128)} %dynamic-slice_bitcast_fusion), channel_id=1, source_target_pairs={{0,8},{8,0},{16,24},{24,16},{32,40},{40,32},{48,56},{56,48},{1,9},... | collective-permute-start | bytes 23592968 | tf_op jit(solution)/shard_map/ppermute | solution.py:52
  94.4 118.6 %all-gather.3.cloned.1.call-start = ((), (), s32[]{:S(2)}) async-start(), calls=%async_computation.2 | async-start | bytes 1671168 | tf_op jit(solution)/shard_map/all_gather | solution.py:161
  109.8 1.9 copy-start.1
  111.8 25.1 %collective-permute-start.10 = (f32[2,96,1280]{2,1,0:T(8,128)S(1)}, f32[2,96,1280]{2,1,0:T(8,128)S(1)}, u32[]{:S(2)}, u32[]{:S(2)}) collective-permute-start(f32[2,96,1280]{2,1,0:T(8,128)S(1)} %dynamic-slice_bitcast_fusion.2), channel_id=1, source_target_pairs={{0,16},{8,24},{16,32},{24,40},{32,48},{40,56},{48,0},{56,8},{1,17}... | collective-permute-start | bytes 2949128 | tf_op jit(solution)/shard_map/ppermute | solution.py:61
  114.6 24.8 %collective-permute-start.13 = (f32[2,96,1280]{2,1,0:T(8,128)S(1)}, f32[2,96,1280]{2,1,0:T(8,128)}, u32[]{:S(2)}, u32[]{:S(2)}) collective-permute-start(f32[2,96,1280]{2,1,0:T(8,128)S(1)} %dynamic-slice_bitcast_fusion.1), channel_id=1, source_target_pairs={{0,48},{8,56},{16,0},{24,8},{32,16},{40,24},{48,32},{56,40},{1,49}... | collective-permute-start | bytes 2949128 | tf_op jit(solution)/shard_map/ppermute | solution.py:62
  139.1 7.4 %copy-start.9 = (bf16[4,64,1536]{2,1,0:T(8,128)(2,1)S(1)}, bf16[4,64,1536]{2,1,0:T(8,128)(2,1)}, u32[]{:S(2)}) copy-start(bf16[4,64,1536]{2,1,0:T(8,128)(2,1)} %copy-done.7) | copy-start | bytes 2359300
  139.1 30.8 %collective-permute-start.11 = (f32[2,96,1280]{2,1,0:T(8,128)}, f32[2,96,1280]{2,1,0:T(8,128)}, u32[]{:S(2)}, u32[]{:S(2)}) collective-permute-start(f32[2,96,1280]{2,1,0:T(8,128)} %bitcast_add_fusion.6), channel_id=1, source_target_pairs={{0,16},{8,24},{16,32},{24,40},{32,48},{40,56},{48,0},{56,8},{1,17}... | collective-permute-start | bytes 2949128 | tf_op jit(solution)/shard_map/ppermute | solution.py:61
  142.0 30.6 %collective-permute-start.14 = (f32[2,96,1280]{2,1,0:T(8,128)}, f32[2,96,1280]{2,1,0:T(8,128)}, u32[]{:S(2)}, u32[]{:S(2)}) collective-permute-start(f32[2,96,1280]{2,1,0:T(8,128)} %bitcast_add_fusion.3), channel_id=1, source_target_pairs={{0,48},{8,56},{16,0},{24,8},{32,16},{40,24},{48,32},{56,40},{1,49}... | collective-permute-start | bytes 2949128 | tf_op jit(solution)/shard_map/ppermute | solution.py:62
  149.6 37.7 %all-to-all-start = ((bf16[1,4,96,16,96]{4,2,1,0,3:T(8,128)(2,1)}), bf16[1,4,96,16,96]{4,2,1,0,3:T(8,128)(2,1)S(1)}, u32[]{:S(2)}, u32[]{:S(2)}) async-start(bf16[1,4,96,16,96]{4,2,1,0,3:T(8,128)(2,1)} %copy.32), calls=%async_computation | async-start | bytes 3145728 | tf_op jit(solution)/shard_map/all_to_all | solution.py:154
  172.5 33.7 %collective-permute-start.12 = (f32[2,96,1280]{2,1,0:T(8,128)}, f32[2,96,1280]{2,1,0:T(8,128)}, u32[]{:S(2)}, u32[]{:S(2)}) collective-permute-start(f32[2,96,1280]{2,1,0:T(8,128)} %bitcast_add_fusion.5), channel_id=1, source_target_pairs={{0,16},{8,24},{16,32},{24,40},{32,48},{40,56},{48,0},{56,8},{1,17}... | collective-permute-start | bytes 2949128 | tf_op jit(solution)/shard_map/ppermute | solution.py:61
  175.1 33.0 %collective-permute-start.15 = (f32[2,96,1280]{2,1,0:T(8,128)}, f32[2,96,1280]{2,1,0:T(8,128)}, u32[]{:S(2)}, u32[]{:S(2)}) collective-permute-start(f32[2,96,1280]{2,1,0:T(8,128)} %bitcast_add_fusion.2), channel_id=1, source_target_pairs={{0,48},{8,56},{16,0},{24,8},{32,16},{40,24},{48,32},{56,40},{1,49}... | collective-permute-start | bytes 2949128 | tf_op jit(solution)/shard_map/ppermute | solution.py:62
  210.7 23.7 %collective-permute-start.16 = (f32[96,2560]{1,0:T(8,128)}, f32[96,2560]{1,0:T(8,128)}, u32[]{:S(2)}, u32[]{:S(2)}) collective-permute-start(f32[96,2560]{1,0:T(8,128)} %fusion.17), channel_id=1, source_target_pairs={{0,64},{64,0},{1,65},{65,1},{2,66},{66,2},{3,67},{67,3},{4,68},{68... | collective-permute-start | bytes 2949128 | tf_op jit(solution)/shard_map/ppermute | solution.py:69
  213.0 2.5 copy-start.2
  213.0 2.5 copy-start.10
  236.5 1.4 collective-permute-start.17
  239.1 3.8 %collective-permute-start.18 = (f32[]{:T(128)}, f32[]{:T(128)}, u32[]{:S(2)}, u32[]{:S(2)}) collective-permute-start(f32[]{:T(128)} %add.300), channel_id=1, source_target_pairs={{0,16},{8,24},{16,0},{24,8},{32,48},{40,56},{48,32},{56,40},{1,17}... | collective-permute-start | bytes 20 | tf_op jit(solution)/shard_map/ppermute | solution.py:80
  243.5 5.3 %collective-permute-start.19 = (f32[]{:T(128)}, f32[]{:T(128)}, u32[]{:S(2)}, u32[]{:S(2)}) collective-permute-start(f32[]{:T(128)} %add.301), channel_id=1, source_target_pairs={{0,32},{8,40},{16,48},{24,56},{32,0},{40,8},{48,16},{56,24},{1,33}... | collective-permute-start | bytes 20 | tf_op jit(solution)/shard_map/ppermute | solution.py:80
  249.3 3.8 %collective-permute-start.20 = (f32[]{:T(128)}, f32[]{:T(128)}, u32[]{:S(2)}, u32[]{:S(2)}) collective-permute-start(f32[]{:T(128)} %add.302), channel_id=1, source_target_pairs={{0,1},{1,0},{2,3},{3,2},{4,5},{5,4},{6,7},{7,6},{8,9},{9,8},{10,11... | collective-permute-start | bytes 20 | tf_op jit(solution)/shard_map/ppermute | solution.py:80
  253.6 5.8 %collective-permute-start.21 = (f32[]{:T(128)}, f32[]{:T(128)}, u32[]{:S(2)}, u32[]{:S(2)}) collective-permute-start(f32[]{:T(128)} %add.303), channel_id=1, source_target_pairs={{0,2},{1,3},{2,0},{3,1},{4,6},{5,7},{6,4},{7,5},{8,10},{9,11},{10,... | collective-permute-start | bytes 20 | tf_op jit(solution)/shard_map/ppermute | solution.py:80
  260.0 3.8 %collective-permute-start.22 = (f32[]{:T(128)}, f32[]{:T(128)}, u32[]{:S(2)}, u32[]{:S(2)}) collective-permute-start(f32[]{:T(128)} %add.304), channel_id=1, source_target_pairs={{0,4},{1,5},{2,6},{3,7},{4,0},{5,1},{6,2},{7,3},{8,12},{9,13},{10,... | collective-permute-start | bytes 20 | tf_op jit(solution)/shard_map/ppermute | solution.py:80
  264.3 5.3 %collective-permute-start.23 = (f32[]{:T(128)}, f32[]{:T(128)}, u32[]{:S(2)}, u32[]{:S(2)}) collective-permute-start(f32[]{:T(128)} %add.305), channel_id=1, source_target_pairs={{0,64},{64,0},{1,65},{65,1},{2,66},{66,2},{3,67},{67,3},{4,68},{68... | collective-permute-start | bytes 20 | tf_op jit(solution)/shard_map/ppermute | solution.py:80
Sparse Core Ops, SparseCore 0:
  94.5 44.2 reduce-scatter.3
  146.7 50.7 all-gather.2

commit v6 on v5

--- a/solution.py
+++ b/solution.py
@@ -107,12 +107,13 @@
     own_cols = lax.dynamic_slice_in_dim(inputs, lax.axis_index("trk") * out_share, out_share, 2)
     mixed_share = (own_cols + convolution_output).astype(jnp.bfloat16)
     trk_n = lax.axis_size("trk")
-    shifted = [mixed_share] + [
-        lax.ppermute(mixed_share, "trk", [(i, (i + k) % trk_n) for i in range(trk_n)])
-        for k in range(1, trk_n)
-    ]
-    order = (lax.axis_index("trk") - jnp.arange(trk_n)) % trk_n
-    mixed_parts = jnp.take(jnp.stack(shifted), order, axis=0)
+    mixed_parts = lax.all_to_all(
+        jnp.broadcast_to(mixed_share[:, :, None, :], (sample_count, local_rows, trk_n, out_share)),
+        "trk",
+        2,
+        0,
+        tiled=False,
+    )
     mixed_all = jnp.transpose(mixed_parts, (1, 2, 0, 3)).reshape(sample_count, local_rows, width_all)
     tiles_here = owner_tiles[0]
     is_mouse = tiles_here >= HTILES
@@ -171,7 +172,12 @@
         for kernel_tap_index in range(tap_count)
     ]
     conv_grad = jnp.stack(per_tap, axis=1)
-    total_sq = butterfly_sum(jnp.sum(grad_share * grad_share))
+    all_axes = ("sec", "seq", "trk")
+    device_count = lax.axis_size(all_axes)
+    sq_parts = lax.all_to_all(
+        jnp.broadcast_to(jnp.sum(grad_share * grad_share), (device_count,)), all_axes, 0, 0, tiled=True
+    )
+    total_sq = jnp.sum(sq_parts)
     entries = width_all * lax.axis_size("trk") * slot_count * lane_count
     factor = jnp.minimum(1.0, grad_clip * lax.rsqrt(total_sq / entries + 1e-06))
     head_grad = (grad_share * factor).reshape(share_rows, 1, slot_count, lane_count)

time: 281 us -> 245 us (0.87)
  starting transfers between devices: 58.6 us -> 37.9 us
  between operations: 19.1 us -> 15.1 us
  other arithmetic: 34.1 us -> 30.3 us
  local copies, waits for them, and re-layouts: 49 us -> 45.4 us
    ppermute x14 -> x0, starting transfers between devices: 36.2 us -> none  [the longest x7 22 us: butterfly_sum(): lax.ppermute(value, axis, [(i, i ^ bit) for i in range(count)])]
    all_to_all x0 -> x2, starting transfers between devices: none -> 16.6 us  [the longest x1 10.2 us: body(): lax.all_to_all(jnp.broadcast_to(jnp.sum(grad_share * grad_share), (device...]
    ppermute x14 -> x0, waiting for transfers between devices: 10.9 us -> none  [the longest x7 6.97 us: butterfly_sum(): lax.ppermute(value, axis, [(i, i ^ bit) for i in range(count)])]
    all_to_all x0 -> x2, waiting for transfers between devices: none -> 10.6 us  [the longest x1 8.71 us: body(): lax.all_to_all(jnp.broadcast_to(jnp.sum(grad_share * grad_share), (device...]
    ppermute x1, waiting for transfers between devices: 17 us -> 10.9 us  [ring_scatter(): lax.ppermute(other, 'sec', [(i, (i - shift) % sec_n) for i in range(sec_n)])]
    ppermute x3, waiting for transfers between devices: 53.7 us -> 58.4 us  [ring_scatter(): got_a = lax.ppermute(send_a, 'seq', to_next)]
    all_to_all x1, waiting for transfers between devices: 6.98 us -> 3.59 us  [body(): lax.all_to_all(padded_input.reshape(sample_count, local_rows + 2 * DILATI...]
    unnamed x35 -> x29, local copies, waits for them, and re-layouts: 22.9 us -> 19.5 us
  transfers between devices with their start and end apart: 27 -> 15, of which waited for: 16 -> 10; matrix products, arithmetic and copies ran while one was open for 24% -> 25% of each run, Pallas kernels for 0% -> 0%
where the time goes in v6:
time: 245 us; the launch traced here: 243 us
  waiting for transfers between devices  91.6 us (37%)
  local copies, waits for them, and re-layouts  45.4 us (19%)
  starting transfers between devices  37.9 us (15%)
  other arithmetic  30.3 us (12%)
  matrix products  23.1 us (9%)
  between operations  15.1 us (6%)
    ppermute x3, waiting for transfers between devices, ring_scatter(): got_a = lax.ppermute(send_a, 'seq', to_next)  58.4 us
    unnamed x29, local copies, waits for them, and re-layouts  19.5 us
    ppermute x1, waiting for transfers between devices, ring_scatter(): lax.ppermute(other, 'sec', [(i, (i - shift) % sec_n) for i in range(sec_n)])  10.9 us
    all_to_all x1, starting transfers between devices, body(): lax.all_to_all(jnp.broadcast_to(jnp.sum(grad_share * grad_share), (device...  10.2 us
    all_to_all x1, waiting for transfers between devices, body(): lax.all_to_all(jnp.broadcast_to(jnp.sum(grad_share * grad_share), (device...  8.71 us
    ppermute x3, starting transfers between devices, ring_scatter(): got_b = lax.ppermute(send_b, 'seq', to_prev)  8.45 us
    dot_general x1, matrix products, body(): jnp.dot(flat_mixed, weights_here, preferred_element_type=jnp.float32)  7.42 us
    add x1, other arithmetic, ring_scatter(): summed = keep + lax.ppermute(give, 'seq', core_pairs)  7.26 us
  transfers between devices with their start and end apart: 15, of which 10 were waited for; matrix products, arithmetic and copies ran while one was open for 25% of the time, Pallas kernels for 0%

profile of v6, /device:TPU:0, one launch (start us, length us, event | category | flops | bytes accessed | tf_op | source)
XLA Modules:
  0.0 243.4 jit_solution(3186703592719846293)
XLA Ops:
  7.2 0.8 convert_element_type.39
  8.0 1.4 multiply_reduce_fusion
  9.3 1.8 fusion.12
  11.2 1.3 collective-permute-start.1
  12.5 3.0 %collective-permute-start = (bf16[4,16,1536]{2,1,0:T(8,128)(2,1)S(1)}, bf16[4,16,1536]{2,1,0:T(8,128)(2,1)S(1)}, u32[]{:S(2)}, u32[]{:S(2)}) collective-permute-start(bf16[4,16,1536]{2,1,0:T(8,128)(2,1)S(1)} %get-tuple-element.13), channel_id=1, source_target_pairs={{0,8},{8,16},{16,24},{24,32},{32,40},{40,48},{48,56},{1,9},{9,17},... | collective-permute-start | bytes 589832 | tf_op jit(solution)/shard_map/ppermute | solution.py:25
  15.8 1.4 fusion.25
  17.5 0.7 broadcast_bitcast_fusion
  18.2 1.4 fusion.21
  19.7 1.5 fusion.15
  21.2 1.1 broadcast_in_dim_broadcast_in_dim.2
  22.2 6.4 %all-to-all-start.1 = ((bf16[1,4,64,8,192]{4,2,1,0,3:T(8,128)(2,1)}), bf16[1,4,64,8,192]{4,2,1,0,3:T(8,128)(2,1)}, u32[]{:S(2)}, u32[]{:S(2)}) async-start(bf16[1,4,64,8,192]{4,2,1,0,3:T(8,128)(2,1)} %broadcast_in_dim_broadcast_in_dim.2), calls=%async_computation.1 | async-start | bytes 2097152 | tf_op jit(solution)/shard_map/all_to_all | solution.py:110
  28.7 2.1 copy.58
  30.8 10.7 %copy.57 = bf16[1536,1,20,128]{0,3,2,1:T(8,128)(2,1)} copy(bf16[1536,1,20,128]{3,0,2,1:T(8,128)(2,1)} %param.10) | data formatting | bytes 15728640 | tf_op args[3]
  41.5 1.4 bitcast_multiply_fusion
  42.9 1.9 all-to-all-done.1
  44.8 2.8 %copy.56 = bf16[4,64,8,192]{3,2,1,0:T(8,128)(2,1)} copy(bf16[4,64,8,192]{3,1,0,2:T(8,128)(2,1)} %bitcast.13) | data formatting | bytes 1572864 | tf_op jit(solution)/shard_map/transpose | solution.py:117
  47.6 2.7 %reshape_reshape.3 = bf16[256,1536]{1,0:T(8,128)(2,1)} reshape(bf16[4,64,8,192]{3,2,1,0:T(8,128)(2,1)} %copy.56) | data formatting | bytes 1572864 | tf_op jit(solution)/shard_map/reshape;reshape | solution.py:130
  50.4 7.4 %fusion.4 = bf16[256,2560]{1,0:T(8,128)(2,1)S(1)} fusion(f32[32,8,20,128]{3,2,1,0:T(8,128)S(1)} %bitcast.124, f32[4,2560]{1,0:T(4,128)} %bitcast_multiply_fusion, bf16[256,1536]{1,0:T(8,128)(2,1)} %reshape_reshape.3, bf16[1536,2560]{0,1:T(8,128)(2,1)} %bitcast.118), kind=kOutput, calls=%fused_computation.8 | convolution fusion | flops 2022440960 | bytes 12623872 | tf_op jit(solution)/shard_map/dot_general | solution.py:131
  57.8 2.2 fusion.39
  60.1 4.0 %dynamic-slice_bitcast_fusion = f32[2,4,96,2560]{3,2,1,0:T(8,128)} fusion(f32[2,4,2,96,2560]{4,3,2,1,0:T(8,128)S(1)} %bitcast.116, s32[]{:T(128)S(6)} %select_n.115), kind=kLoop, calls=%fused_computation.1 | loop fusion | bytes 15728644 | tf_op jit(solution)/shard_map/jit(dynamic_index_in_dim)/squeeze | solution.py:50
  64.1 4.0 %copy-done = f32[1536,2560]{1,0:T(8,128)} copy-done((f32[1536,2560]{1,0:T(8,128)}, f32[1536,2560]{1,0:T(8,128)S(1)}, u32[]{:S(2)}) %copy-start) | copy-done | bytes 15728664
  68.1 5.4 %convolution_bitcast_fusion = f32[1536,256]{0,1:T(8,128)S(1)} fusion(bf16[256,2560]{1,0:T(8,128)(2,1)S(1)} %copy-done.6, bf16[1536,2560]{0,1:T(8,128)(2,1)} %bitcast.119), kind=kOutput, calls=%fused_computation.3 | convolution fusion | flops 2013265920 | bytes 10747904 | tf_op jit(solution)/shard_map/dot_general | solution.py:149
  73.5 1.6 copy.67
  75.2 5.6 %collective-permute-done.2 = f32[2,4,96,2560]{3,2,1,0:T(8,128)} collective-permute-done((f32[2,4,96,2560]{3,2,1,0:T(8,128)}, f32[2,4,96,2560]{3,2,1,0:T(8,128)}, u32[]{:S(2)}, u32[]{:S(2)}) %collective-permute-start.2) | collective-permute-done | bytes 7864352 | tf_op jit(solution)/shard_map/ppermute | solution.py:52
  80.8 7.3 %bitcast_add_fusion = f32[2,4,96,2560]{3,2,1,0:T(8,128)S(1)} fusion(f32[2,4,96,2560]{3,2,1,0:T(8,128)} %collective-permute-done.2, f32[2,4,2,96,2560]{4,3,2,1,0:T(8,128)} %bitcast.117, s32[]{:T(128)S(6)} %select_n.114), kind=kLoop, calls=%fused_computation | loop fusion | flops 1966080 | bytes 23592964 | tf_op jit(solution)/shard_map/add | solution.py:52
  88.1 2.6 %fusion.36 = (f32[2,4,96,1280]{3,2,1,0:T(8,128)}, f32[2,4,96,1280]{3,2,1,0:T(8,128)S(1)}) fusion(f32[2,4,96,2560]{3,2,1,0:T(8,128)S(1)} %bitcast_add_fusion), kind=kLoop, calls=%fused_computation.76 | loop fusion | bytes 15728640 | tf_op jit(solution)/shard_map/slice | solution.py:55
  90.7 1.9 copy-done.1
  92.7 1.6 collective-permute-start.3
  94.2 2.2 dynamic-slice_bitcast_fusion.1
  96.4 1.8 collective-permute-start.6
  98.2 19.5 %collective-permute-done.3 = f32[2,96,1280]{2,1,0:T(8,128)S(1)} collective-permute-done((f32[2,96,1280]{2,1,0:T(8,128)S(1)}, f32[2,96,1280]{2,1,0:T(8,128)S(1)}, u32[]{:S(2)}, u32[]{:S(2)}) %collective-permute-start.3) | collective-permute-done | bytes 983072 | tf_op jit(solution)/shard_map/ppermute | solution.py:61
  117.7 1.3 bitcast_add_fusion.6
  119.1 0.4 collective-permute-start.4
  119.4 0.9 collective-permute-done.6
  120.3 1.6 bitcast_add_fusion.3
  121.9 3.0 %collective-permute-start.7 = (f32[2,96,1280]{2,1,0:T(8,128)S(1)}, f32[2,96,1280]{2,1,0:T(8,128)}, u32[]{:S(2)}, u32[]{:S(2)}) collective-permute-start(f32[2,96,1280]{2,1,0:T(8,128)S(1)} %bitcast_add_fusion.3), channel_id=1, source_target_pairs={{0,48},{8,56},{16,0},{24,8},{32,16},{40,24},{48,32},{56,40},{1,49}... | collective-permute-start | bytes 2949128 | tf_op jit(solution)/shard_map/ppermute | solution.py:62
  124.9 1.6 convert_element_type.47
  126.5 17.9 %collective-permute-done.4 = f32[2,96,1280]{2,1,0:T(8,128)S(1)} collective-permute-done((f32[2,96,1280]{2,1,0:T(8,128)S(1)}, f32[2,96,1280]{2,1,0:T(8,128)S(1)}, u32[]{:S(2)}, u32[]{:S(2)}) %collective-permute-start.4) | collective-permute-done | bytes 983072 | tf_op jit(solution)/shard_map/ppermute | solution.py:61
  144.5 2.3 bitcast_add_fusion.5
  146.7 2.7 %bitcast_add_fusion.2 = f32[2,96,1280]{2,1,0:T(8,128)} fusion(f32[2,96,1280]{2,1,0:T(8,128)} %collective-permute-done.7, f32[2,4,96,1280]{3,2,1,0:T(8,128)} %get-tuple-element.8, s32[]{:T(128)S(6)} %select_n.130), kind=kLoop, calls=%fused_computation.37 | loop fusion | flops 245760 | bytes 2949124 | tf_op jit(solution)/shard_map/add | solution.py:64
  149.4 3.7 %collective-permute-start.8 = (f32[2,96,1280]{2,1,0:T(8,128)}, f32[2,96,1280]{2,1,0:T(8,128)}, u32[]{:S(2)}, u32[]{:S(2)}) collective-permute-start(f32[2,96,1280]{2,1,0:T(8,128)} %bitcast_add_fusion.2), channel_id=1, source_target_pairs={{0,48},{8,56},{16,0},{24,8},{32,16},{40,24},{48,32},{56,40},{1,49}... | collective-permute-start | bytes 2949128 | tf_op jit(solution)/shard_map/ppermute | solution.py:62
  153.2 1.4 broadcast_in_dim_reshape.3
  154.5 1.6 copy.55
  156.1 4.3 %all-to-all-start = ((bf16[1,4,96,16,96]{4,2,1,0,3:T(8,128)(2,1)}), bf16[1,4,96,16,96]{4,2,1,0,3:T(8,128)(2,1)S(1)}, u32[]{:S(2)}, u32[]{:S(2)}) async-start(bf16[1,4,96,16,96]{4,2,1,0,3:T(8,128)(2,1)} %copy.55), calls=%async_computation | async-start | bytes 3145728 | tf_op jit(solution)/shard_map/all_to_all | solution.py:155
  160.4 20.9 %collective-permute-done.5 = f32[2,96,1280]{2,1,0:T(8,128)} collective-permute-done((f32[2,96,1280]{2,1,0:T(8,128)}, f32[2,96,1280]{2,1,0:T(8,128)}, u32[]{:S(2)}, u32[]{:S(2)}) %collective-permute-start.5) | collective-permute-done | bytes 983072 | tf_op jit(solution)/shard_map/ppermute | solution.py:61
  181.3 1.6 bitcast_add_fusion.4
  182.9 1.5 collective-permute-done.8
  184.4 1.6 bitcast_add_fusion.1
  186.0 1.0 fusion.17
  187.1 2.3 collective-permute-start.9
  189.3 3.6 %all-to-all-done = bf16[1,4,96,16,96]{4,2,1,0,3:T(8,128)(2,1)S(1)} async-done(((bf16[1,4,96,16,96]{4,2,1,0,3:T(8,128)(2,1)}), bf16[1,4,96,16,96]{4,2,1,0,3:T(8,128)(2,1)S(1)}, u32[]{:S(2)}, u32[]{:S(2)}) %all-to-all-start) | async-done | bytes 1179680 | tf_op jit(solution)/shard_map/all_to_all | solution.py:155
  192.9 1.8 fusion.37
  194.7 2.5 %convolution_bitcast_fusion.1 = f32[96,1,192]{2,0,1:T(8,128)S(1)} fusion(bf16[16,256,96]{2,1,0:T(8,128)(2,1)} %bitcast.127, bf16[16,192,256]{2,1,0:T(8,128)(2,1)} %bitcast.121), kind=kOutput, calls=%fused_computation.28 | convolution fusion | flops 150994944 | bytes 2433024 | tf_op jit(solution)/shard_map/dot_general | solution.py:164
  197.2 0.6 convolution_bitcast_fusion.2
  197.8 0.6 copy-done.9
  198.4 0.6 convolution_bitcast_fusion.3
  199.0 10.9 %collective-permute-done.9 = f32[96,2560]{1,0:T(8,128)} collective-permute-done((f32[96,2560]{1,0:T(8,128)}, f32[96,2560]{1,0:T(8,128)}, u32[]{:S(2)}, u32[]{:S(2)}) %collective-permute-start.9) | collective-permute-done | bytes 983072 | tf_op jit(solution)/shard_map/ppermute | solution.py:69
  209.9 2.1 multiply_reduce_fusion.1
  212.0 1.3 broadcast_in_dim.15
  213.3 10.2 %all-to-all-start.2 = ((f32[128,1,1]{2,1,0:T(1,128)}), f32[128,1,1]{2,1,0:T(1,128)S(1)}, u32[]{:S(2)}, u32[]{:S(2)}) async-start(f32[128,1,1]{2,1,0:T(1,128)} %broadcast_in_dim.15), calls=%async_computation.2 | async-start | bytes 131072 | tf_op jit(solution)/shard_map/all_to_all | solution.py:177
  223.5 0.7 pad_maximum_fusion.5
  224.2 8.7 %all-to-all-done.2 = f32[128,1,1]{2,1,0:T(1,128)S(1)} async-done(((f32[128,1,1]{2,1,0:T(1,128)}), f32[128,1,1]{2,1,0:T(1,128)S(1)}, u32[]{:S(2)}, u32[]{:S(2)}) %all-to-all-start.2) | async-done | bytes 544 | tf_op jit(solution)/shard_map/all_to_all | solution.py:177
  232.9 0.7 reduce_sum.29
  234.4 2.1 reshape.152
  (46 shorter events, 0.8 us)
Async XLA Ops:
  7.2 8.5 %copy-start.4 = (bf16[4,64,1536]{2,1,0:T(8,128)(2,1)S(1)}, bf16[4,64,1536]{2,1,0:T(8,128)(2,1)}, u32[]{:S(2)}) copy-start(bf16[4,64,1536]{2,1,0:T(8,128)(2,1)} %param.7) | copy-start | bytes 2359300
  7.2 8.4 %copy-start.11 = (s32[1,20]{1,0:T(1,128)S(1)}, s32[1,20]{1,0:T(1,128)}, u32[]{:S(2)}) copy-start(s32[1,20]{1,0:T(1,128)} %param.12) | copy-start | bytes 244
  11.2 8.5 %copy-start.7 = (bf16[4,64,1536]{2,1,0:T(8,128)(2,1)}, bf16[4,64,1536]{2,1,0:T(8,128)(2,1)S(1)}, u32[]{:S(2)}) copy-start(bf16[4,64,1536]{2,1,0:T(8,128)(2,1)S(1)} %fusion.12) | copy-start | bytes 2359300
  11.2 4.6 %copy-start.12 = (s32[4]{0:T(128)S(1)}, s32[4]{0:T(128)}, u32[]{:S(2)}) copy-start(s32[4]{0:T(128)} %param.13) | copy-start | bytes 52
  11.2 7.0 %collective-permute-start.1 = (bf16[4,16,1536]{2,1,0:T(8,128)(2,1)S(1)}, bf16[4,16,1536]{2,1,0:T(8,128)(2,1)S(1)}, u32[]{:S(2)}, u32[]{:S(2)}) collective-permute-start(bf16[4,16,1536]{2,1,0:T(8,128)(2,1)S(1)} %get-tuple-element.14), channel_id=1, source_target_pairs={{8,0},{16,8},{24,16},{32,24},{40,32},{48,40},{56,48},{9,1},{17,9},... | collective-permute-start | bytes 589832 | tf_op jit(solution)/shard_map/ppermute | solution.py:27
  12.5 7.1 %collective-permute-start = (bf16[4,16,1536]{2,1,0:T(8,128)(2,1)S(1)}, bf16[4,16,1536]{2,1,0:T(8,128)(2,1)S(1)}, u32[]{:S(2)}, u32[]{:S(2)}) collective-permute-start(bf16[4,16,1536]{2,1,0:T(8,128)(2,1)S(1)} %get-tuple-element.13), channel_id=1, source_target_pairs={{0,8},{8,16},{16,24},{24,32},{32,40},{40,48},{48,56},{1,9},{9,17},... | collective-permute-start | bytes 589832 | tf_op jit(solution)/shard_map/ppermute | solution.py:25
  22.2 22.6 %all-to-all-start.1 = ((bf16[1,4,64,8,192]{4,2,1,0,3:T(8,128)(2,1)}), bf16[1,4,64,8,192]{4,2,1,0,3:T(8,128)(2,1)}, u32[]{:S(2)}, u32[]{:S(2)}) async-start(bf16[1,4,64,8,192]{4,2,1,0,3:T(8,128)(2,1)} %broadcast_in_dim_broadcast_in_dim.2), calls=%async_computation.1 | async-start | bytes 2097152 | tf_op jit(solution)/shard_map/all_to_all | solution.py:110
  28.7 96.2 %reduce-scatter.4.cloned.1.call-start = ((), (), s32[]{:S(2)}) async-start(), calls=%async_computation.5 | async-start | bytes 1769472 | tf_op jit(solution)/shard_map/reduce_scatter | solution.py:150
  50.4 7.4 %copy-start.3 = (bf16[256,1536]{1,0:T(8,128)(2,1)S(1)}, bf16[256,1536]{1,0:T(8,128)(2,1)}, u32[]{:S(2)}) copy-start(bf16[256,1536]{1,0:T(8,128)(2,1)} %reshape_reshape.3) | copy-start | bytes 2359300
  57.8 2.3 copy-start.5
  60.1 8.0 %copy-start = (f32[1536,2560]{1,0:T(8,128)}, f32[1536,2560]{1,0:T(8,128)S(1)}, u32[]{:S(2)}) copy-start(f32[1536,2560]{1,0:T(8,128)S(1)} %fusion.39) | copy-start | bytes 47185924
  60.1 8.0 %copy-start.6 = (bf16[256,2560]{1,0:T(8,128)(2,1)S(1)}, bf16[256,2560]{1,0:T(8,128)(2,1)}, u32[]{:S(2)}) copy-start(bf16[256,2560]{1,0:T(8,128)(2,1)} %copy-done.5) | copy-start | bytes 3932164
  68.1 12.8 %collective-permute-start.2 = (f32[2,4,96,2560]{3,2,1,0:T(8,128)}, f32[2,4,96,2560]{3,2,1,0:T(8,128)}, u32[]{:S(2)}, u32[]{:S(2)}) collective-permute-start(f32[2,4,96,2560]{3,2,1,0:T(8,128)} %dynamic-slice_bitcast_fusion), channel_id=1, source_target_pairs={{0,8},{8,0},{16,24},{24,16},{32,40},{40,32},{48,56},{56,48},{1,9},... | collective-permute-start | bytes 23592968 | tf_op jit(solution)/shard_map/ppermute | solution.py:52
  75.2 119.6 %all-gather.3.cloned.1.call-start = ((), (), s32[]{:S(2)}) async-start(), calls=%async_computation.4 | async-start | bytes 1671168 | tf_op jit(solution)/shard_map/all_gather | solution.py:162
  90.7 1.9 copy-start.1
  92.7 25.1 %collective-permute-start.3 = (f32[2,96,1280]{2,1,0:T(8,128)S(1)}, f32[2,96,1280]{2,1,0:T(8,128)S(1)}, u32[]{:S(2)}, u32[]{:S(2)}) collective-permute-start(f32[2,96,1280]{2,1,0:T(8,128)S(1)} %dynamic-slice_bitcast_fusion.2), channel_id=1, source_target_pairs={{0,16},{8,24},{16,32},{24,40},{32,48},{40,56},{48,0},{56,8},{1,17}... | collective-permute-start | bytes 2949128 | tf_op jit(solution)/shard_map/ppermute | solution.py:61
  96.4 23.8 %collective-permute-start.6 = (f32[2,96,1280]{2,1,0:T(8,128)}, f32[2,96,1280]{2,1,0:T(8,128)}, u32[]{:S(2)}, u32[]{:S(2)}) collective-permute-start(f32[2,96,1280]{2,1,0:T(8,128)} %dynamic-slice_bitcast_fusion.1), channel_id=1, source_target_pairs={{0,48},{8,56},{16,0},{24,8},{32,16},{40,24},{48,32},{56,40},{1,49}... | collective-permute-start | bytes 2949128 | tf_op jit(solution)/shard_map/ppermute | solution.py:62
  119.1 25.4 %collective-permute-start.4 = (f32[2,96,1280]{2,1,0:T(8,128)S(1)}, f32[2,96,1280]{2,1,0:T(8,128)S(1)}, u32[]{:S(2)}, u32[]{:S(2)}) collective-permute-start(f32[2,96,1280]{2,1,0:T(8,128)S(1)} %bitcast_add_fusion.6), channel_id=1, source_target_pairs={{0,16},{8,24},{16,32},{24,40},{32,48},{40,56},{48,0},{56,8},{1,17}... | collective-permute-start | bytes 2949128 | tf_op jit(solution)/shard_map/ppermute | solution.py:61
  121.9 24.8 %collective-permute-start.7 = (f32[2,96,1280]{2,1,0:T(8,128)S(1)}, f32[2,96,1280]{2,1,0:T(8,128)}, u32[]{:S(2)}, u32[]{:S(2)}) collective-permute-start(f32[2,96,1280]{2,1,0:T(8,128)S(1)} %bitcast_add_fusion.3), channel_id=1, source_target_pairs={{0,48},{8,56},{16,0},{24,8},{32,16},{40,24},{48,32},{56,40},{1,49}... | collective-permute-start | bytes 2949128 | tf_op jit(solution)/shard_map/ppermute | solution.py:62
  146.7 6.4 %copy-start.8 = (bf16[4,64,1536]{2,1,0:T(8,128)(2,1)S(1)}, bf16[4,64,1536]{2,1,0:T(8,128)(2,1)}, u32[]{:S(2)}) copy-start(bf16[4,64,1536]{2,1,0:T(8,128)(2,1)} %copy-done.7) | copy-start | bytes 2359300
  146.7 34.6 %collective-permute-start.5 = (f32[2,96,1280]{2,1,0:T(8,128)}, f32[2,96,1280]{2,1,0:T(8,128)}, u32[]{:S(2)}, u32[]{:S(2)}) collective-permute-start(f32[2,96,1280]{2,1,0:T(8,128)} %bitcast_add_fusion.5), channel_id=1, source_target_pairs={{0,16},{8,24},{16,32},{24,40},{32,48},{40,56},{48,0},{56,8},{1,17}... | collective-permute-start | bytes 2949128 | tf_op jit(solution)/shard_map/ppermute | solution.py:61
  149.4 35.0 %collective-permute-start.8 = (f32[2,96,1280]{2,1,0:T(8,128)}, f32[2,96,1280]{2,1,0:T(8,128)}, u32[]{:S(2)}, u32[]{:S(2)}) collective-permute-start(f32[2,96,1280]{2,1,0:T(8,128)} %bitcast_add_fusion.2), channel_id=1, source_target_pairs={{0,48},{8,56},{16,0},{24,8},{32,16},{40,24},{48,32},{56,40},{1,49}... | collective-permute-start | bytes 2949128 | tf_op jit(solution)/shard_map/ppermute | solution.py:62
  156.1 36.8 %all-to-all-start = ((bf16[1,4,96,16,96]{4,2,1,0,3:T(8,128)(2,1)}), bf16[1,4,96,16,96]{4,2,1,0,3:T(8,128)(2,1)S(1)}, u32[]{:S(2)}, u32[]{:S(2)}) async-start(bf16[1,4,96,16,96]{4,2,1,0,3:T(8,128)(2,1)} %copy.55), calls=%async_computation | async-start | bytes 3145728 | tf_op jit(solution)/shard_map/all_to_all | solution.py:155
  187.1 22.8 %collective-permute-start.9 = (f32[96,2560]{1,0:T(8,128)}, f32[96,2560]{1,0:T(8,128)}, u32[]{:S(2)}, u32[]{:S(2)}) collective-permute-start(f32[96,2560]{1,0:T(8,128)} %fusion.17), channel_id=1, source_target_pairs={{0,64},{64,0},{1,65},{65,1},{2,66},{66,2},{3,67},{67,3},{4,68},{68... | collective-permute-start | bytes 2949128 | tf_op jit(solution)/shard_map/ppermute | solution.py:69
  194.7 2.5 %copy-start.10 = (bf16[16,4,64,96]{3,2,1,0:T(8,128)(2,1)S(1)}, bf16[16,4,64,96]{3,2,1,0:T(8,128)(2,1)}, u32[]{:S(2)}) copy-start(bf16[16,4,64,96]{3,2,1,0:T(8,128)(2,1)} %get-tuple-element.12) | copy-start | bytes 2359300
  194.7 2.5 %copy-start.2 = (bf16[3072,256]{1,0:T(8,128)(2,1)S(1)}, bf16[3072,256]{1,0:T(8,128)(2,1)}, u32[]{:S(2)}) copy-start(bf16[3072,256]{1,0:T(8,128)(2,1)} %all-gather.3.cloned.1.call-done) | copy-start | bytes 4718596
  197.2 1.2 copy-start.9
  213.3 19.6 %all-to-all-start.2 = ((f32[128,1,1]{2,1,0:T(1,128)}), f32[128,1,1]{2,1,0:T(1,128)S(1)}, u32[]{:S(2)}, u32[]{:S(2)}) async-start(f32[128,1,1]{2,1,0:T(1,128)} %broadcast_in_dim.15), calls=%async_computation.2 | async-start | bytes 131072 | tf_op jit(solution)/shard_map/all_to_all | solution.py:177
Sparse Core Ops, SparseCore 0:
  75.3 41.4 reduce-scatter.3
  126.6 45.3 all-gather.2

commit v7 on v6

--- a/solution.py
+++ b/solution.py
@@ -37,17 +37,26 @@
     )
 
 
-def ring_scatter(partial):
-    rows_all, cols = partial.shape
+def core_halves(rows):
+    count, width = rows.shape
     sec_n = lax.axis_size("sec")
     x_n = lax.axis_size("seq") // 2
-    share = rows_all // (sec_n * x_n * 2)
+    core_i = lax.axis_index("seq") % 2
+    grouped = rows.reshape(count, sec_n, x_n, 2, width // (sec_n * x_n * 2))
+    keep = lax.dynamic_index_in_dim(grouped, core_i, 3, keepdims=False).reshape(count, width // 2)
+    give = lax.dynamic_index_in_dim(grouped, 1 - core_i, 3, keepdims=False).reshape(count, width // 2)
+    return keep, give
+
+
+def ring_scatter(keep, give):
+    rows_half, cols = keep.shape
+    sec_n = lax.axis_size("sec")
+    x_n = lax.axis_size("seq") // 2
+    share = rows_half // (sec_n * x_n)
     sec_i = lax.axis_index("sec")
     x_i = lax.axis_index("seq") // 2
-    core_i = lax.axis_index("seq") % 2
-    blocks = partial.reshape(sec_n, x_n, 2, share, cols)
-    keep = lax.dynamic_index_in_dim(blocks, core_i, 2, keepdims=False)
-    give = lax.dynamic_index_in_dim(blocks, 1 - core_i, 2, keepdims=False)
+    keep = keep.reshape(sec_n, x_n, share, cols)
+    give = give.reshape(sec_n, x_n, share, cols)
     core_pairs = [(2 * i + j, 2 * i + 1 - j) for i in range(x_n) for j in range(2)]
     summed = keep + lax.ppermute(give, "seq", core_pairs)
     half = cols // 2
@@ -143,9 +152,11 @@
         * live_rows
     )
     flat_deltas = delta_f.astype(jnp.bfloat16)
-    head_partial = contracted_rows(flat_mixed, flat_deltas)
-    deltas_for_back, head_partial = lax.optimization_barrier((flat_deltas, head_partial))
-    grad_share = ring_scatter(head_partial)
+    mixed_keep, mixed_give = core_halves(flat_mixed)
+    head_give = contracted_rows(mixed_give, flat_deltas)
+    deltas_for_back, head_give = lax.optimization_barrier((flat_deltas, head_give))
+    head_keep = contracted_rows(mixed_keep, flat_deltas)
+    grad_share = ring_scatter(head_keep, head_give)
     back_t = jnp.dot(weights_here, deltas_for_back.T, preferred_element_type=jnp.float32)
     backward_portion = lax.psum_scatter(back_t, "trk", scatter_dimension=0, tiled=True).astype(
         jnp.bfloat16

time: 245 us -> 248 us (1.012)
  other arithmetic: 30.3 us -> 22.2 us
  matrix products: 23.1 us -> 30 us
  starting transfers between devices: 37.9 us -> 40.4 us
    dynamic_slice x0 -> x3, local copies, waits for them, and re-layouts: none -> 8.32 us  [the longest x2 6.01 us: core_halves(): lax.dynamic_index_in_dim(grouped, core_i, 3, keepdims=False)]
    add x1 -> x0, other arithmetic: 7.26 us -> none  [ring_scatter(): summed = keep + lax.ppermute(give, 'seq', core_pairs)]
    dot_general x1 -> x2, matrix products: 2.24 us -> 8.74 us  [contracted_rows(): lax.dot_general(left, right, (((0,), (0,)), ((), ())), preferred_element_...]
    unnamed x29 -> x35, local copies, waits for them, and re-layouts: 19.5 us -> 15.1 us
    squeeze x1 -> x0, local copies, waits for them, and re-layouts: 4.02 us -> none  [ring_scatter(): give = lax.dynamic_index_in_dim(blocks, 1 - core_i, 2, keepdims=False)]
    ppermute x1, starting transfers between devices: 0.01 us -> 3.87 us  [ring_scatter(): summed = keep + lax.ppermute(give, 'seq', core_pairs)]
  transfers between devices with their start and end apart: 15 -> 15, of which waited for: 10 -> 11; matrix products, arithmetic and copies ran while one was open for 25% -> 23% of each run, Pallas kernels for 0% -> 0%
where the time goes in v7:
time: 248 us; the launch traced here: 246 us
  waiting for transfers between devices  90.8 us (37%)
  local copies, waits for them, and re-layouts  47.8 us (19%)
  starting transfers between devices  40.4 us (16%)
  matrix products  30 us (12%)
  other arithmetic  22.2 us (9%)
  between operations  15.1 us (6%)
    ppermute x3, waiting for transfers between devices, ring_scatter(): got_a = lax.ppermute(send_a, 'seq', to_next)  58.3 us
    unnamed x35, local copies, waits for them, and re-layouts  15.1 us
    ppermute x1, waiting for transfers between devices, ring_scatter(): lax.ppermute(other, 'sec', [(i, (i - shift) % sec_n) for i in range(sec_n)])  11.1 us
    all_to_all x1, starting transfers between devices, body(): lax.all_to_all(jnp.broadcast_to(jnp.sum(grad_share * grad_share), (device...  10.1 us
    dot_general x2, matrix products, contracted_rows(): lax.dot_general(left, right, (((0,), (0,)), ((), ())), preferred_element_...  8.74 us
    all_to_all x1, waiting for transfers between devices, body(): lax.all_to_all(jnp.broadcast_to(jnp.sum(grad_share * grad_share), (device...  8.71 us
    dot_general x1, matrix products, body(): jnp.dot(flat_mixed, weights_here, preferred_element_type=jnp.float32)  7.36 us
    all_to_all x1, starting transfers between devices, body(): lax.all_to_all(jnp.broadcast_to(mixed_share[:, :, None, :], (sample_count...  6.32 us
  transfers between devices with their start and end apart: 15, of which 11 were waited for; matrix products, arithmetic and copies ran while one was open for 23% of the time, Pallas kernels for 0%

profile of v7, /device:TPU:0, one launch (start us, length us, event | category | flops | bytes accessed | tf_op | source)
XLA Modules:
  0.0 246.4 jit_solution(2610414754588330481)
XLA Ops:
  7.2 1.4 multiply_reduce_fusion
  8.6 0.7 convert_element_type.39
  9.3 1.8 fusion.12
  11.2 1.3 collective-permute-start
  12.5 1.3 collective-permute-start.1
  14.1 1.4 fusion.26
  15.8 1.9 collective-permute-done.1
  17.7 1.5 fusion.22
  19.3 1.5 fusion.16
  20.8 1.1 broadcast_in_dim_broadcast_in_dim.2
  21.9 6.3 %all-to-all-start.1 = ((bf16[1,4,64,8,192]{4,2,1,0,3:T(8,128)(2,1)}), bf16[1,4,64,8,192]{4,2,1,0,3:T(8,128)(2,1)}, u32[]{:S(2)}, u32[]{:S(2)}) async-start(bf16[1,4,64,8,192]{4,2,1,0,3:T(8,128)(2,1)} %broadcast_in_dim_broadcast_in_dim.2), calls=%async_computation.1 | async-start | bytes 2097152 | tf_op jit(solution)/shard_map/all_to_all | solution.py:119
  28.5 2.1 copy.79
  30.6 10.7 %copy.78 = bf16[1536,1,20,128]{0,3,2,1:T(8,128)(2,1)} copy(bf16[1536,1,20,128]{3,0,2,1:T(8,128)(2,1)} %param.10) | data formatting | bytes 15728640 | tf_op args[3]
  41.3 0.6 bitcast_multiply_fusion
  41.9 2.4 reshape.174
  44.3 2.8 %copy.77 = bf16[4,64,8,192]{3,2,1,0:T(8,128)(2,1)} copy(bf16[4,64,8,192]{3,1,0,2:T(8,128)(2,1)} %bitcast.13) | data formatting | bytes 1572864 | tf_op jit(solution)/shard_map/transpose | solution.py:126
  47.1 2.7 %reshape_reshape.3 = bf16[256,1536]{1,0:T(8,128)(2,1)} reshape(bf16[4,64,8,192]{3,2,1,0:T(8,128)(2,1)} %copy.77) | data formatting | bytes 1572864 | tf_op jit(solution)/shard_map/reshape;reshape | solution.py:139
  49.8 5.4 %constant_dynamic-slice_fusion = (bf16[256,2,4,1,96]{4,3,0,2,1:T(2,128)(2,1)}, bf16[256,2,4,1,96]{4,3,0,2,1:T(2,128)(2,1)}) fusion(bf16[256,2,4,2,96]{4,3,0,2,1:T(2,128)(2,1)} %reshape.174, s32[]{:T(128)S(6)} %select_n.115, s32[]{:T(128)S(6)} %select_n.114), kind=kLoop, calls=%fused_computation.67 | loop fusion | bytes 1572872 | tf_op jit(solution)/shard_map/jit(dynamic_index_in_dim)/dynamic_slice | solution.py:46
  55.2 2.3 copy.81
  57.5 7.4 %fusion.4 = bf16[256,2560]{1,0:T(8,128)(2,1)S(1)} fusion(f32[32,8,20,128]{3,2,1,0:T(8,128)S(1)} %bitcast.135, f32[4,2560]{1,0:T(4,128)} %bitcast_multiply_fusion, bf16[256,1536]{1,0:T(8,128)(2,1)} %reshape_reshape.3, bf16[1536,2560]{0,1:T(8,128)(2,1)} %bitcast.129), kind=kOutput, calls=%fused_computation.7 | convolution fusion | flops 2022440960 | bytes 12623872 | tf_op jit(solution)/shard_map/dot_general | solution.py:140
  64.9 4.3 %fusion.41 = f32[768,2560]{1,0:T(8,128)} fusion(bf16[256,768]{0,1:T(8,128)(2,1)S(1)} %bitcast.139, bf16[256,2560]{1,0:T(8,128)(2,1)S(1)} %fusion.4), kind=kOutput, calls=%fused_computation.82 | convolution fusion | flops 1006632960 | bytes 9568256 | tf_op jit(solution)/shard_map/dot_general | solution.py:35
  69.2 3.9 %collective-permute-start.2 = (f32[2,4,96,2560]{3,2,1,0:T(8,128)}, f32[2,4,96,2560]{3,2,1,0:T(8,128)}, u32[]{:S(2)}, u32[]{:S(2)}) collective-permute-start(f32[2,4,96,2560]{3,2,1,0:T(8,128)} %bitcast.41), channel_id=1, source_target_pairs={{0,8},{8,0},{16,24},{24,16},{32,40},{40,32},{48,56},{56,48},{1,9},... | collective-permute-start | bytes 23592968 | tf_op jit(solution)/shard_map/ppermute | solution.py:61
  73.1 0.6 copy.86
  73.7 5.8 %convolution_bitcast_fusion = f32[1536,256]{0,1:T(8,128)S(1)} fusion(bf16[256,2560]{1,0:T(8,128)(2,1)} %copy-done.2, bf16[1536,2560]{0,1:T(8,128)(2,1)} %bitcast.130), kind=kOutput, calls=%fused_computation.2 | convolution fusion | flops 2013265920 | bytes 10747904 | tf_op jit(solution)/shard_map/dot_general | solution.py:160
  79.6 1.7 copy.93
  81.6 3.9 %collective-permute-done.2 = f32[2,4,96,2560]{3,2,1,0:T(8,128)} collective-permute-done((f32[2,4,96,2560]{3,2,1,0:T(8,128)}, f32[2,4,96,2560]{3,2,1,0:T(8,128)}, u32[]{:S(2)}, u32[]{:S(2)}) %collective-permute-start.2) | collective-permute-done | bytes 7864352 | tf_op jit(solution)/shard_map/ppermute | solution.py:61
  85.5 4.4 %convolution_add_fusion = f32[2,4,96,2560]{3,2,1,0:T(8,128)S(1)} fusion(f32[2,4,96,2560]{3,2,1,0:T(8,128)} %collective-permute-done.2, bf16[256,2560]{1,0:T(8,128)(2,1)S(1)} %copy-done.3, bf16[256,2,4,1,96]{0,4,2,1,3:T(8,128)(2,1)S(1)} %copy.86), kind=kOutput, calls=%fused_computation.1 | convolution fusion | flops 1008599040 | bytes 17432576 | tf_op jit(solution)/shard_map/dot_general | solution.py:35
  89.9 2.8 %fusion.38 = (f32[2,4,96,1280]{3,2,1,0:T(8,128)}, f32[2,4,96,1280]{3,2,1,0:T(8,128)S(1)}) fusion(f32[2,4,96,2560]{3,2,1,0:T(8,128)S(1)} %convolution_add_fusion), kind=kLoop, calls=%fused_computation.79 | loop fusion | bytes 15728640 | tf_op jit(solution)/shard_map/slice | solution.py:64
  92.7 1.9 copy-done
  94.6 2.7 %collective-permute-start.3 = (f32[2,96,1280]{2,1,0:T(8,128)S(1)}, f32[2,96,1280]{2,1,0:T(8,128)S(1)}, u32[]{:S(2)}, u32[]{:S(2)}) collective-permute-start(f32[2,96,1280]{2,1,0:T(8,128)S(1)} %dynamic-slice_bitcast_fusion.1), channel_id=1, source_target_pairs={{0,16},{8,24},{16,32},{24,40},{32,48},{40,56},{48,0},{56,8},{1,17}... | collective-permute-start | bytes 2949128 | tf_op jit(solution)/shard_map/ppermute | solution.py:70
  97.3 2.2 dynamic-slice_bitcast_fusion
  99.5 0.6 collective-permute-start.6
  100.1 19.8 %collective-permute-done.3 = f32[2,96,1280]{2,1,0:T(8,128)S(1)} collective-permute-done((f32[2,96,1280]{2,1,0:T(8,128)S(1)}, f32[2,96,1280]{2,1,0:T(8,128)S(1)}, u32[]{:S(2)}, u32[]{:S(2)}) %collective-permute-start.3) | collective-permute-done | bytes 983072 | tf_op jit(solution)/shard_map/ppermute | solution.py:70
  119.9 1.3 bitcast_add_fusion.5
  121.2 1.3 collective-permute-start.4
  122.6 0.9 collective-permute-done.6
  123.4 1.6 bitcast_add_fusion.2
  125.1 2.1 collective-permute-start.7
  127.1 1.6 convert_element_type.47
  128.7 17.9 %collective-permute-done.4 = f32[2,96,1280]{2,1,0:T(8,128)S(1)} collective-permute-done((f32[2,96,1280]{2,1,0:T(8,128)S(1)}, f32[2,96,1280]{2,1,0:T(8,128)S(1)}, u32[]{:S(2)}, u32[]{:S(2)}) %collective-permute-start.4) | collective-permute-done | bytes 983072 | tf_op jit(solution)/shard_map/ppermute | solution.py:70
  146.6 2.2 bitcast_add_fusion.4
  149.5 2.6 %bitcast_add_fusion.1 = f32[2,96,1280]{2,1,0:T(8,128)} fusion(f32[2,96,1280]{2,1,0:T(8,128)} %collective-permute-done.7, f32[2,4,96,1280]{3,2,1,0:T(8,128)} %get-tuple-element.8, s32[]{:T(128)S(6)} %select_n.130), kind=kLoop, calls=%fused_computation.37 | loop fusion | flops 245760 | bytes 2949124 | tf_op jit(solution)/shard_map/add | solution.py:73
  152.1 3.4 %collective-permute-start.8 = (f32[2,96,1280]{2,1,0:T(8,128)}, f32[2,96,1280]{2,1,0:T(8,128)}, u32[]{:S(2)}, u32[]{:S(2)}) collective-permute-start(f32[2,96,1280]{2,1,0:T(8,128)} %bitcast_add_fusion.1), channel_id=1, source_target_pairs={{0,48},{8,56},{16,0},{24,8},{32,16},{40,24},{48,32},{56,40},{1,49}... | collective-permute-start | bytes 2949128 | tf_op jit(solution)/shard_map/ppermute | solution.py:71
  155.6 1.4 broadcast_in_dim_reshape.3
  156.9 1.6 copy.76
  158.5 4.3 %all-to-all-start = ((bf16[1,4,96,16,96]{4,2,1,0,3:T(8,128)(2,1)}), bf16[1,4,96,16,96]{4,2,1,0,3:T(8,128)(2,1)S(1)}, u32[]{:S(2)}, u32[]{:S(2)}) async-start(bf16[1,4,96,16,96]{4,2,1,0,3:T(8,128)(2,1)} %copy.76), calls=%async_computation | async-start | bytes 3145728 | tf_op jit(solution)/shard_map/all_to_all | solution.py:166
  162.8 20.7 %collective-permute-done.5 = f32[2,96,1280]{2,1,0:T(8,128)} collective-permute-done((f32[2,96,1280]{2,1,0:T(8,128)}, f32[2,96,1280]{2,1,0:T(8,128)}, u32[]{:S(2)}, u32[]{:S(2)}) %collective-permute-start.5) | collective-permute-done | bytes 983072 | tf_op jit(solution)/shard_map/ppermute | solution.py:70
  183.5 1.6 bitcast_add_fusion.3
  185.1 1.5 collective-permute-done.8
  186.5 1.6 bitcast_add_fusion
  188.1 1.0 fusion.18
  189.2 2.6 %collective-permute-start.9 = (f32[96,2560]{1,0:T(8,128)}, f32[96,2560]{1,0:T(8,128)}, u32[]{:S(2)}, u32[]{:S(2)}) collective-permute-start(f32[96,2560]{1,0:T(8,128)} %fusion.18), channel_id=1, source_target_pairs={{0,64},{64,0},{1,65},{65,1},{2,66},{66,2},{3,67},{67,3},{4,68},{68... | collective-permute-start | bytes 2949128 | tf_op jit(solution)/shard_map/ppermute | solution.py:78
  191.8 4.1 %all-to-all-done = bf16[1,4,96,16,96]{4,2,1,0,3:T(8,128)(2,1)S(1)} async-done(((bf16[1,4,96,16,96]{4,2,1,0,3:T(8,128)(2,1)}), bf16[1,4,96,16,96]{4,2,1,0,3:T(8,128)(2,1)S(1)}, u32[]{:S(2)}, u32[]{:S(2)}) %all-to-all-start) | async-done | bytes 1179680 | tf_op jit(solution)/shard_map/all_to_all | solution.py:166
  195.9 1.8 fusion.39
  197.7 2.5 convolution_bitcast_fusion.1
  200.8 0.6 copy-done.8
  201.9 11.1 %collective-permute-done.9 = f32[96,2560]{1,0:T(8,128)} collective-permute-done((f32[96,2560]{1,0:T(8,128)}, f32[96,2560]{1,0:T(8,128)}, u32[]{:S(2)}, u32[]{:S(2)}) %collective-permute-start.9) | collective-permute-done | bytes 983072 | tf_op jit(solution)/shard_map/ppermute | solution.py:78
  213.0 2.1 multiply_reduce_fusion.1
  215.1 1.3 broadcast_in_dim.15
  216.4 10.1 %all-to-all-start.2 = ((f32[128,1,1]{2,1,0:T(1,128)}), f32[128,1,1]{2,1,0:T(1,128)S(1)}, u32[]{:S(2)}, u32[]{:S(2)}) async-start(f32[128,1,1]{2,1,0:T(1,128)} %broadcast_in_dim.15), calls=%async_computation.2 | async-start | bytes 131072 | tf_op jit(solution)/shard_map/all_to_all | solution.py:188
  226.5 0.7 pad_maximum_fusion.5
  227.2 8.7 %all-to-all-done.2 = f32[128,1,1]{2,1,0:T(1,128)S(1)} async-done(((f32[128,1,1]{2,1,0:T(1,128)}), f32[128,1,1]{2,1,0:T(1,128)S(1)}, u32[]{:S(2)}, u32[]{:S(2)}) %all-to-all-start.2) | async-done | bytes 544 | tf_op jit(solution)/shard_map/all_to_all | solution.py:188
  235.9 0.7 reduce_sum.29
  237.4 2.1 reshape.164
  (55 shorter events, 3.1 us)
Async XLA Ops:
  7.2 6.7 %copy-start.4 = (bf16[4,64,1536]{2,1,0:T(8,128)(2,1)S(1)}, bf16[4,64,1536]{2,1,0:T(8,128)(2,1)}, u32[]{:S(2)}) copy-start(bf16[4,64,1536]{2,1,0:T(8,128)(2,1)} %param.7) | copy-start | bytes 2359300
  7.2 6.7 %copy-start.14 = (s32[1,20]{1,0:T(1,128)S(1)}, s32[1,20]{1,0:T(1,128)}, u32[]{:S(2)}) copy-start(s32[1,20]{1,0:T(1,128)} %param.12) | copy-start | bytes 244
  11.2 8.1 %copy-start.5 = (bf16[4,64,1536]{2,1,0:T(8,128)(2,1)}, bf16[4,64,1536]{2,1,0:T(8,128)(2,1)S(1)}, u32[]{:S(2)}) copy-start(bf16[4,64,1536]{2,1,0:T(8,128)(2,1)S(1)} %fusion.12) | copy-start | bytes 2359300
  11.2 2.9 %copy-start.15 = (s32[4]{0:T(128)S(1)}, s32[4]{0:T(128)}, u32[]{:S(2)}) copy-start(s32[4]{0:T(128)} %param.13) | copy-start | bytes 52
  11.2 8.0 %collective-permute-start = (bf16[4,16,1536]{2,1,0:T(8,128)(2,1)S(1)}, bf16[4,16,1536]{2,1,0:T(8,128)(2,1)S(1)}, u32[]{:S(2)}, u32[]{:S(2)}) collective-permute-start(bf16[4,16,1536]{2,1,0:T(8,128)(2,1)S(1)} %get-tuple-element.15), channel_id=1, source_target_pairs={{0,8},{8,16},{16,24},{24,32},{32,40},{40,48},{48,56},{1,9},{9,17},... | collective-permute-start | bytes 589832 | tf_op jit(solution)/shard_map/ppermute | solution.py:25
  12.5 5.2 %collective-permute-start.1 = (bf16[4,16,1536]{2,1,0:T(8,128)(2,1)S(1)}, bf16[4,16,1536]{2,1,0:T(8,128)(2,1)S(1)}, u32[]{:S(2)}, u32[]{:S(2)}) collective-permute-start(bf16[4,16,1536]{2,1,0:T(8,128)(2,1)S(1)} %get-tuple-element.16), channel_id=1, source_target_pairs={{8,0},{16,8},{24,16},{32,24},{40,32},{48,40},{56,48},{9,1},{17,9},... | collective-permute-start | bytes 589832 | tf_op jit(solution)/shard_map/ppermute | solution.py:27
  17.7 3.1 %copy-start.12 = (bf16[4,16,1536]{2,1,0:T(8,128)(2,1)}, bf16[4,16,1536]{2,1,0:T(8,128)(2,1)S(1)}, u32[]{:S(2)}) copy-start(bf16[4,16,1536]{2,1,0:T(8,128)(2,1)S(1)} %collective-permute-done.1) | copy-start | bytes 589828
  19.3 2.6 %copy-start.10 = (bf16[4,16,1536]{2,1,0:T(8,128)(2,1)}, bf16[4,16,1536]{2,1,0:T(8,128)(2,1)S(1)}, u32[]{:S(2)}) copy-start(bf16[4,16,1536]{2,1,0:T(8,128)(2,1)S(1)} %collective-permute-done) | copy-start | bytes 589828
  21.9 20.0 %all-to-all-start.1 = ((bf16[1,4,64,8,192]{4,2,1,0,3:T(8,128)(2,1)}), bf16[1,4,64,8,192]{4,2,1,0,3:T(8,128)(2,1)}, u32[]{:S(2)}, u32[]{:S(2)}) async-start(bf16[1,4,64,8,192]{4,2,1,0,3:T(8,128)(2,1)} %broadcast_in_dim_broadcast_in_dim.2), calls=%async_computation.1 | async-start | bytes 2097152 | tf_op jit(solution)/shard_map/all_to_all | solution.py:119
  28.2 98.9 %reduce-scatter.4.cloned.1.call-start = ((), (), s32[]{:S(2)}) async-start(), calls=%async_computation.5 | async-start | bytes 1769472 | tf_op jit(solution)/shard_map/reduce_scatter | solution.py:161
  64.9 4.3 %copy-start.2 = (bf16[256,2560]{1,0:T(8,128)(2,1)}, bf16[256,2560]{1,0:T(8,128)(2,1)S(1)}, u32[]{:S(2)}) copy-start(bf16[256,2560]{1,0:T(8,128)(2,1)S(1)} %fusion.4) | copy-start | bytes 3932164
  64.9 8.2 %copy-start.7 = (bf16[256,2,4,1,96]{4,3,0,2,1:T(2,128)(2,1)S(1)}, bf16[256,2,4,1,96]{4,3,0,2,1:T(2,128)(2,1)}, u32[]{:S(2)}) copy-start(bf16[256,2,4,1,96]{4,3,0,2,1:T(2,128)(2,1)} %get-tuple-element.13) | copy-start | bytes 1179652
  69.2 16.2 %collective-permute-start.2 = (f32[2,4,96,2560]{3,2,1,0:T(8,128)}, f32[2,4,96,2560]{3,2,1,0:T(8,128)}, u32[]{:S(2)}, u32[]{:S(2)}) collective-permute-start(f32[2,4,96,2560]{3,2,1,0:T(8,128)} %bitcast.41), channel_id=1, source_target_pairs={{0,8},{8,0},{16,24},{24,16},{32,40},{40,32},{48,56},{56,48},{1,9},... | collective-permute-start | bytes 23592968 | tf_op jit(solution)/shard_map/ppermute | solution.py:61
  79.6 5.9 %copy-start.3 = (bf16[256,2560]{1,0:T(8,128)(2,1)S(1)}, bf16[256,2560]{1,0:T(8,128)(2,1)}, u32[]{:S(2)}) copy-start(bf16[256,2560]{1,0:T(8,128)(2,1)} %copy-done.2) | copy-start | bytes 3932164
  81.3 116.3 %all-gather.3.cloned.1.call-start = ((), (), s32[]{:S(2)}) async-start(), calls=%async_computation.4 | async-start | bytes 1671168 | tf_op jit(solution)/shard_map/all_gather | solution.py:173
  92.7 1.9 copy-start
  94.6 25.3 %collective-permute-start.3 = (f32[2,96,1280]{2,1,0:T(8,128)S(1)}, f32[2,96,1280]{2,1,0:T(8,128)S(1)}, u32[]{:S(2)}, u32[]{:S(2)}) collective-permute-start(f32[2,96,1280]{2,1,0:T(8,128)S(1)} %dynamic-slice_bitcast_fusion.1), channel_id=1, source_target_pairs={{0,16},{8,24},{16,32},{24,40},{32,48},{40,56},{48,0},{56,8},{1,17}... | collective-permute-start | bytes 2949128 | tf_op jit(solution)/shard_map/ppermute | solution.py:70
  99.5 23.9 %collective-permute-start.6 = (f32[2,96,1280]{2,1,0:T(8,128)}, f32[2,96,1280]{2,1,0:T(8,128)}, u32[]{:S(2)}, u32[]{:S(2)}) collective-permute-start(f32[2,96,1280]{2,1,0:T(8,128)} %dynamic-slice_bitcast_fusion), channel_id=1, source_target_pairs={{0,48},{8,56},{16,0},{24,8},{32,16},{40,24},{48,32},{56,40},{1,49}... | collective-permute-start | bytes 2949128 | tf_op jit(solution)/shard_map/ppermute | solution.py:71
  121.2 25.4 %collective-permute-start.4 = (f32[2,96,1280]{2,1,0:T(8,128)S(1)}, f32[2,96,1280]{2,1,0:T(8,128)S(1)}, u32[]{:S(2)}, u32[]{:S(2)}) collective-permute-start(f32[2,96,1280]{2,1,0:T(8,128)S(1)} %bitcast_add_fusion.5), channel_id=1, source_target_pairs={{0,16},{8,24},{16,32},{24,40},{32,48},{40,56},{48,0},{56,8},{1,17}... | collective-permute-start | bytes 2949128 | tf_op jit(solution)/shard_map/ppermute | solution.py:70
  125.1 24.4 %collective-permute-start.7 = (f32[2,96,1280]{2,1,0:T(8,128)S(1)}, f32[2,96,1280]{2,1,0:T(8,128)}, u32[]{:S(2)}, u32[]{:S(2)}) collective-permute-start(f32[2,96,1280]{2,1,0:T(8,128)S(1)} %bitcast_add_fusion.2), channel_id=1, source_target_pairs={{0,48},{8,56},{16,0},{24,8},{32,16},{40,24},{48,32},{56,40},{1,49}... | collective-permute-start | bytes 2949128 | tf_op jit(solution)/shard_map/ppermute | solution.py:71
  148.9 6.6 %copy-start.6 = (bf16[4,64,1536]{2,1,0:T(8,128)(2,1)S(1)}, bf16[4,64,1536]{2,1,0:T(8,128)(2,1)}, u32[]{:S(2)}) copy-start(bf16[4,64,1536]{2,1,0:T(8,128)(2,1)} %copy-done.5) | copy-start | bytes 2359300
  148.9 6.6 %copy-start.11 = (bf16[4,16,1536]{2,1,0:T(8,128)(2,1)S(1)}, bf16[4,16,1536]{2,1,0:T(8,128)(2,1)}, u32[]{:S(2)}) copy-start(bf16[4,16,1536]{2,1,0:T(8,128)(2,1)} %copy-done.10) | copy-start | bytes 589828
  148.9 6.6 %copy-start.13 = (bf16[4,16,1536]{2,1,0:T(8,128)(2,1)S(1)}, bf16[4,16,1536]{2,1,0:T(8,128)(2,1)}, u32[]{:S(2)}) copy-start(bf16[4,16,1536]{2,1,0:T(8,128)(2,1)} %copy-done.12) | copy-start | bytes 589828
  148.9 34.6 %collective-permute-start.5 = (f32[2,96,1280]{2,1,0:T(8,128)}, f32[2,96,1280]{2,1,0:T(8,128)}, u32[]{:S(2)}, u32[]{:S(2)}) collective-permute-start(f32[2,96,1280]{2,1,0:T(8,128)} %bitcast_add_fusion.4), channel_id=1, source_target_pairs={{0,16},{8,24},{16,32},{24,40},{32,48},{40,56},{48,0},{56,8},{1,17}... | collective-permute-start | bytes 2949128 | tf_op jit(solution)/shard_map/ppermute | solution.py:70
  152.1 34.4 %collective-permute-start.8 = (f32[2,96,1280]{2,1,0:T(8,128)}, f32[2,96,1280]{2,1,0:T(8,128)}, u32[]{:S(2)}, u32[]{:S(2)}) collective-permute-start(f32[2,96,1280]{2,1,0:T(8,128)} %bitcast_add_fusion.1), channel_id=1, source_target_pairs={{0,48},{8,56},{16,0},{24,8},{32,16},{40,24},{48,32},{56,40},{1,49}... | collective-permute-start | bytes 2949128 | tf_op jit(solution)/shard_map/ppermute | solution.py:71
  158.5 37.4 %all-to-all-start = ((bf16[1,4,96,16,96]{4,2,1,0,3:T(8,128)(2,1)}), bf16[1,4,96,16,96]{4,2,1,0,3:T(8,128)(2,1)S(1)}, u32[]{:S(2)}, u32[]{:S(2)}) async-start(bf16[1,4,96,16,96]{4,2,1,0,3:T(8,128)(2,1)} %copy.76), calls=%async_computation | async-start | bytes 3145728 | tf_op jit(solution)/shard_map/all_to_all | solution.py:166
  189.2 23.8 %collective-permute-start.9 = (f32[96,2560]{1,0:T(8,128)}, f32[96,2560]{1,0:T(8,128)}, u32[]{:S(2)}, u32[]{:S(2)}) collective-permute-start(f32[96,2560]{1,0:T(8,128)} %fusion.18), channel_id=1, source_target_pairs={{0,64},{64,0},{1,65},{65,1},{2,66},{66,2},{3,67},{67,3},{4,68},{68... | collective-permute-start | bytes 2949128 | tf_op jit(solution)/shard_map/ppermute | solution.py:78
  197.7 2.5 %copy-start.9 = (bf16[16,4,64,96]{3,2,1,0:T(8,128)(2,1)S(1)}, bf16[16,4,64,96]{3,2,1,0:T(8,128)(2,1)}, u32[]{:S(2)}) copy-start(bf16[16,4,64,96]{3,2,1,0:T(8,128)(2,1)} %get-tuple-element.12) | copy-start | bytes 2359300
  197.7 2.5 %copy-start.1 = (bf16[3072,256]{1,0:T(8,128)(2,1)S(1)}, bf16[3072,256]{1,0:T(8,128)(2,1)}, u32[]{:S(2)}) copy-start(bf16[3072,256]{1,0:T(8,128)(2,1)} %all-gather.3.cloned.1.call-done) | copy-start | bytes 4718596
  200.1 1.2 copy-start.8
  216.4 19.5 %all-to-all-start.2 = ((f32[128,1,1]{2,1,0:T(1,128)}), f32[128,1,1]{2,1,0:T(1,128)S(1)}, u32[]{:S(2)}, u32[]{:S(2)}) async-start(f32[128,1,1]{2,1,0:T(1,128)} %broadcast_in_dim.15), calls=%async_computation.2 | async-start | bytes 131072 | tf_op jit(solution)/shard_map/all_to_all | solution.py:188
Sparse Core Ops, SparseCore 0:
  81.5 42.0 reduce-scatter.3
  128.8 46.2 all-gather.2

commit v8 on v6

--- a/solution.py
+++ b/solution.py
@@ -50,26 +50,39 @@
     give = lax.dynamic_index_in_dim(blocks, 1 - core_i, 2, keepdims=False)
     core_pairs = [(2 * i + j, 2 * i + 1 - j) for i in range(x_n) for j in range(2)]
     summed = keep + lax.ppermute(give, "seq", core_pairs)
-    half = cols // 2
-    ahead = summed[..., :half]
-    behind = summed[..., half:]
     to_next = [(2 * i + j, 2 * ((i + 1) % x_n) + j) for i in range(x_n) for j in range(2)]
     to_prev = [(2 * i + j, 2 * ((i - 1) % x_n) + j) for i in range(x_n) for j in range(2)]
-    send_a = lax.dynamic_index_in_dim(ahead, (x_i - 1) % x_n, 1, keepdims=False)
-    send_b = lax.dynamic_index_in_dim(behind, (x_i + 1) % x_n, 1, keepdims=False)
-    for step in range(x_n - 1):
-        got_a = lax.ppermute(send_a, "seq", to_next)
-        got_b = lax.ppermute(send_b, "seq", to_prev)
-        send_a = got_a + lax.dynamic_index_in_dim(ahead, (x_i - step - 2) % x_n, 1, keepdims=False)
-        send_b = got_b + lax.dynamic_index_in_dim(behind, (x_i + step + 2) % x_n, 1, keepdims=False)
-    reduced = jnp.concatenate([send_a, send_b], axis=-1)
-    total = lax.dynamic_index_in_dim(reduced, sec_i, 0, keepdims=False)
-    for shift in range(1, sec_n):
-        other = lax.dynamic_index_in_dim(reduced, (sec_i - shift) % sec_n, 0, keepdims=False)
-        total = total + lax.ppermute(
-            other, "sec", [(i, (i - shift) % sec_n) for i in range(sec_n)]
-        )
-    return total
+
+    def x_ring(data, axis):
+        quarter = data.shape[-1] // 2
+        ahead = data[..., :quarter]
+        behind = data[..., quarter:]
+        send_a = lax.dynamic_index_in_dim(ahead, (x_i - 1) % x_n, axis, keepdims=False)
+        send_b = lax.dynamic_index_in_dim(behind, (x_i + 1) % x_n, axis, keepdims=False)
+        for step in range(x_n - 1):
+            got_a = lax.ppermute(send_a, "seq", to_next)
+            got_b = lax.ppermute(send_b, "seq", to_prev)
+            send_a = got_a + lax.dynamic_index_in_dim(
+                ahead, (x_i - step - 2) % x_n, axis, keepdims=False
+            )
+            send_b = got_b + lax.dynamic_index_in_dim(
+                behind, (x_i + step + 2) % x_n, axis, keepdims=False
+            )
+        return jnp.concatenate([send_a, send_b], axis=-1)
+
+    def sec_pair(data):
+        total = lax.dynamic_index_in_dim(data, sec_i, 0, keepdims=False)
+        for shift in range(1, sec_n):
+            other = lax.dynamic_index_in_dim(data, (sec_i - shift) % sec_n, 0, keepdims=False)
+            total = total + lax.ppermute(
+                other, "sec", [(i, (i - shift) % sec_n) for i in range(sec_n)]
+            )
+        return total
+
+    half = cols // 2
+    first = sec_pair(x_ring(summed[..., :half], 1))
+    second = x_ring(sec_pair(summed[..., half:]), 0)
+    return jnp.concatenate([first, second], axis=-1)
 
 
 def butterfly_sum(value):

time: 245 us -> 263 us (1.073)
  waiting for transfers between devices: 91.6 us -> 106 us
  starting transfers between devices: 37.9 us -> 46.7 us
  other arithmetic: 30.3 us -> 23.6 us
    reduce_scatter x1, waiting for transfers between devices: 0.01 us -> 41.4 us  [body(): lax.psum_scatter(back_t, 'trk', scatter_dimension=0, tiled=True)]
    ppermute x7 -> x14, waiting for transfers between devices: 71.7 us -> 42.6 us  [the longest x6 28.4 us: x_ring(): got_b = lax.ppermute(send_b, 'seq', to_prev)]
    ppermute x7 -> x14, starting transfers between devices: 12.6 us -> 23 us  [the longest x6 14.7 us: x_ring(): got_b = lax.ppermute(send_b, 'seq', to_prev)]
    all_to_all x1, waiting for transfers between devices: 3.59 us -> 10.9 us  [body(): lax.all_to_all(padded_input.reshape(sample_count, local_rows + 2 * DILATI...]
    ppermute x1, waiting for transfers between devices: 5.63 us -> 0.01 us  [ring_scatter(): summed = keep + lax.ppermute(give, 'seq', core_pairs)]
    add x6 -> x14, other arithmetic: 11.1 us -> 6.65 us  [the longest x6 2.63 us: x_ring(): got_a + lax.dynamic_index_in_dim(ahead, (x_i - step - 2) % x_n, axis, kee...]
    all_to_all x1, starting transfers between devices: 10.2 us -> 6.31 us  [body(): lax.all_to_all(jnp.broadcast_to(jnp.sum(grad_share * grad_share), (device...]
    dot_general x1, matrix products: 5.41 us -> 2.21 us  [body(): jnp.dot(weights_here, deltas_for_back.T, preferred_element_type=jnp.float32)]
  transfers between devices with their start and end apart: 15 -> 22, of which waited for: 10 -> 15; matrix products, arithmetic and copies ran while one was open for 25% -> 20% of each run, Pallas kernels for 0% -> 0%
where the time goes in v8:
time: 263 us; the launch traced here: 262 us
  waiting for transfers between devices  106 us (40%)
  local copies, waits for them, and re-layouts  47.6 us (18%)
  starting transfers between devices  46.7 us (18%)
  other arithmetic  23.6 us (9%)
  matrix products  23 us (9%)
  between operations  15.4 us (6%)
    reduce_scatter x1, waiting for transfers between devices, body(): lax.psum_scatter(back_t, 'trk', scatter_dimension=0, tiled=True)  41.4 us
    ppermute x6, waiting for transfers between devices, x_ring(): got_b = lax.ppermute(send_b, 'seq', to_prev)  28.4 us
    unnamed x43, local copies, waits for them, and re-layouts  20 us
    ppermute x6, starting transfers between devices, x_ring(): got_b = lax.ppermute(send_b, 'seq', to_prev)  14.7 us
    all_to_all x1, waiting for transfers between devices, body(): lax.all_to_all(padded_input.reshape(sample_count, local_rows + 2 * DILATI...  10.9 us
    all_to_all x1, waiting for transfers between devices, body(): lax.all_to_all(jnp.broadcast_to(jnp.sum(grad_share * grad_share), (device...  8.7 us
    dot_general x1, matrix products, body(): jnp.dot(flat_mixed, weights_here, preferred_element_type=jnp.float32)  8.57 us
    ppermute x6, waiting for transfers between devices, x_ring(): got_a = lax.ppermute(send_a, 'seq', to_next)  7.95 us
  transfers between devices with their start and end apart: 22, of which 15 were waited for; matrix products, arithmetic and copies ran while one was open for 20% of the time, Pallas kernels for 0%

profile of v8, /device:TPU:0, one launch (start us, length us, event | category | flops | bytes accessed | tf_op | source)
XLA Modules:
  0.0 261.9 jit_solution(11376937274187317137)
XLA Ops:
  8.0 1.4 multiply_reduce_fusion
  9.3 1.8 fusion.12
  11.2 1.3 collective-permute-start.1
  12.5 3.0 %collective-permute-start = (bf16[4,16,1536]{2,1,0:T(8,128)(2,1)S(1)}, bf16[4,16,1536]{2,1,0:T(8,128)(2,1)S(1)}, u32[]{:S(2)}, u32[]{:S(2)}) collective-permute-start(bf16[4,16,1536]{2,1,0:T(8,128)(2,1)S(1)} %get-tuple-element.13), channel_id=1, source_target_pairs={{0,8},{8,16},{16,24},{24,32},{32,40},{40,48},{48,56},{1,9},{9,17},... | collective-permute-start | bytes 589832 | tf_op jit(solution)/shard_map/ppermute | solution.py:25
  15.8 1.4 fusion.21
  18.2 1.4 fusion.16
  19.7 1.5 fusion.15
  21.1 1.1 broadcast_in_dim_broadcast_in_dim.2
  22.2 6.4 %all-to-all-start.1 = ((bf16[1,4,64,8,192]{4,2,1,0,3:T(8,128)(2,1)}), bf16[1,4,64,8,192]{4,2,1,0,3:T(8,128)(2,1)}, u32[]{:S(2)}, u32[]{:S(2)}) async-start(bf16[1,4,64,8,192]{4,2,1,0,3:T(8,128)(2,1)} %broadcast_in_dim_broadcast_in_dim.2), calls=%async_computation.1 | async-start | bytes 2097152 | tf_op jit(solution)/shard_map/all_to_all | solution.py:123
  28.7 2.1 copy.58
  30.8 10.6 %copy.57 = bf16[1536,1,20,128]{0,3,2,1:T(8,128)(2,1)} copy(bf16[1536,1,20,128]{3,0,2,1:T(8,128)(2,1)} %param.10) | data formatting | bytes 15728640 | tf_op args[3]
  41.5 1.4 bitcast_multiply_fusion
  42.9 1.9 all-to-all-done.1
  44.9 2.8 %copy.56 = bf16[4,64,8,192]{3,2,1,0:T(8,128)(2,1)} copy(bf16[4,64,8,192]{3,1,0,2:T(8,128)(2,1)} %bitcast.13) | data formatting | bytes 1572864 | tf_op jit(solution)/shard_map/transpose | solution.py:130
  47.6 2.7 %reshape_reshape.3 = bf16[256,1536]{1,0:T(8,128)(2,1)} reshape(bf16[4,64,8,192]{3,2,1,0:T(8,128)(2,1)} %copy.56) | data formatting | bytes 1572864 | tf_op jit(solution)/shard_map/reshape;reshape | solution.py:143
  50.4 8.6 %fusion.4 = bf16[256,2560]{1,0:T(8,128)(2,1)} fusion(f32[32,8,20,128]{3,2,1,0:T(8,128)S(1)} %bitcast.145, f32[4,2560]{1,0:T(4,128)} %bitcast_multiply_fusion, bf16[256,1536]{1,0:T(8,128)(2,1)} %reshape_reshape.3, bf16[1536,2560]{0,1:T(8,128)(2,1)} %bitcast.137), kind=kOutput, calls=%fused_computation.8 | convolution fusion | flops 2022440960 | bytes 12623872 | tf_op jit(solution)/shard_map/dot_general | solution.py:144
  58.9 3.9 %fusion.40 = f32[1536,2560]{1,0:T(8,128)S(1)} fusion(bf16[256,1536]{1,0:T(8,128)(2,1)} %reshape_reshape.3, bf16[256,2560]{1,0:T(8,128)(2,1)} %fusion.4), kind=kOutput, calls=%fused_computation.91 | convolution fusion | flops 2013265920 | bytes 17825792 | tf_op jit(solution)/shard_map/dot_general | solution.py:35
  62.9 3.7 %dynamic-slice_bitcast_fusion = f32[2,4,96,2560]{3,2,1,0:T(8,128)} fusion(f32[2,4,2,96,2560]{4,3,2,1,0:T(8,128)S(1)} %bitcast.135, s32[]{:T(128)S(6)} %select_n.145), kind=kLoop, calls=%fused_computation.1 | loop fusion | bytes 15728644 | tf_op jit(solution)/shard_map/jit(dynamic_index_in_dim)/squeeze | solution.py:50
  66.6 4.3 %copy-done = f32[1536,2560]{1,0:T(8,128)} copy-done((f32[1536,2560]{1,0:T(8,128)}, f32[1536,2560]{1,0:T(8,128)S(1)}, u32[]{:S(2)}) %copy-start) | copy-done | bytes 15728664
  70.9 2.2 convolution_bitcast_fusion
  73.2 1.6 copy.67
  75.1 41.4 %reduce-scatter.4.cloned.1.call-done = f32[192,256]{1,0:T(8,128)} async-done(((f32[1536,256]{1,0:T(8,128)}), f32[192,256]{1,0:T(8,128)}) %reduce-scatter.4.cloned.1.call-update) | async-done | bytes 196624 | tf_op jit(solution)/shard_map/reduce_scatter | solution.py:163
  116.4 1.6 convert_element_type.47
  118.1 1.4 broadcast_in_dim_reshape.3
  119.5 1.6 copy.55
  121.1 6.6 %all-to-all-start = ((bf16[1,4,96,16,96]{4,2,1,0,3:T(8,128)(2,1)}), bf16[1,4,96,16,96]{4,2,1,0,3:T(8,128)(2,1)S(1)}, u32[]{:S(2)}, u32[]{:S(2)}) async-start(bf16[1,4,96,16,96]{4,2,1,0,3:T(8,128)(2,1)} %copy.55), calls=%async_computation | async-start | bytes 3145728 | tf_op jit(solution)/shard_map/all_to_all | solution.py:168
  127.7 7.1 %bitcast_add_fusion = f32[2,4,96,2560]{3,2,1,0:T(8,128)S(1)} fusion(f32[2,4,96,2560]{3,2,1,0:T(8,128)} %collective-permute-done.2, f32[2,4,2,96,2560]{4,3,2,1,0:T(8,128)} %bitcast.136, s32[]{:T(128)S(6)} %select_n.144), kind=kLoop, calls=%fused_computation | loop fusion | flops 1966080 | bytes 23592964 | tf_op jit(solution)/shard_map/add | solution.py:52
  134.8 1.8 fusion.36
  136.6 1.9 copy-done.1
  138.5 0.9 dynamic-slice_bitcast_fusion.3
  140.0 1.9 collective-permute-start.3
  141.9 10.9 %all-to-all-done = bf16[1,4,96,16,96]{4,2,1,0,3:T(8,128)(2,1)S(1)} async-done(((bf16[1,4,96,16,96]{4,2,1,0,3:T(8,128)(2,1)}), bf16[1,4,96,16,96]{4,2,1,0,3:T(8,128)(2,1)S(1)}, u32[]{:S(2)}, u32[]{:S(2)}) %all-to-all-start) | async-done | bytes 1179680 | tf_op jit(solution)/shard_map/all_to_all | solution.py:168
  152.8 1.8 fusion.38
  154.6 2.5 slice.72
  157.4 1.0 collective-permute-start.6
  158.4 1.4 dynamic-slice_bitcast_fusion.1
  160.5 1.5 collective-permute-done.3
  162.0 1.2 bitcast_add_fusion.7
  163.3 2.2 collective-permute-start.4
  165.5 7.2 %collective-permute-done.6 = f32[2,96,640]{2,1,0:T(8,128)S(1)} collective-permute-done((f32[2,96,640]{2,1,0:T(8,128)S(1)}, f32[2,96,640]{2,1,0:T(8,128)S(1)}, u32[]{:S(2)}, u32[]{:S(2)}) %collective-permute-start.6) | collective-permute-done | bytes 491552 | tf_op jit(solution)/shard_map/ppermute | solution.py:64
  173.5 2.2 collective-permute-start.7
  175.7 2.8 %convolution_bitcast_fusion.1 = f32[96,1,192]{2,0,1:T(8,128)} fusion(bf16[16,256,96]{2,1,0:T(8,128)(2,1)S(1)} %bitcast.148, bf16[16,192,256]{2,1,0:T(8,128)(2,1)} %bitcast.142), kind=kOutput, calls=%fused_computation.30 | convolution fusion | flops 150994944 | bytes 2433024 | tf_op jit(solution)/shard_map/dot_general | solution.py:177
  178.7 1.2 bitcast_add_fusion.6
  180.6 5.5 %collective-permute-done.7 = f32[2,96,640]{2,1,0:T(8,128)} collective-permute-done((f32[2,96,640]{2,1,0:T(8,128)}, f32[2,96,640]{2,1,0:T(8,128)}, u32[]{:S(2)}, u32[]{:S(2)}) %collective-permute-start.7) | collective-permute-done | bytes 491552 | tf_op jit(solution)/shard_map/ppermute | solution.py:64
  186.1 1.1 bitcast_add_fusion.3
  187.2 3.6 %collective-permute-start.8 = (f32[2,96,640]{2,1,0:T(8,128)S(1)}, f32[2,96,640]{2,1,0:T(8,128)S(1)}, u32[]{:S(2)}, u32[]{:S(2)}) collective-permute-start(f32[2,96,640]{2,1,0:T(8,128)S(1)} %bitcast_add_fusion.3), channel_id=1, source_target_pairs={{0,48},{8,56},{16,0},{24,8},{32,16},{40,24},{48,32},{56,40},{1,49}... | collective-permute-start | bytes 1474568 | tf_op jit(solution)/shard_map/ppermute | solution.py:64
  191.4 2.5 collective-permute-done.5
  194.0 5.9 %collective-permute-done.8 = f32[2,96,640]{2,1,0:T(8,128)S(1)} collective-permute-done((f32[2,96,640]{2,1,0:T(8,128)S(1)}, f32[2,96,640]{2,1,0:T(8,128)S(1)}, u32[]{:S(2)}, u32[]{:S(2)}) %collective-permute-start.8) | collective-permute-done | bytes 491552 | tf_op jit(solution)/shard_map/ppermute | solution.py:64
  200.0 6.2 %collective-permute-done.10 = f32[4,96,1280]{2,1,0:T(8,128)} collective-permute-done((f32[4,96,1280]{2,1,0:T(8,128)}, f32[4,96,1280]{2,1,0:T(8,128)}, u32[]{:S(2)}, u32[]{:S(2)}) %collective-permute-start.10) | collective-permute-done | bytes 1966112 | tf_op jit(solution)/shard_map/ppermute | solution.py:77
  206.2 1.9 bitcast_add_fusion.1
  208.2 1.2 collective-permute-start.14
  209.4 1.0 collective-permute-start.11
  210.4 1.5 collective-permute-start.9
  211.9 3.2 %collective-permute-done.14 = f32[96,640]{1,0:T(8,128)S(1)} collective-permute-done((f32[96,640]{1,0:T(8,128)S(1)}, f32[96,640]{1,0:T(8,128)S(1)}, u32[]{:S(2)}, u32[]{:S(2)}) %collective-permute-start.14) | collective-permute-done | bytes 245792 | tf_op jit(solution)/shard_map/ppermute | solution.py:64
  215.1 3.0 %collective-permute-start.15 = (f32[96,640]{1,0:T(8,128)S(1)}, f32[96,640]{1,0:T(8,128)S(1)}, u32[]{:S(2)}, u32[]{:S(2)}) collective-permute-start(f32[96,640]{1,0:T(8,128)S(1)} %bitcast_add_fusion.10), channel_id=1, source_target_pairs={{0,48},{8,56},{16,0},{24,8},{32,16},{40,24},{48,32},{56,40},{1,49}... | collective-permute-start | bytes 737288 | tf_op jit(solution)/shard_map/ppermute | solution.py:64
  219.0 3.1 %collective-permute-done.15 = f32[96,640]{1,0:T(8,128)S(1)} collective-permute-done((f32[96,640]{1,0:T(8,128)S(1)}, f32[96,640]{1,0:T(8,128)S(1)}, u32[]{:S(2)}, u32[]{:S(2)}) %collective-permute-start.15) | collective-permute-done | bytes 245792 | tf_op jit(solution)/shard_map/ppermute | solution.py:64
  222.1 3.8 %collective-permute-start.16 = (f32[96,640]{1,0:T(8,128)S(1)}, f32[96,640]{1,0:T(8,128)S(1)}, u32[]{:S(2)}, u32[]{:S(2)}) collective-permute-start(f32[96,640]{1,0:T(8,128)S(1)} %bitcast_add_fusion.9), channel_id=1, source_target_pairs={{0,48},{8,56},{16,0},{24,8},{32,16},{40,24},{48,32},{56,40},{1,49}... | collective-permute-start | bytes 737288 | tf_op jit(solution)/shard_map/ppermute | solution.py:64
  226.1 3.5 %collective-permute-done.16 = f32[96,640]{1,0:T(8,128)S(1)} collective-permute-done((f32[96,640]{1,0:T(8,128)S(1)}, f32[96,640]{1,0:T(8,128)S(1)}, u32[]{:S(2)}, u32[]{:S(2)}) %collective-permute-start.16) | collective-permute-done | bytes 245792 | tf_op jit(solution)/shard_map/ppermute | solution.py:64
  229.7 3.8 %collective-permute-done.13 = f32[96,640]{1,0:T(8,128)S(1)} collective-permute-done((f32[96,640]{1,0:T(8,128)S(1)}, f32[96,640]{1,0:T(8,128)S(1)}, u32[]{:S(2)}, u32[]{:S(2)}) %collective-permute-start.13) | collective-permute-done | bytes 245792 | tf_op jit(solution)/shard_map/ppermute | solution.py:63
  233.5 0.9 multiply_reduce_fusion.1
  234.4 1.3 broadcast_in_dim.15
  235.7 6.3 %all-to-all-start.2 = ((f32[128,1,1]{2,1,0:T(1,128)}), f32[128,1,1]{2,1,0:T(1,128)S(1)}, u32[]{:S(2)}, u32[]{:S(2)}) async-start(f32[128,1,1]{2,1,0:T(1,128)} %broadcast_in_dim.15), calls=%async_computation.2 | async-start | bytes 131072 | tf_op jit(solution)/shard_map/all_to_all | solution.py:190
  242.7 8.7 %all-to-all-done.2 = f32[128,1,1]{2,1,0:T(1,128)S(1)} async-done(((f32[128,1,1]{2,1,0:T(1,128)}), f32[128,1,1]{2,1,0:T(1,128)S(1)}, u32[]{:S(2)}, u32[]{:S(2)}) %all-to-all-start.2) | async-done | bytes 544 | tf_op jit(solution)/shard_map/all_to_all | solution.py:190
  252.9 2.1 mul.126
  (88 shorter events, 9.2 us)
Async XLA Ops:
  7.2 8.5 %copy-start.8 = (bf16[4,64,1536]{2,1,0:T(8,128)(2,1)S(1)}, bf16[4,64,1536]{2,1,0:T(8,128)(2,1)}, u32[]{:S(2)}) copy-start(bf16[4,64,1536]{2,1,0:T(8,128)(2,1)} %param.7) | copy-start | bytes 2359300
  7.2 8.4 %copy-start.16 = (s32[1,20]{1,0:T(1,128)S(1)}, s32[1,20]{1,0:T(1,128)}, u32[]{:S(2)}) copy-start(s32[1,20]{1,0:T(1,128)} %param.12) | copy-start | bytes 244
  11.2 8.5 %copy-start.10 = (bf16[4,64,1536]{2,1,0:T(8,128)(2,1)}, bf16[4,64,1536]{2,1,0:T(8,128)(2,1)S(1)}, u32[]{:S(2)}) copy-start(bf16[4,64,1536]{2,1,0:T(8,128)(2,1)S(1)} %fusion.12) | copy-start | bytes 2359300
  11.2 4.6 %copy-start.17 = (s32[4]{0:T(128)S(1)}, s32[4]{0:T(128)}, u32[]{:S(2)}) copy-start(s32[4]{0:T(128)} %param.13) | copy-start | bytes 52
  11.2 7.0 %collective-permute-start.1 = (bf16[4,16,1536]{2,1,0:T(8,128)(2,1)S(1)}, bf16[4,16,1536]{2,1,0:T(8,128)(2,1)S(1)}, u32[]{:S(2)}, u32[]{:S(2)}) collective-permute-start(bf16[4,16,1536]{2,1,0:T(8,128)(2,1)S(1)} %get-tuple-element.14), channel_id=1, source_target_pairs={{8,0},{16,8},{24,16},{32,24},{40,32},{48,40},{56,48},{9,1},{17,9},... | collective-permute-start | bytes 589832 | tf_op jit(solution)/shard_map/ppermute | solution.py:27
  12.5 7.1 %collective-permute-start = (bf16[4,16,1536]{2,1,0:T(8,128)(2,1)S(1)}, bf16[4,16,1536]{2,1,0:T(8,128)(2,1)S(1)}, u32[]{:S(2)}, u32[]{:S(2)}) collective-permute-start(bf16[4,16,1536]{2,1,0:T(8,128)(2,1)S(1)} %get-tuple-element.13), channel_id=1, source_target_pairs={{0,8},{8,16},{16,24},{24,32},{32,40},{40,48},{48,56},{1,9},{9,17},... | collective-permute-start | bytes 589832 | tf_op jit(solution)/shard_map/ppermute | solution.py:25
  22.2 22.6 %all-to-all-start.1 = ((bf16[1,4,64,8,192]{4,2,1,0,3:T(8,128)(2,1)}), bf16[1,4,64,8,192]{4,2,1,0,3:T(8,128)(2,1)}, u32[]{:S(2)}, u32[]{:S(2)}) async-start(bf16[1,4,64,8,192]{4,2,1,0,3:T(8,128)(2,1)} %broadcast_in_dim_broadcast_in_dim.2), calls=%async_computation.1 | async-start | bytes 2097152 | tf_op jit(solution)/shard_map/all_to_all | solution.py:123
  28.7 87.8 %reduce-scatter.4.cloned.1.call-start = ((), (), s32[]{:S(2)}) async-start(), calls=%async_computation.5 | async-start | bytes 1769472 | tf_op jit(solution)/shard_map/reduce_scatter | solution.py:163
  50.4 20.6 %slice-start = ((s8[7864320]{0:T(1024)(128)(4,1)}), s8[4194304]{0:T(1024)(128)(4,1)S(1)}, s32[]{:S(2)}) async-start(s8[7864320]{0:T(1024)(128)(4,1)} %bitcast.138), calls=%async_computation.6 | async-start | bytes 8388608
  58.9 12.0 %slice-start.1 = ((s8[7864320]{0:T(1024)(128)(4,1)}), s8[3670016]{0:T(1024)(128)(4,1)S(1)}, s32[]{:S(2)}) async-start(s8[7864320]{0:T(1024)(128)(4,1)} %bitcast.138), calls=%async_computation.7 | async-start | bytes 7340032
  62.9 8.0 %copy-start = (f32[1536,2560]{1,0:T(8,128)}, f32[1536,2560]{1,0:T(8,128)S(1)}, u32[]{:S(2)}) copy-start(f32[1536,2560]{1,0:T(8,128)S(1)} %fusion.40) | copy-start | bytes 47185924
  62.9 8.0 %copy-start.9 = (bf16[256,2560]{1,0:T(8,128)(2,1)S(1)}, bf16[256,2560]{1,0:T(8,128)(2,1)}, u32[]{:S(2)}) copy-start(bf16[256,2560]{1,0:T(8,128)(2,1)} %fusion.4) | copy-start | bytes 3932164
  70.9 56.7 %collective-permute-start.2 = (f32[2,4,96,2560]{3,2,1,0:T(8,128)}, f32[2,4,96,2560]{3,2,1,0:T(8,128)}, u32[]{:S(2)}, u32[]{:S(2)}) collective-permute-start(f32[2,4,96,2560]{3,2,1,0:T(8,128)} %dynamic-slice_bitcast_fusion), channel_id=1, source_target_pairs={{0,8},{8,0},{16,24},{24,16},{32,40},{40,32},{48,56},{56,48},{1,9},... | collective-permute-start | bytes 23592968 | tf_op jit(solution)/shard_map/ppermute | solution.py:52
  73.2 44.9 %copy-start.11 = (bf16[4,64,1536]{2,1,0:T(8,128)(2,1)S(1)}, bf16[4,64,1536]{2,1,0:T(8,128)(2,1)}, u32[]{:S(2)}) copy-start(bf16[4,64,1536]{2,1,0:T(8,128)(2,1)} %copy-done.10) | copy-start | bytes 2359300
  74.8 100.9 %all-gather.3.cloned.1.call-start = ((), (), s32[]{:S(2)}) async-start(), calls=%async_computation.4 | async-start | bytes 1671168 | tf_op jit(solution)/shard_map/all_gather | solution.py:175
  121.1 31.7 %all-to-all-start = ((bf16[1,4,96,16,96]{4,2,1,0,3:T(8,128)(2,1)}), bf16[1,4,96,16,96]{4,2,1,0,3:T(8,128)(2,1)S(1)}, u32[]{:S(2)}, u32[]{:S(2)}) async-start(bf16[1,4,96,16,96]{4,2,1,0,3:T(8,128)(2,1)} %copy.55), calls=%async_computation | async-start | bytes 3145728 | tf_op jit(solution)/shard_map/all_to_all | solution.py:168
  134.8 3.7 %copy-start.1 = (f32[2,4,96,2560]{3,2,1,0:T(8,128)}, f32[2,4,96,2560]{3,2,1,0:T(8,128)S(1)}, u32[]{:S(2)}) copy-start(f32[2,4,96,2560]{3,2,1,0:T(8,128)S(1)} %bitcast_add_fusion) | copy-start | bytes 23592964
  138.5 1.5 copy-start.6
  140.0 22.0 %collective-permute-start.3 = (f32[2,96,640]{2,1,0:T(8,128)}, f32[2,96,640]{2,1,0:T(8,128)}, u32[]{:S(2)}, u32[]{:S(2)}) collective-permute-start(f32[2,96,640]{2,1,0:T(8,128)} %dynamic-slice_bitcast_fusion.3), channel_id=1, source_target_pairs={{0,16},{8,24},{16,32},{24,40},{32,48},{40,56},{48,0},{56,8},{1,17}... | collective-permute-start | bytes 1474568 | tf_op jit(solution)/shard_map/ppermute | solution.py:63
  154.6 2.7 %copy-start.5 = (f32[2,4,96,640]{3,2,1,0:T(8,128)S(1)}, f32[2,4,96,640]{3,2,1,0:T(8,128)}, u32[]{:S(2)}) copy-start(f32[2,4,96,640]{3,2,1,0:T(8,128)} %get-tuple-element.6) | copy-start | bytes 5898244
  157.2 2.7 %copy-start.2 = (f32[2,4,96,1280]{3,2,1,0:T(8,128)}, f32[2,4,96,1280]{3,2,1,0:T(8,128)S(1)}, u32[]{:S(2)}) copy-start(f32[2,4,96,1280]{3,2,1,0:T(8,128)S(1)} %slice.72) | copy-start | bytes 11796484
  157.4 15.2 %collective-permute-start.6 = (f32[2,96,640]{2,1,0:T(8,128)S(1)}, f32[2,96,640]{2,1,0:T(8,128)S(1)}, u32[]{:S(2)}, u32[]{:S(2)}) collective-permute-start(f32[2,96,640]{2,1,0:T(8,128)S(1)} %dynamic-slice_bitcast_fusion.2), channel_id=1, source_target_pairs={{0,48},{8,56},{16,0},{24,8},{32,16},{40,24},{48,32},{56,40},{1,49}... | collective-permute-start | bytes 1474568 | tf_op jit(solution)/shard_map/ppermute | solution.py:64
  159.8 15.9 %copy-start.14 = (bf16[16,4,64,96]{3,2,1,0:T(8,128)(2,1)S(1)}, bf16[16,4,64,96]{3,2,1,0:T(8,128)(2,1)}, u32[]{:S(2)}) copy-start(bf16[16,4,64,96]{3,2,1,0:T(8,128)(2,1)} %get-tuple-element.11) | copy-start | bytes 2359300
  159.8 46.3 %collective-permute-start.10 = (f32[4,96,1280]{2,1,0:T(8,128)}, f32[4,96,1280]{2,1,0:T(8,128)}, u32[]{:S(2)}, u32[]{:S(2)}) collective-permute-start(f32[4,96,1280]{2,1,0:T(8,128)} %dynamic-slice_bitcast_fusion.1), channel_id=1, source_target_pairs={{0,64},{64,0},{1,65},{65,1},{2,66},{66,2},{3,67},{67,3},{4,68},{68... | collective-permute-start | bytes 5898248 | tf_op jit(solution)/shard_map/ppermute | solution.py:77
  163.3 15.4 %collective-permute-start.4 = (f32[2,96,640]{2,1,0:T(8,128)S(1)}, f32[2,96,640]{2,1,0:T(8,128)}, u32[]{:S(2)}, u32[]{:S(2)}) collective-permute-start(f32[2,96,640]{2,1,0:T(8,128)S(1)} %bitcast_add_fusion.7), channel_id=1, source_target_pairs={{0,16},{8,24},{16,32},{24,40},{32,48},{40,56},{48,0},{56,8},{1,17}... | collective-permute-start | bytes 1474568 | tf_op jit(solution)/shard_map/ppermute | solution.py:63
  173.5 12.6 %collective-permute-start.7 = (f32[2,96,640]{2,1,0:T(8,128)}, f32[2,96,640]{2,1,0:T(8,128)}, u32[]{:S(2)}, u32[]{:S(2)}) collective-permute-start(f32[2,96,640]{2,1,0:T(8,128)} %bitcast_add_fusion.4), channel_id=1, source_target_pairs={{0,48},{8,56},{16,0},{24,8},{32,16},{40,24},{48,32},{56,40},{1,49}... | collective-permute-start | bytes 1474568 | tf_op jit(solution)/shard_map/ppermute | solution.py:64
  175.7 3.0 %copy-start.7 = (f32[2,4,96,640]{3,2,1,0:T(8,128)S(1)}, f32[2,4,96,640]{3,2,1,0:T(8,128)}, u32[]{:S(2)}) copy-start(f32[2,4,96,640]{3,2,1,0:T(8,128)} %copy-done.6) | copy-start | bytes 5898244
  178.5 12.3 %copy-start.4 = (bf16[3072,256]{1,0:T(8,128)(2,1)S(1)}, bf16[3072,256]{1,0:T(8,128)(2,1)}, u32[]{:S(2)}) copy-start(bf16[3072,256]{1,0:T(8,128)(2,1)} %all-gather.3.cloned.1.call-done) | copy-start | bytes 4718596
  178.5 12.3 %copy-start.13 = (bf16[16,4,64,96]{3,2,1,0:T(8,128)(2,1)S(1)}, bf16[16,4,64,96]{3,2,1,0:T(8,128)(2,1)}, u32[]{:S(2)}) copy-start(bf16[16,4,64,96]{3,2,1,0:T(8,128)(2,1)} %get-tuple-element.12) | copy-start | bytes 2359300
  179.9 14.0 %collective-permute-start.5 = (f32[2,96,640]{2,1,0:T(8,128)S(1)}, f32[2,96,640]{2,1,0:T(8,128)S(1)}, u32[]{:S(2)}, u32[]{:S(2)}) collective-permute-start(f32[2,96,640]{2,1,0:T(8,128)S(1)} %bitcast_add_fusion.6), channel_id=1, source_target_pairs={{0,16},{8,24},{16,32},{24,40},{32,48},{40,56},{48,0},{56,8},{1,17}... | collective-permute-start | bytes 1474568 | tf_op jit(solution)/shard_map/ppermute | solution.py:63
  187.2 12.7 %collective-permute-start.8 = (f32[2,96,640]{2,1,0:T(8,128)S(1)}, f32[2,96,640]{2,1,0:T(8,128)S(1)}, u32[]{:S(2)}, u32[]{:S(2)}) collective-permute-start(f32[2,96,640]{2,1,0:T(8,128)S(1)} %bitcast_add_fusion.3), channel_id=1, source_target_pairs={{0,48},{8,56},{16,0},{24,8},{32,16},{40,24},{48,32},{56,40},{1,49}... | collective-permute-start | bytes 1474568 | tf_op jit(solution)/shard_map/ppermute | solution.py:64
  190.8 15.3 %copy-start.3 = (f32[2,4,96,1280]{3,2,1,0:T(8,128)S(1)}, f32[2,4,96,1280]{3,2,1,0:T(8,128)}, u32[]{:S(2)}) copy-start(f32[2,4,96,1280]{3,2,1,0:T(8,128)} %copy-done.2) | copy-start | bytes 11796484
  208.2 10.2 %copy-start.12 = (bf16[16,4,64,96]{3,2,1,0:T(8,128)(2,1)S(1)}, bf16[16,4,64,96]{3,2,1,0:T(8,128)(2,1)}, u32[]{:S(2)}) copy-start(bf16[16,4,64,96]{3,2,1,0:T(8,128)(2,1)} %get-tuple-element.10) | copy-start | bytes 2359300
  208.2 6.9 %collective-permute-start.14 = (f32[96,640]{1,0:T(8,128)S(1)}, f32[96,640]{1,0:T(8,128)S(1)}, u32[]{:S(2)}, u32[]{:S(2)}) collective-permute-start(f32[96,640]{1,0:T(8,128)S(1)} %dynamic-slice_bitcast_fusion.4), channel_id=1, source_target_pairs={{0,48},{8,56},{16,0},{24,8},{32,16},{40,24},{48,32},{56,40},{1,49}... | collective-permute-start | bytes 737288 | tf_op jit(solution)/shard_map/ppermute | solution.py:64
  209.4 8.7 %collective-permute-start.11 = (f32[96,640]{1,0:T(8,128)S(1)}, f32[96,640]{1,0:T(8,128)S(1)}, u32[]{:S(2)}, u32[]{:S(2)}) collective-permute-start(f32[96,640]{1,0:T(8,128)S(1)} %dynamic-slice_bitcast_fusion.5), channel_id=1, source_target_pairs={{0,16},{8,24},{16,32},{24,40},{32,48},{40,56},{48,0},{56,8},{1,17}... | collective-permute-start | bytes 737288 | tf_op jit(solution)/shard_map/ppermute | solution.py:63
  210.4 15.6 %collective-permute-start.9 = (f32[96,1280]{1,0:T(8,128)S(1)}, f32[96,1280]{1,0:T(8,128)S(1)}, u32[]{:S(2)}, u32[]{:S(2)}) collective-permute-start(f32[96,1280]{1,0:T(8,128)S(1)} %fusion.28), channel_id=1, source_target_pairs={{0,64},{64,0},{1,65},{65,1},{2,66},{66,2},{3,67},{67,3},{4,68},{68... | collective-permute-start | bytes 1474568 | tf_op jit(solution)/shard_map/ppermute | solution.py:77
  215.1 7.0 %collective-permute-start.15 = (f32[96,640]{1,0:T(8,128)S(1)}, f32[96,640]{1,0:T(8,128)S(1)}, u32[]{:S(2)}, u32[]{:S(2)}) collective-permute-start(f32[96,640]{1,0:T(8,128)S(1)} %bitcast_add_fusion.10), channel_id=1, source_target_pairs={{0,48},{8,56},{16,0},{24,8},{32,16},{40,24},{48,32},{56,40},{1,49}... | collective-permute-start | bytes 737288 | tf_op jit(solution)/shard_map/ppermute | solution.py:64
  218.1 7.8 %collective-permute-start.12 = (f32[96,640]{1,0:T(8,128)S(1)}, f32[96,640]{1,0:T(8,128)S(1)}, u32[]{:S(2)}, u32[]{:S(2)}) collective-permute-start(f32[96,640]{1,0:T(8,128)S(1)} %bitcast_add_fusion.13), channel_id=1, source_target_pairs={{0,16},{8,24},{16,32},{24,40},{32,48},{40,56},{48,0},{56,8},{1,17}... | collective-permute-start | bytes 737288 | tf_op jit(solution)/shard_map/ppermute | solution.py:63
  222.1 7.5 %collective-permute-start.16 = (f32[96,640]{1,0:T(8,128)S(1)}, f32[96,640]{1,0:T(8,128)S(1)}, u32[]{:S(2)}, u32[]{:S(2)}) collective-permute-start(f32[96,640]{1,0:T(8,128)S(1)} %bitcast_add_fusion.9), channel_id=1, source_target_pairs={{0,48},{8,56},{16,0},{24,8},{32,16},{40,24},{48,32},{56,40},{1,49}... | collective-permute-start | bytes 737288 | tf_op jit(solution)/shard_map/ppermute | solution.py:64
  225.9 16.0 %copy-start.15 = (f32[96,1,192]{2,0,1:T(8,128)S(1)}, f32[96,1,192]{2,0,1:T(8,128)}, u32[]{:S(2)}) copy-start(f32[96,1,192]{2,0,1:T(8,128)} %convolution_bitcast_fusion.1) | copy-start | bytes 221188
  226.0 7.5 %collective-permute-start.13 = (f32[96,640]{1,0:T(8,128)S(1)}, f32[96,640]{1,0:T(8,128)S(1)}, u32[]{:S(2)}, u32[]{:S(2)}) collective-permute-start(f32[96,640]{1,0:T(8,128)S(1)} %bitcast_add_fusion.12), channel_id=1, source_target_pairs={{0,16},{8,24},{16,32},{24,40},{32,48},{40,56},{48,0},{56,8},{1,17}... | collective-permute-start | bytes 737288 | tf_op jit(solution)/shard_map/ppermute | solution.py:63
  235.7 15.8 %all-to-all-start.2 = ((f32[128,1,1]{2,1,0:T(1,128)}), f32[128,1,1]{2,1,0:T(1,128)S(1)}, u32[]{:S(2)}, u32[]{:S(2)}) async-start(f32[128,1,1]{2,1,0:T(1,128)} %broadcast_in_dim.15), calls=%async_computation.2 | async-start | bytes 131072 | tf_op jit(solution)/shard_map/all_to_all | solution.py:190
Sparse Core Ops, SparseCore 0:
  74.9 41.4 reduce-scatter.3
  119.5 52.4 all-gather.2

commit v9 on v6

--- a/solution.py
+++ b/solution.py
@@ -147,9 +147,10 @@
     deltas_for_back, head_partial = lax.optimization_barrier((flat_deltas, head_partial))
     grad_share = ring_scatter(head_partial)
     back_t = jnp.dot(weights_here, deltas_for_back.T, preferred_element_type=jnp.float32)
-    backward_portion = lax.psum_scatter(back_t, "trk", scatter_dimension=0, tiled=True).astype(
-        jnp.bfloat16
-    )
+    back_from_owners = lax.all_to_all(
+        back_t.reshape(trk_n, out_share, sample_count * local_rows), "trk", 0, 0, tiled=True
+    )
+    backward_portion = jnp.sum(back_from_owners, axis=0).astype(jnp.bfloat16)
     group_count = lax.axis_size("sec") * lax.axis_size("seq")
     share_rows = width_all // group_count
     hidden_parts = lax.all_to_all(
@@ -159,7 +160,13 @@
         0,
         tiled=False,
     )
-    back_parts = lax.all_gather(backward_portion, ("sec", "seq"), axis=0, tiled=False)
+    back_parts = lax.all_to_all(
+        jnp.broadcast_to(backward_portion[None], (group_count,) + backward_portion.shape),
+        ("sec", "seq"),
+        0,
+        0,
+        tiled=True,
+    )
     per_tap = [
         lax.dot_general(
             hidden_parts[

time: 245 us -> 242 us (0.988)
  between operations: 15.1 us -> 1.7 us
  starting transfers between devices: 37.9 us -> 49.1 us
  waiting for transfers between devices: 91.6 us -> 85.3 us
  local copies, waits for them, and re-layouts: 45.4 us -> 49.2 us
    ppermute x3, waiting for transfers between devices: 58.4 us -> 36.3 us  [ring_scatter(): got_a = lax.ppermute(send_a, 'seq', to_next)]
    all_to_all x0 -> x2, starting transfers between devices: none -> 10.7 us  [the longest x1 6.72 us: body(): lax.all_to_all(jnp.broadcast_to(backward_portion[None], (group_count,) +...]
    ppermute x1, waiting for transfers between devices: 5.63 us -> 12.7 us  [ring_scatter(): summed = keep + lax.ppermute(give, 'seq', core_pairs)]
    all_to_all x0 -> x2, waiting for transfers between devices: none -> 4.94 us  [the longest x1 4.94 us: body(): lax.all_to_all(jnp.broadcast_to(backward_portion[None], (group_count,) +...]
    ppermute x1, waiting for transfers between devices: 10.9 us -> 14.8 us  [ring_scatter(): lax.ppermute(other, 'sec', [(i, (i - shift) % sec_n) for i in range(sec_n)])]
    unnamed x29 -> x34, local copies, waits for them, and re-layouts: 19.5 us -> 17.2 us
  transfers between devices with their start and end apart: 15 -> 15, of which waited for: 10 -> 10; matrix products, arithmetic and copies ran while one was open for 25% -> 23% of each run, Pallas kernels for 0% -> 0%
where the time goes in v9:
time: 242 us; the launch traced here: 240 us
  waiting for transfers between devices  85.3 us (35%)
  local copies, waits for them, and re-layouts  49.2 us (20%)
  starting transfers between devices  49.1 us (20%)
  other arithmetic  32.3 us (13%)
  matrix products  22.4 us (9%)
    ppermute x3, waiting for transfers between devices, ring_scatter(): got_a = lax.ppermute(send_a, 'seq', to_next)  36.3 us
    unnamed x34, local copies, waits for them, and re-layouts  17.2 us
    ppermute x1, waiting for transfers between devices, ring_scatter(): lax.ppermute(other, 'sec', [(i, (i - shift) % sec_n) for i in range(sec_n)])  14.8 us
    ppermute x1, waiting for transfers between devices, ring_scatter(): summed = keep + lax.ppermute(give, 'seq', core_pairs)  12.7 us
    ppermute x3, starting transfers between devices, ring_scatter(): got_b = lax.ppermute(send_b, 'seq', to_prev)  9.89 us
    all_to_all x1, starting transfers between devices, body(): lax.all_to_all(jnp.broadcast_to(jnp.sum(grad_share * grad_share), (device...  8.76 us
    all_to_all x1, waiting for transfers between devices, body(): lax.all_to_all(jnp.broadcast_to(jnp.sum(grad_share * grad_share), (device...  8.71 us
    dot_general x1, matrix products, body(): jnp.dot(flat_mixed, weights_here, preferred_element_type=jnp.float32)  7.42 us
  transfers between devices with their start and end apart: 15, of which 10 were waited for; matrix products, arithmetic and copies ran while one was open for 23% of the time, Pallas kernels for 0%

profile of v9, /device:TPU:0, one launch (start us, length us, event | category | flops | bytes accessed | tf_op | source)
XLA Modules:
  0.0 240.0 jit_solution(17557242984880943477)
XLA Ops:
  0.7 0.8 convert_element_type.43
  1.4 1.4 multiply_reduce_fusion
  2.8 1.8 fusion.12
  4.7 1.3 collective-permute-start.1
  6.0 3.0 %collective-permute-start = (bf16[4,16,1536]{2,1,0:T(8,128)(2,1)S(1)}, bf16[4,16,1536]{2,1,0:T(8,128)(2,1)S(1)}, u32[]{:S(2)}, u32[]{:S(2)}) collective-permute-start(bf16[4,16,1536]{2,1,0:T(8,128)(2,1)S(1)} %get-tuple-element.13), channel_id=1, source_target_pairs={{0,8},{8,16},{16,24},{24,32},{32,40},{40,48},{48,56},{1,9},{9,17},... | collective-permute-start | bytes 589832 | tf_op jit(solution)/shard_map/ppermute | solution.py:25
  9.3 1.4 fusion.25
  11.0 0.7 broadcast_bitcast_fusion
  11.7 1.4 fusion.21
  13.2 1.5 fusion.15
  14.6 1.1 broadcast_in_dim_broadcast_in_dim.2
  15.7 6.4 %all-to-all-start.1 = ((bf16[1,4,64,8,192]{4,2,1,0,3:T(8,128)(2,1)}), bf16[1,4,64,8,192]{4,2,1,0,3:T(8,128)(2,1)}, u32[]{:S(2)}, u32[]{:S(2)}) async-start(bf16[1,4,64,8,192]{4,2,1,0,3:T(8,128)(2,1)} %broadcast_in_dim_broadcast_in_dim.2), calls=%async_computation.1 | async-start | bytes 2097152 | tf_op jit(solution)/shard_map/all_to_all | solution.py:110
  22.1 2.1 copy.46
  24.2 10.6 %copy.45 = bf16[1536,1,20,128]{0,3,2,1:T(8,128)(2,1)} copy(bf16[1536,1,20,128]{3,0,2,1:T(8,128)(2,1)} %param.10) | data formatting | bytes 15728640 | tf_op args[3]
  34.9 1.4 bitcast_multiply_fusion
  36.3 2.0 all-to-all-done.1
  38.3 2.8 %copy.44 = bf16[4,64,8,192]{3,2,1,0:T(8,128)(2,1)} copy(bf16[4,64,8,192]{3,1,0,2:T(8,128)(2,1)} %bitcast.13) | data formatting | bytes 1572864 | tf_op jit(solution)/shard_map/transpose | solution.py:117
  41.1 2.7 %reshape_reshape.3 = bf16[256,1536]{1,0:T(8,128)(2,1)} reshape(bf16[4,64,8,192]{3,2,1,0:T(8,128)(2,1)} %copy.44) | data formatting | bytes 1572864 | tf_op jit(solution)/shard_map/reshape;reshape | solution.py:130
  43.8 7.4 %fusion.4 = bf16[256,2560]{1,0:T(8,128)(2,1)S(1)} fusion(f32[32,8,20,128]{3,2,1,0:T(8,128)S(1)} %bitcast.120, f32[4,2560]{1,0:T(4,128)} %bitcast_multiply_fusion, bf16[256,1536]{1,0:T(8,128)(2,1)} %reshape_reshape.3, bf16[1536,2560]{0,1:T(8,128)(2,1)} %bitcast.117), kind=kOutput, calls=%fused_computation.8 | convolution fusion | flops 2022440960 | bytes 12623872 | tf_op jit(solution)/shard_map/dot_general | solution.py:131
  51.3 2.2 fusion.39
  53.5 4.5 %dynamic-slice_bitcast_fusion = f32[2,4,96,2560]{3,2,1,0:T(8,128)} fusion(f32[2,4,2,96,2560]{4,3,2,1,0:T(8,128)S(1)} %bitcast.115, s32[]{:T(128)S(6)} %select_n.115), kind=kLoop, calls=%fused_computation.1 | loop fusion | bytes 15728644 | tf_op jit(solution)/shard_map/jit(dynamic_index_in_dim)/squeeze | solution.py:50
  58.0 3.3 %copy-done = f32[1536,2560]{1,0:T(8,128)} copy-done((f32[1536,2560]{1,0:T(8,128)}, f32[1536,2560]{1,0:T(8,128)S(1)}, u32[]{:S(2)}) %copy-start) | copy-done | bytes 15728664
  61.3 12.7 %collective-permute-done.2 = f32[2,4,96,2560]{3,2,1,0:T(8,128)} collective-permute-done((f32[2,4,96,2560]{3,2,1,0:T(8,128)}, f32[2,4,96,2560]{3,2,1,0:T(8,128)}, u32[]{:S(2)}, u32[]{:S(2)}) %collective-permute-start.2) | collective-permute-done | bytes 7864352 | tf_op jit(solution)/shard_map/ppermute | solution.py:52
  74.1 7.1 %bitcast_add_fusion = f32[2,4,96,2560]{3,2,1,0:T(8,128)S(1)} fusion(f32[2,4,96,2560]{3,2,1,0:T(8,128)} %collective-permute-done.2, f32[2,4,2,96,2560]{4,3,2,1,0:T(8,128)} %bitcast.116, s32[]{:T(128)S(6)} %select_n.114), kind=kLoop, calls=%fused_computation | loop fusion | flops 1966080 | bytes 23592964 | tf_op jit(solution)/shard_map/add | solution.py:52
  81.2 2.6 %fusion.36 = (f32[2,4,96,1280]{3,2,1,0:T(8,128)}, f32[2,4,96,1280]{3,2,1,0:T(8,128)S(1)}) fusion(f32[2,4,96,2560]{3,2,1,0:T(8,128)S(1)} %bitcast_add_fusion), kind=kLoop, calls=%fused_computation.76 | loop fusion | bytes 15728640 | tf_op jit(solution)/shard_map/slice | solution.py:55
  83.8 1.9 copy-done.1
  85.7 1.0 dynamic-slice_bitcast_fusion.2
  86.7 1.5 collective-permute-start.3
  88.2 2.3 dynamic-slice_bitcast_fusion.1
  90.5 1.7 collective-permute-start.6
  92.2 5.4 %convolution_bitcast_fusion = f32[1536,256]{0,1:T(8,128)S(1)} fusion(bf16[256,2560]{1,0:T(8,128)(2,1)S(1)} %copy-done.9, bf16[1536,2560]{0,1:T(8,128)(2,1)} %bitcast.118), kind=kOutput, calls=%fused_computation.3 | convolution fusion | flops 2013265920 | bytes 10747904 | tf_op jit(solution)/shard_map/dot_general | solution.py:149
  97.6 1.7 copy.47
  99.4 4.0 %all-to-all-start.2 = ((f32[8,192,256]{2,1,0:T(8,128)}), f32[8,192,256]{2,1,0:T(8,128)S(1)}, u32[]{:S(2)}, u32[]{:S(2)}) async-start(f32[8,192,256]{2,1,0:T(8,128)} %bitcast.21), calls=%async_computation.2 | async-start | bytes 3145728 | tf_op jit(solution)/shard_map/all_to_all | solution.py:150
  103.4 8.7 %collective-permute-done.3 = f32[2,96,1280]{2,1,0:T(8,128)} collective-permute-done((f32[2,96,1280]{2,1,0:T(8,128)}, f32[2,96,1280]{2,1,0:T(8,128)}, u32[]{:S(2)}, u32[]{:S(2)}) %collective-permute-start.3) | collective-permute-done | bytes 983072 | tf_op jit(solution)/shard_map/ppermute | solution.py:61
  112.0 2.5 %bitcast_add_fusion.6 = f32[2,96,1280]{2,1,0:T(8,128)} fusion(f32[2,96,1280]{2,1,0:T(8,128)} %collective-permute-done.3, f32[2,4,96,1280]{3,2,1,0:T(8,128)} %copy-done.1, s32[]{:T(128)S(6)} %select_n.120), kind=kLoop, calls=%fused_computation.41 | loop fusion | flops 245760 | bytes 2949124 | tf_op jit(solution)/shard_map/add | solution.py:63
  114.9 2.6 %bitcast_add_fusion.3 = f32[2,96,1280]{2,1,0:T(8,128)} fusion(f32[2,96,1280]{2,1,0:T(8,128)} %collective-permute-done.6, f32[2,4,96,1280]{3,2,1,0:T(8,128)} %get-tuple-element.8, s32[]{:T(128)S(6)} %select_n.128), kind=kLoop, calls=%fused_computation.38 | loop fusion | flops 245760 | bytes 2949124 | tf_op jit(solution)/shard_map/add | solution.py:64
  117.5 2.9 %collective-permute-start.7 = (f32[2,96,1280]{2,1,0:T(8,128)}, f32[2,96,1280]{2,1,0:T(8,128)}, u32[]{:S(2)}, u32[]{:S(2)}) collective-permute-start(f32[2,96,1280]{2,1,0:T(8,128)} %bitcast_add_fusion.3), channel_id=1, source_target_pairs={{0,48},{8,56},{16,0},{24,8},{32,16},{40,24},{48,32},{56,40},{1,49}... | collective-permute-start | bytes 2949128 | tf_op jit(solution)/shard_map/ppermute | solution.py:62
  120.4 1.2 pad_maximum_fusion
  121.6 2.8 %broadcast_in_dim_reshape.3 = bf16[1,4,96,16,96]{4,3,2,1,0:T(8,128)(2,1)S(1)} reshape(bf16[4,96,1536]{2,1,0:T(8,128)(2,1)} %pad_maximum_fusion) | data formatting | bytes 2359296 | tf_op jit(solution)/shard_map/broadcast_in_dim;reshape | solution.py:156
  124.4 1.5 copy.43
  126.0 4.3 %all-to-all-start = ((bf16[1,4,96,16,96]{4,2,1,0,3:T(8,128)(2,1)}), bf16[1,4,96,16,96]{4,2,1,0,3:T(8,128)(2,1)S(1)}, u32[]{:S(2)}, u32[]{:S(2)}) async-start(bf16[1,4,96,16,96]{4,2,1,0,3:T(8,128)(2,1)} %copy.43), calls=%async_computation | async-start | bytes 3145728 | tf_op jit(solution)/shard_map/all_to_all | solution.py:156
  130.3 13.7 %collective-permute-done.4 = f32[2,96,1280]{2,1,0:T(8,128)} collective-permute-done((f32[2,96,1280]{2,1,0:T(8,128)}, f32[2,96,1280]{2,1,0:T(8,128)}, u32[]{:S(2)}, u32[]{:S(2)}) %collective-permute-start.4) | collective-permute-done | bytes 983072 | tf_op jit(solution)/shard_map/ppermute | solution.py:61
  144.0 2.5 %bitcast_add_fusion.5 = f32[2,96,1280]{2,1,0:T(8,128)} fusion(f32[2,96,1280]{2,1,0:T(8,128)} %collective-permute-done.4, f32[2,4,96,1280]{3,2,1,0:T(8,128)} %copy-done.1, s32[]{:T(128)S(6)} %select_n.122), kind=kLoop, calls=%fused_computation.40 | loop fusion | flops 245760 | bytes 2949124 | tf_op jit(solution)/shard_map/add | solution.py:63
  146.6 2.6 %bitcast_add_fusion.2 = f32[2,96,1280]{2,1,0:T(8,128)} fusion(f32[2,96,1280]{2,1,0:T(8,128)} %collective-permute-done.7, f32[2,4,96,1280]{3,2,1,0:T(8,128)} %get-tuple-element.8, s32[]{:T(128)S(6)} %select_n.130), kind=kLoop, calls=%fused_computation.37 | loop fusion | flops 245760 | bytes 2949124 | tf_op jit(solution)/shard_map/add | solution.py:64
  149.2 5.2 %collective-permute-start.8 = (f32[2,96,1280]{2,1,0:T(8,128)}, f32[2,96,1280]{2,1,0:T(8,128)}, u32[]{:S(2)}, u32[]{:S(2)}) collective-permute-start(f32[2,96,1280]{2,1,0:T(8,128)} %bitcast_add_fusion.2), channel_id=1, source_target_pairs={{0,48},{8,56},{16,0},{24,8},{32,16},{40,24},{48,32},{56,40},{1,49}... | collective-permute-start | bytes 2949128 | tf_op jit(solution)/shard_map/ppermute | solution.py:62
  154.5 5.3 %all-to-all-done = bf16[1,4,96,16,96]{4,2,1,0,3:T(8,128)(2,1)S(1)} async-done(((bf16[1,4,96,16,96]{4,2,1,0,3:T(8,128)(2,1)}), bf16[1,4,96,16,96]{4,2,1,0,3:T(8,128)(2,1)S(1)}, u32[]{:S(2)}, u32[]{:S(2)}) %all-to-all-start) | async-done | bytes 1179680 | tf_op jit(solution)/shard_map/all_to_all | solution.py:156
  159.8 1.4 broadcast_in_dim.17
  161.2 6.7 %all-to-all-start.3 = ((bf16[16,192,256]{2,1,0:T(8,128)(2,1)}), bf16[16,192,256]{2,1,0:T(8,128)(2,1)S(1)}, u32[]{:S(2)}, u32[]{:S(2)}) async-start(bf16[16,192,256]{2,1,0:T(8,128)(2,1)} %broadcast_in_dim.17), calls=%async_computation.3 | async-start | bytes 3145728 | tf_op jit(solution)/shard_map/all_to_all | solution.py:163
  168.0 14.0 %collective-permute-done.5 = f32[2,96,1280]{2,1,0:T(8,128)} collective-permute-done((f32[2,96,1280]{2,1,0:T(8,128)}, f32[2,96,1280]{2,1,0:T(8,128)}, u32[]{:S(2)}, u32[]{:S(2)}) %collective-permute-start.5) | collective-permute-done | bytes 983072 | tf_op jit(solution)/shard_map/ppermute | solution.py:61
  181.9 1.6 bitcast_add_fusion.4
  183.9 1.6 bitcast_add_fusion.1
  185.5 1.1 fusion.17
  186.7 2.9 %collective-permute-start.9 = (f32[96,2560]{1,0:T(8,128)}, f32[96,2560]{1,0:T(8,128)}, u32[]{:S(2)}, u32[]{:S(2)}) collective-permute-start(f32[96,2560]{1,0:T(8,128)} %fusion.17), channel_id=1, source_target_pairs={{0,64},{64,0},{1,65},{65,1},{2,66},{66,2},{3,67},{67,3},{4,68},{68... | collective-permute-start | bytes 2949128 | tf_op jit(solution)/shard_map/ppermute | solution.py:69
  189.6 1.8 fusion.37
  191.3 4.9 %all-to-all-done.3 = bf16[16,192,256]{2,1,0:T(8,128)(2,1)S(1)} async-done(((bf16[16,192,256]{2,1,0:T(8,128)(2,1)}), bf16[16,192,256]{2,1,0:T(8,128)(2,1)S(1)}, u32[]{:S(2)}, u32[]{:S(2)}) %all-to-all-start.3) | async-done | bytes 1572896 | tf_op jit(solution)/shard_map/all_to_all | solution.py:163
  196.3 1.8 convolution_bitcast_fusion.1
  198.7 0.6 copy-done.12
  199.9 14.8 %collective-permute-done.9 = f32[96,2560]{1,0:T(8,128)} collective-permute-done((f32[96,2560]{1,0:T(8,128)}, f32[96,2560]{1,0:T(8,128)}, u32[]{:S(2)}, u32[]{:S(2)}) %collective-permute-start.9) | collective-permute-done | bytes 983072 | tf_op jit(solution)/shard_map/ppermute | solution.py:69
  214.7 2.1 multiply_reduce_fusion.1
  216.8 1.3 broadcast_in_dim.18
  218.1 8.8 %all-to-all-start.4 = ((f32[128,1,1]{2,1,0:T(1,128)}), f32[128,1,1]{2,1,0:T(1,128)S(1)}, u32[]{:S(2)}, u32[]{:S(2)}) async-start(f32[128,1,1]{2,1,0:T(1,128)} %broadcast_in_dim.18), calls=%async_computation.4 | async-start | bytes 131072 | tf_op jit(solution)/shard_map/all_to_all | solution.py:184
  226.9 0.7 pad_maximum_fusion.5
  227.7 8.7 %all-to-all-done.4 = f32[128,1,1]{2,1,0:T(1,128)S(1)} async-done(((f32[128,1,1]{2,1,0:T(1,128)}), f32[128,1,1]{2,1,0:T(1,128)S(1)}, u32[]{:S(2)}, u32[]{:S(2)}) %all-to-all-start.4) | async-done | bytes 544 | tf_op jit(solution)/shard_map/all_to_all | solution.py:184
  236.4 0.7 reduce_sum.39
  237.9 2.1 reshape.159
  (51 shorter events, 2.5 us)
Async XLA Ops:
  0.6 8.5 %copy-start.7 = (bf16[4,64,1536]{2,1,0:T(8,128)(2,1)S(1)}, bf16[4,64,1536]{2,1,0:T(8,128)(2,1)}, u32[]{:S(2)}) copy-start(bf16[4,64,1536]{2,1,0:T(8,128)(2,1)} %param.7) | copy-start | bytes 2359300
  0.6 8.4 %copy-start.14 = (s32[1,20]{1,0:T(1,128)S(1)}, s32[1,20]{1,0:T(1,128)}, u32[]{:S(2)}) copy-start(s32[1,20]{1,0:T(1,128)} %param.12) | copy-start | bytes 244
  4.6 8.5 %copy-start.10 = (bf16[4,64,1536]{2,1,0:T(8,128)(2,1)}, bf16[4,64,1536]{2,1,0:T(8,128)(2,1)S(1)}, u32[]{:S(2)}) copy-start(bf16[4,64,1536]{2,1,0:T(8,128)(2,1)S(1)} %fusion.12) | copy-start | bytes 2359300
  4.7 4.6 %copy-start.15 = (s32[4]{0:T(128)S(1)}, s32[4]{0:T(128)}, u32[]{:S(2)}) copy-start(s32[4]{0:T(128)} %param.13) | copy-start | bytes 52
  4.7 7.0 %collective-permute-start.1 = (bf16[4,16,1536]{2,1,0:T(8,128)(2,1)S(1)}, bf16[4,16,1536]{2,1,0:T(8,128)(2,1)S(1)}, u32[]{:S(2)}, u32[]{:S(2)}) collective-permute-start(bf16[4,16,1536]{2,1,0:T(8,128)(2,1)S(1)} %get-tuple-element.14), channel_id=1, source_target_pairs={{8,0},{16,8},{24,16},{32,24},{40,32},{48,40},{56,48},{9,1},{17,9},... | collective-permute-start | bytes 589832 | tf_op jit(solution)/shard_map/ppermute | solution.py:27
  6.0 7.1 %collective-permute-start = (bf16[4,16,1536]{2,1,0:T(8,128)(2,1)S(1)}, bf16[4,16,1536]{2,1,0:T(8,128)(2,1)S(1)}, u32[]{:S(2)}, u32[]{:S(2)}) collective-permute-start(bf16[4,16,1536]{2,1,0:T(8,128)(2,1)S(1)} %get-tuple-element.13), channel_id=1, source_target_pairs={{0,8},{8,16},{16,24},{24,32},{32,40},{40,48},{48,56},{1,9},{9,17},... | collective-permute-start | bytes 589832 | tf_op jit(solution)/shard_map/ppermute | solution.py:25
  15.7 22.6 %all-to-all-start.1 = ((bf16[1,4,64,8,192]{4,2,1,0,3:T(8,128)(2,1)}), bf16[1,4,64,8,192]{4,2,1,0,3:T(8,128)(2,1)}, u32[]{:S(2)}, u32[]{:S(2)}) async-start(bf16[1,4,64,8,192]{4,2,1,0,3:T(8,128)(2,1)} %broadcast_in_dim_broadcast_in_dim.2), calls=%async_computation.1 | async-start | bytes 2097152 | tf_op jit(solution)/shard_map/all_to_all | solution.py:110
  43.8 7.4 %copy-start.6 = (bf16[256,1536]{1,0:T(8,128)(2,1)S(1)}, bf16[256,1536]{1,0:T(8,128)(2,1)}, u32[]{:S(2)}) copy-start(bf16[256,1536]{1,0:T(8,128)(2,1)} %reshape_reshape.3) | copy-start | bytes 2359300
  51.2 2.3 copy-start.8
  53.5 7.8 %copy-start = (f32[1536,2560]{1,0:T(8,128)}, f32[1536,2560]{1,0:T(8,128)S(1)}, u32[]{:S(2)}) copy-start(f32[1536,2560]{1,0:T(8,128)S(1)} %fusion.39) | copy-start | bytes 47185924
  61.3 12.8 %collective-permute-start.2 = (f32[2,4,96,2560]{3,2,1,0:T(8,128)}, f32[2,4,96,2560]{3,2,1,0:T(8,128)}, u32[]{:S(2)}, u32[]{:S(2)}) collective-permute-start(f32[2,4,96,2560]{3,2,1,0:T(8,128)} %dynamic-slice_bitcast_fusion), channel_id=1, source_target_pairs={{0,8},{8,0},{16,24},{24,16},{32,40},{40,32},{48,56},{56,48},{1,9},... | collective-permute-start | bytes 23592968 | tf_op jit(solution)/shard_map/ppermute | solution.py:52
  83.8 1.9 copy-start.1
  85.7 6.5 %copy-start.9 = (bf16[256,2560]{1,0:T(8,128)(2,1)S(1)}, bf16[256,2560]{1,0:T(8,128)(2,1)}, u32[]{:S(2)}) copy-start(bf16[256,2560]{1,0:T(8,128)(2,1)} %copy-done.8) | copy-start | bytes 3932164
  86.7 25.3 %collective-permute-start.3 = (f32[2,96,1280]{2,1,0:T(8,128)}, f32[2,96,1280]{2,1,0:T(8,128)}, u32[]{:S(2)}, u32[]{:S(2)}) collective-permute-start(f32[2,96,1280]{2,1,0:T(8,128)} %dynamic-slice_bitcast_fusion.2), channel_id=1, source_target_pairs={{0,16},{8,24},{16,32},{24,40},{32,48},{40,56},{48,0},{56,8},{1,17}... | collective-permute-start | bytes 2949128 | tf_op jit(solution)/shard_map/ppermute | solution.py:61
  90.5 24.4 %collective-permute-start.6 = (f32[2,96,1280]{2,1,0:T(8,128)}, f32[2,96,1280]{2,1,0:T(8,128)}, u32[]{:S(2)}, u32[]{:S(2)}) collective-permute-start(f32[2,96,1280]{2,1,0:T(8,128)} %dynamic-slice_bitcast_fusion.1), channel_id=1, source_target_pairs={{0,48},{8,56},{16,0},{24,8},{32,16},{40,24},{48,32},{56,40},{1,49}... | collective-permute-start | bytes 2949128 | tf_op jit(solution)/shard_map/ppermute | solution.py:62
  99.4 26.6 %all-to-all-start.2 = ((f32[8,192,256]{2,1,0:T(8,128)}), f32[8,192,256]{2,1,0:T(8,128)S(1)}, u32[]{:S(2)}, u32[]{:S(2)}) async-start(f32[8,192,256]{2,1,0:T(8,128)} %bitcast.21), calls=%async_computation.2 | async-start | bytes 3145728 | tf_op jit(solution)/shard_map/all_to_all | solution.py:150
  114.6 5.9 %copy-start.11 = (bf16[4,64,1536]{2,1,0:T(8,128)(2,1)S(1)}, bf16[4,64,1536]{2,1,0:T(8,128)(2,1)}, u32[]{:S(2)}) copy-start(bf16[4,64,1536]{2,1,0:T(8,128)(2,1)} %copy-done.10) | copy-start | bytes 2359300
  114.6 29.4 %collective-permute-start.4 = (f32[2,96,1280]{2,1,0:T(8,128)}, f32[2,96,1280]{2,1,0:T(8,128)}, u32[]{:S(2)}, u32[]{:S(2)}) collective-permute-start(f32[2,96,1280]{2,1,0:T(8,128)} %bitcast_add_fusion.6), channel_id=1, source_target_pairs={{0,16},{8,24},{16,32},{24,40},{32,48},{40,56},{48,0},{56,8},{1,17}... | collective-permute-start | bytes 2949128 | tf_op jit(solution)/shard_map/ppermute | solution.py:61
  117.5 29.1 %collective-permute-start.7 = (f32[2,96,1280]{2,1,0:T(8,128)}, f32[2,96,1280]{2,1,0:T(8,128)}, u32[]{:S(2)}, u32[]{:S(2)}) collective-permute-start(f32[2,96,1280]{2,1,0:T(8,128)} %bitcast_add_fusion.3), channel_id=1, source_target_pairs={{0,48},{8,56},{16,0},{24,8},{32,16},{40,24},{48,32},{56,40},{1,49}... | collective-permute-start | bytes 2949128 | tf_op jit(solution)/shard_map/ppermute | solution.py:62
  126.0 33.8 %all-to-all-start = ((bf16[1,4,96,16,96]{4,2,1,0,3:T(8,128)(2,1)}), bf16[1,4,96,16,96]{4,2,1,0,3:T(8,128)(2,1)S(1)}, u32[]{:S(2)}, u32[]{:S(2)}) async-start(bf16[1,4,96,16,96]{4,2,1,0,3:T(8,128)(2,1)} %copy.43), calls=%async_computation | async-start | bytes 3145728 | tf_op jit(solution)/shard_map/all_to_all | solution.py:156
  146.6 35.4 %collective-permute-start.5 = (f32[2,96,1280]{2,1,0:T(8,128)}, f32[2,96,1280]{2,1,0:T(8,128)}, u32[]{:S(2)}, u32[]{:S(2)}) collective-permute-start(f32[2,96,1280]{2,1,0:T(8,128)} %bitcast_add_fusion.5), channel_id=1, source_target_pairs={{0,16},{8,24},{16,32},{24,40},{32,48},{40,56},{48,0},{56,8},{1,17}... | collective-permute-start | bytes 2949128 | tf_op jit(solution)/shard_map/ppermute | solution.py:61
  149.2 34.8 %collective-permute-start.8 = (f32[2,96,1280]{2,1,0:T(8,128)}, f32[2,96,1280]{2,1,0:T(8,128)}, u32[]{:S(2)}, u32[]{:S(2)}) collective-permute-start(f32[2,96,1280]{2,1,0:T(8,128)} %bitcast_add_fusion.2), channel_id=1, source_target_pairs={{0,48},{8,56},{16,0},{24,8},{32,16},{40,24},{48,32},{56,40},{1,49}... | collective-permute-start | bytes 2949128 | tf_op jit(solution)/shard_map/ppermute | solution.py:62
  161.2 35.1 %all-to-all-start.3 = ((bf16[16,192,256]{2,1,0:T(8,128)(2,1)}), bf16[16,192,256]{2,1,0:T(8,128)(2,1)S(1)}, u32[]{:S(2)}, u32[]{:S(2)}) async-start(bf16[16,192,256]{2,1,0:T(8,128)(2,1)} %broadcast_in_dim.17), calls=%async_computation.3 | async-start | bytes 3145728 | tf_op jit(solution)/shard_map/all_to_all | solution.py:163
  183.5 3.1 %copy-start.2 = (f32[2,96,1280]{2,1,0:T(8,128)}, f32[2,96,1280]{2,1,0:T(8,128)S(1)}, u32[]{:S(2)}) copy-start(f32[2,96,1280]{2,1,0:T(8,128)S(1)} %bitcast_add_fusion.4) | copy-start | bytes 2949124
  185.5 4.0 %copy-start.4 = (f32[2,96,1280]{2,1,0:T(8,128)}, f32[2,96,1280]{2,1,0:T(8,128)S(1)}, u32[]{:S(2)}) copy-start(f32[2,96,1280]{2,1,0:T(8,128)S(1)} %bitcast_add_fusion.1) | copy-start | bytes 2949124
  186.7 28.1 %collective-permute-start.9 = (f32[96,2560]{1,0:T(8,128)}, f32[96,2560]{1,0:T(8,128)}, u32[]{:S(2)}, u32[]{:S(2)}) collective-permute-start(f32[96,2560]{1,0:T(8,128)} %fusion.17), channel_id=1, source_target_pairs={{0,64},{64,0},{1,65},{65,1},{2,66},{66,2},{3,67},{67,3},{4,68},{68... | collective-permute-start | bytes 2949128 | tf_op jit(solution)/shard_map/ppermute | solution.py:69
  191.3 6.8 %copy-start.13 = (bf16[16,4,64,96]{3,2,1,0:T(8,128)(2,1)S(1)}, bf16[16,4,64,96]{3,2,1,0:T(8,128)(2,1)}, u32[]{:S(2)}) copy-start(bf16[16,4,64,96]{3,2,1,0:T(8,128)(2,1)} %get-tuple-element.12) | copy-start | bytes 2359300
  198.1 1.2 copy-start.12
  198.7 16.0 %copy-start.3 = (f32[2,96,1280]{2,1,0:T(8,128)S(1)}, f32[2,96,1280]{2,1,0:T(8,128)}, u32[]{:S(2)}) copy-start(f32[2,96,1280]{2,1,0:T(8,128)} %copy-done.2) | copy-start | bytes 2949124
  198.7 16.0 %copy-start.5 = (f32[2,96,1280]{2,1,0:T(8,128)S(1)}, f32[2,96,1280]{2,1,0:T(8,128)}, u32[]{:S(2)}) copy-start(f32[2,96,1280]{2,1,0:T(8,128)} %copy-done.4) | copy-start | bytes 2949124
  218.1 18.2 %all-to-all-start.4 = ((f32[128,1,1]{2,1,0:T(1,128)}), f32[128,1,1]{2,1,0:T(1,128)S(1)}, u32[]{:S(2)}, u32[]{:S(2)}) async-start(f32[128,1,1]{2,1,0:T(1,128)} %broadcast_in_dim.18), calls=%async_computation.4 | async-start | bytes 131072 | tf_op jit(solution)/shard_map/all_to_all | solution.py:184

commit v10 on v8

--- a/solution.py
+++ b/solution.py
@@ -160,9 +160,10 @@
     deltas_for_back, head_partial = lax.optimization_barrier((flat_deltas, head_partial))
     grad_share = ring_scatter(head_partial)
     back_t = jnp.dot(weights_here, deltas_for_back.T, preferred_element_type=jnp.float32)
-    backward_portion = lax.psum_scatter(back_t, "trk", scatter_dimension=0, tiled=True).astype(
-        jnp.bfloat16
-    )
+    back_from_owners = lax.all_to_all(
+        back_t.reshape(trk_n, out_share, sample_count * local_rows), "trk", 0, 0, tiled=True
+    )
+    backward_portion = jnp.sum(back_from_owners, axis=0).astype(jnp.bfloat16)
     group_count = lax.axis_size("sec") * lax.axis_size("seq")
     share_rows = width_all // group_count
     hidden_parts = lax.all_to_all(
@@ -172,7 +173,13 @@
         0,
         tiled=False,
     )
-    back_parts = lax.all_gather(backward_portion, ("sec", "seq"), axis=0, tiled=False)
+    back_parts = lax.all_to_all(
+        jnp.broadcast_to(backward_portion[None], (group_count,) + backward_portion.shape),
+        ("sec", "seq"),
+        0,
+        0,
+        tiled=True,
+    )
     per_tap = [
         lax.dot_general(
             hidden_parts[

time: 263 us -> 244 us (0.928)
  waiting for transfers between devices: 106 us -> 86.9 us
  between operations: 15.4 us -> 1.83 us
  starting transfers between devices: 46.7 us -> 56.4 us
    reduce_scatter x1 -> x0, waiting for transfers between devices: 41.4 us -> none  [body(): lax.psum_scatter(back_t, 'trk', scatter_dimension=0, tiled=True)]
    ppermute x6, waiting for transfers between devices: 7.95 us -> 35.5 us  [x_ring(): got_a = lax.ppermute(send_a, 'seq', to_next)]
    ppermute x6, waiting for transfers between devices: 28.4 us -> 10.3 us  [x_ring(): got_b = lax.ppermute(send_b, 'seq', to_prev)]
    all_to_all x0 -> x2, waiting for transfers between devices: none -> 15 us  [the longest x1 15 us: body(): lax.all_to_all(back_t.reshape(trk_n, out_share, sample_count * local_rows...]
    all_to_all x0 -> x2, starting transfers between devices: none -> 8.15 us  [the longest x1 4.44 us: body(): lax.all_to_all(back_t.reshape(trk_n, out_share, sample_count * local_rows...]
    unnamed x43 -> x40, local copies, waits for them, and re-layouts: 20 us -> 15.8 us
    ppermute x2, waiting for transfers between devices: 6.2 us -> 2.14 us  [sec_pair(): lax.ppermute(other, 'sec', [(i, (i - shift) % sec_n) for i in range(sec_n)])]
    ppermute x2, starting transfers between devices: 2.12 us -> 5.72 us  [sec_pair(): lax.ppermute(other, 'sec', [(i, (i - shift) % sec_n) for i in range(sec_n)])]
  transfers between devices with their start and end apart: 22 -> 22, of which waited for: 15 -> 13; matrix products, arithmetic and copies ran while one was open for 20% -> 23% of each run, Pallas kernels for 0% -> 0%
where the time goes in v10:
time: 244 us; the launch traced here: 242 us
  waiting for transfers between devices  86.9 us (36%)
  starting transfers between devices  56.4 us (23%)
  local copies, waits for them, and re-layouts  47.5 us (19%)
  other arithmetic  25.7 us (11%)
  matrix products  23.5 us (10%)
    ppermute x6, waiting for transfers between devices, x_ring(): got_a = lax.ppermute(send_a, 'seq', to_next)  35.5 us
    ppermute x6, starting transfers between devices, x_ring(): got_b = lax.ppermute(send_b, 'seq', to_prev)  15.8 us
    unnamed x40, local copies, waits for them, and re-layouts  15.8 us
    all_to_all x1, waiting for transfers between devices, body(): lax.all_to_all(back_t.reshape(trk_n, out_share, sample_count * local_rows...  15 us
    all_to_all x1, waiting for transfers between devices, body(): lax.all_to_all(padded_input.reshape(sample_count, local_rows + 2 * DILATI...  13.2 us
    ppermute x6, waiting for transfers between devices, x_ring(): got_b = lax.ppermute(send_b, 'seq', to_prev)  10.3 us
    add x1, other arithmetic, ring_scatter(): summed = keep + lax.ppermute(give, 'seq', core_pairs)  10.2 us
    all_to_all x1, waiting for transfers between devices, body(): lax.all_to_all(jnp.broadcast_to(jnp.sum(grad_share * grad_share), (device...  8.75 us
  transfers between devices with their start and end apart: 22, of which 13 were waited for; matrix products, arithmetic and copies ran while one was open for 23% of the time, Pallas kernels for 0%

profile of v10, /device:TPU:0, one launch (start us, length us, event | category | flops | bytes accessed | tf_op | source)
XLA Modules:
  0.0 241.8 jit_solution(3241933032590107665)
XLA Ops:
  1.4 1.4 multiply_reduce_fusion
  2.8 1.8 fusion.12
  4.7 1.3 collective-permute-start.1
  6.0 3.0 %collective-permute-start = (bf16[4,16,1536]{2,1,0:T(8,128)(2,1)S(1)}, bf16[4,16,1536]{2,1,0:T(8,128)(2,1)S(1)}, u32[]{:S(2)}, u32[]{:S(2)}) collective-permute-start(bf16[4,16,1536]{2,1,0:T(8,128)(2,1)S(1)} %get-tuple-element.13), channel_id=1, source_target_pairs={{0,8},{8,16},{16,24},{24,32},{32,40},{40,48},{48,56},{1,9},{9,17},... | collective-permute-start | bytes 589832 | tf_op jit(solution)/shard_map/ppermute | solution.py:25
  9.3 1.4 fusion.21
  11.7 1.4 fusion.16
  13.1 1.5 fusion.15
  14.6 1.1 broadcast_in_dim_broadcast_in_dim.2
  15.7 6.4 %all-to-all-start.1 = ((bf16[1,4,64,8,192]{4,2,1,0,3:T(8,128)(2,1)}), bf16[1,4,64,8,192]{4,2,1,0,3:T(8,128)(2,1)}, u32[]{:S(2)}, u32[]{:S(2)}) async-start(bf16[1,4,64,8,192]{4,2,1,0,3:T(8,128)(2,1)} %broadcast_in_dim_broadcast_in_dim.2), calls=%async_computation.1 | async-start | bytes 2097152 | tf_op jit(solution)/shard_map/all_to_all | solution.py:123
  22.1 2.1 copy.46
  24.2 10.7 %copy.45 = bf16[1536,1,20,128]{0,3,2,1:T(8,128)(2,1)} copy(bf16[1536,1,20,128]{3,0,2,1:T(8,128)(2,1)} %param.10) | data formatting | bytes 15728640 | tf_op args[3]
  34.9 1.4 bitcast_multiply_fusion
  36.4 1.9 all-to-all-done.1
  38.3 2.8 %copy.44 = bf16[4,64,8,192]{3,2,1,0:T(8,128)(2,1)} copy(bf16[4,64,8,192]{3,1,0,2:T(8,128)(2,1)} %bitcast.13) | data formatting | bytes 1572864 | tf_op jit(solution)/shard_map/transpose | solution.py:130
  41.1 2.8 %reshape_reshape.3 = bf16[256,1536]{1,0:T(8,128)(2,1)} reshape(bf16[4,64,8,192]{3,2,1,0:T(8,128)(2,1)} %copy.44) | data formatting | bytes 1572864 | tf_op jit(solution)/shard_map/reshape;reshape | solution.py:143
  43.8 8.6 %fusion.4 = bf16[256,2560]{1,0:T(8,128)(2,1)} fusion(f32[32,8,20,128]{3,2,1,0:T(8,128)S(1)} %bitcast.141, f32[4,2560]{1,0:T(4,128)} %bitcast_multiply_fusion, bf16[256,1536]{1,0:T(8,128)(2,1)} %reshape_reshape.3, bf16[1536,2560]{0,1:T(8,128)(2,1)} %bitcast.136), kind=kOutput, calls=%fused_computation.8 | convolution fusion | flops 2022440960 | bytes 12623872 | tf_op jit(solution)/shard_map/dot_general | solution.py:144
  52.4 3.9 %fusion.40 = f32[1536,2560]{1,0:T(8,128)S(1)} fusion(bf16[256,1536]{1,0:T(8,128)(2,1)} %reshape_reshape.3, bf16[256,2560]{1,0:T(8,128)(2,1)} %fusion.4), kind=kOutput, calls=%fused_computation.91 | convolution fusion | flops 2013265920 | bytes 17825792 | tf_op jit(solution)/shard_map/dot_general | solution.py:35
  56.4 3.7 %dynamic-slice_bitcast_fusion = f32[2,4,96,2560]{3,2,1,0:T(8,128)} fusion(f32[2,4,2,96,2560]{4,3,2,1,0:T(8,128)S(1)} %bitcast.134, s32[]{:T(128)S(6)} %select_n.145), kind=kLoop, calls=%fused_computation.1 | loop fusion | bytes 15728644 | tf_op jit(solution)/shard_map/jit(dynamic_index_in_dim)/squeeze | solution.py:50
  60.1 4.3 %copy-done = f32[1536,2560]{1,0:T(8,128)} copy-done((f32[1536,2560]{1,0:T(8,128)}, f32[1536,2560]{1,0:T(8,128)S(1)}, u32[]{:S(2)}) %copy-start) | copy-done | bytes 15728664
  64.4 2.2 convolution_bitcast_fusion
  66.6 1.6 copy.47
  68.3 4.4 %all-to-all-start.2 = ((f32[8,192,256]{2,1,0:T(8,128)}), f32[8,192,256]{2,1,0:T(8,128)S(1)}, u32[]{:S(2)}, u32[]{:S(2)}) async-start(f32[8,192,256]{2,1,0:T(8,128)} %bitcast.21), calls=%async_computation.2 | async-start | bytes 3145728 | tf_op jit(solution)/shard_map/all_to_all | solution.py:163
  72.7 1.1 pad_maximum_fusion
  73.8 2.8 %broadcast_in_dim_reshape.3 = bf16[1,4,96,16,96]{4,3,2,1,0:T(8,128)(2,1)S(1)} reshape(bf16[4,96,1536]{2,1,0:T(8,128)(2,1)} %pad_maximum_fusion) | data formatting | bytes 2359296 | tf_op jit(solution)/shard_map/broadcast_in_dim;reshape | solution.py:169
  76.7 1.6 copy.43
  78.3 15.0 %all-to-all-done.2 = f32[8,192,256]{2,1,0:T(8,128)S(1)} async-done(((f32[8,192,256]{2,1,0:T(8,128)}), f32[8,192,256]{2,1,0:T(8,128)S(1)}, u32[]{:S(2)}, u32[]{:S(2)}) %all-to-all-start.2) | async-done | bytes 1572896 | tf_op jit(solution)/shard_map/all_to_all | solution.py:163
  93.3 7.2 %all-to-all-start = ((bf16[1,4,96,16,96]{4,2,1,0,3:T(8,128)(2,1)}), bf16[1,4,96,16,96]{4,2,1,0,3:T(8,128)(2,1)S(1)}, u32[]{:S(2)}, u32[]{:S(2)}) async-start(bf16[1,4,96,16,96]{4,2,1,0,3:T(8,128)(2,1)} %copy.43), calls=%async_computation | async-start | bytes 3145728 | tf_op jit(solution)/shard_map/all_to_all | solution.py:169
  100.6 10.2 %bitcast_add_fusion = f32[2,4,96,2560]{3,2,1,0:T(8,128)} fusion(f32[2,4,96,2560]{3,2,1,0:T(8,128)} %collective-permute-done.2, f32[2,4,2,96,2560]{4,3,2,1,0:T(8,128)} %bitcast.135, s32[]{:T(128)S(6)} %select_n.144), kind=kLoop, calls=%fused_computation | loop fusion | flops 1966080 | bytes 23592964 | tf_op jit(solution)/shard_map/add | solution.py:52
  110.8 13.2 %all-to-all-done = bf16[1,4,96,16,96]{4,2,1,0,3:T(8,128)(2,1)S(1)} async-done(((bf16[1,4,96,16,96]{4,2,1,0,3:T(8,128)(2,1)}), bf16[1,4,96,16,96]{4,2,1,0,3:T(8,128)(2,1)S(1)}, u32[]{:S(2)}, u32[]{:S(2)}) %all-to-all-start) | async-done | bytes 1179680 | tf_op jit(solution)/shard_map/all_to_all | solution.py:169
  124.0 1.3 broadcast_in_dim.17
  125.3 3.7 %all-to-all-start.3 = ((bf16[16,192,256]{2,1,0:T(8,128)(2,1)}), bf16[16,192,256]{2,1,0:T(8,128)(2,1)S(1)}, u32[]{:S(2)}, u32[]{:S(2)}) async-start(bf16[16,192,256]{2,1,0:T(8,128)(2,1)} %broadcast_in_dim.17), calls=%async_computation.3 | async-start | bytes 3145728 | tf_op jit(solution)/shard_map/all_to_all | solution.py:176
  129.1 2.4 %fusion.36 = (f32[2,4,96,640]{3,2,1,0:T(8,128)S(1)}, f32[2,4,96,640]{3,2,1,0:T(8,128)S(1)}) fusion(f32[2,4,96,2560]{3,2,1,0:T(8,128)} %bitcast_add_fusion), kind=kLoop, calls=%fused_computation.87 | loop fusion | bytes 7864320 | tf_op jit(solution)/shard_map/slice | solution.py:59
  131.6 1.9 collective-permute-start.3
  133.4 1.9 fusion.38
  135.3 2.4 slice.72
  137.7 1.9 collective-permute-start.6
  139.6 1.5 dynamic-slice_bitcast_fusion.1
  141.1 3.3 %collective-permute-start.10 = (f32[4,96,1280]{2,1,0:T(8,128)}, f32[4,96,1280]{2,1,0:T(8,128)}, u32[]{:S(2)}, u32[]{:S(2)}) collective-permute-start(f32[4,96,1280]{2,1,0:T(8,128)} %dynamic-slice_bitcast_fusion.1), channel_id=1, source_target_pairs={{0,64},{64,0},{1,65},{65,1},{2,66},{66,2},{3,67},{67,3},{4,68},{68... | collective-permute-start | bytes 5898248 | tf_op jit(solution)/shard_map/ppermute | solution.py:77
  144.4 16.3 %collective-permute-done.3 = f32[2,96,640]{2,1,0:T(8,128)S(1)} collective-permute-done((f32[2,96,640]{2,1,0:T(8,128)S(1)}, f32[2,96,640]{2,1,0:T(8,128)S(1)}, u32[]{:S(2)}, u32[]{:S(2)}) %collective-permute-start.3) | collective-permute-done | bytes 491552 | tf_op jit(solution)/shard_map/ppermute | solution.py:63
  161.5 1.5 collective-permute-start.4
  163.0 0.9 bitcast_add_fusion.4
  163.9 1.7 collective-permute-start.7
  165.6 2.6 %convolution_bitcast_fusion.1 = f32[96,1,192]{2,0,1:T(8,128)} fusion(bf16[16,256,96]{2,1,0:T(8,128)(2,1)} %bitcast.144, bf16[16,192,256]{2,1,0:T(8,128)(2,1)S(1)} %all-to-all-done.3), kind=kOutput, calls=%fused_computation.30 | convolution fusion | flops 150994944 | bytes 2433024 | tf_op jit(solution)/shard_map/dot_general | solution.py:184
  168.2 7.8 %collective-permute-done.4 = f32[2,96,640]{2,1,0:T(8,128)} collective-permute-done((f32[2,96,640]{2,1,0:T(8,128)}, f32[2,96,640]{2,1,0:T(8,128)}, u32[]{:S(2)}, u32[]{:S(2)}) %collective-permute-start.4) | collective-permute-done | bytes 491552 | tf_op jit(solution)/shard_map/ppermute | solution.py:63
  176.0 1.1 bitcast_add_fusion.6
  177.6 1.1 bitcast_add_fusion.3
  178.7 2.9 %collective-permute-start.8 = (f32[2,96,640]{2,1,0:T(8,128)S(1)}, f32[2,96,640]{2,1,0:T(8,128)S(1)}, u32[]{:S(2)}, u32[]{:S(2)}) collective-permute-start(f32[2,96,640]{2,1,0:T(8,128)S(1)} %bitcast_add_fusion.3), channel_id=1, source_target_pairs={{0,48},{8,56},{16,0},{24,8},{32,16},{40,24},{48,32},{56,40},{1,49}... | collective-permute-start | bytes 1474568 | tf_op jit(solution)/shard_map/ppermute | solution.py:64
  181.6 1.2 convolution_bitcast_fusion.2
  182.8 7.7 %collective-permute-done.5 = f32[2,96,640]{2,1,0:T(8,128)S(1)} collective-permute-done((f32[2,96,640]{2,1,0:T(8,128)S(1)}, f32[2,96,640]{2,1,0:T(8,128)S(1)}, u32[]{:S(2)}, u32[]{:S(2)}) %collective-permute-start.5) | collective-permute-done | bytes 491552 | tf_op jit(solution)/shard_map/ppermute | solution.py:63
  191.0 2.1 collective-permute-done.10
  193.1 1.9 bitcast_add_fusion.1
  195.2 2.4 collective-permute-start.14
  197.7 2.4 collective-permute-start.9
  200.1 3.0 %collective-permute-done.14 = f32[96,640]{1,0:T(8,128)S(1)} collective-permute-done((f32[96,640]{1,0:T(8,128)S(1)}, f32[96,640]{1,0:T(8,128)S(1)}, u32[]{:S(2)}, u32[]{:S(2)}) %collective-permute-start.14) | collective-permute-done | bytes 245792 | tf_op jit(solution)/shard_map/ppermute | solution.py:64
  203.1 3.2 %collective-permute-start.15 = (f32[96,640]{1,0:T(8,128)S(1)}, f32[96,640]{1,0:T(8,128)S(1)}, u32[]{:S(2)}, u32[]{:S(2)}) collective-permute-start(f32[96,640]{1,0:T(8,128)S(1)} %bitcast_add_fusion.10), channel_id=1, source_target_pairs={{0,48},{8,56},{16,0},{24,8},{32,16},{40,24},{48,32},{56,40},{1,49}... | collective-permute-start | bytes 737288 | tf_op jit(solution)/shard_map/ppermute | solution.py:64
  207.1 3.5 %collective-permute-done.15 = f32[96,640]{1,0:T(8,128)S(1)} collective-permute-done((f32[96,640]{1,0:T(8,128)S(1)}, f32[96,640]{1,0:T(8,128)S(1)}, u32[]{:S(2)}, u32[]{:S(2)}) %collective-permute-start.15) | collective-permute-done | bytes 245792 | tf_op jit(solution)/shard_map/ppermute | solution.py:64
  210.6 3.8 %collective-permute-start.16 = (f32[96,640]{1,0:T(8,128)S(1)}, f32[96,640]{1,0:T(8,128)S(1)}, u32[]{:S(2)}, u32[]{:S(2)}) collective-permute-start(f32[96,640]{1,0:T(8,128)S(1)} %bitcast_add_fusion.9), channel_id=1, source_target_pairs={{0,48},{8,56},{16,0},{24,8},{32,16},{40,24},{48,32},{56,40},{1,49}... | collective-permute-start | bytes 737288 | tf_op jit(solution)/shard_map/ppermute | solution.py:64
  214.6 3.5 %collective-permute-done.16 = f32[96,640]{1,0:T(8,128)S(1)} collective-permute-done((f32[96,640]{1,0:T(8,128)S(1)}, f32[96,640]{1,0:T(8,128)S(1)}, u32[]{:S(2)}, u32[]{:S(2)}) %collective-permute-start.16) | collective-permute-done | bytes 245792 | tf_op jit(solution)/shard_map/ppermute | solution.py:64
  218.1 3.8 %collective-permute-done.13 = f32[96,640]{1,0:T(8,128)S(1)} collective-permute-done((f32[96,640]{1,0:T(8,128)S(1)}, f32[96,640]{1,0:T(8,128)S(1)}, u32[]{:S(2)}, u32[]{:S(2)}) %collective-permute-start.13) | collective-permute-done | bytes 245792 | tf_op jit(solution)/shard_map/ppermute | solution.py:63
  221.9 0.9 multiply_reduce_fusion.1
  222.8 1.3 broadcast_in_dim.18
  224.1 4.6 %all-to-all-start.4 = ((f32[128,1,1]{2,1,0:T(1,128)}), f32[128,1,1]{2,1,0:T(1,128)S(1)}, u32[]{:S(2)}, u32[]{:S(2)}) async-start(f32[128,1,1]{2,1,0:T(1,128)} %broadcast_in_dim.18), calls=%async_computation.4 | async-start | bytes 131072 | tf_op jit(solution)/shard_map/all_to_all | solution.py:197
  229.4 8.8 %all-to-all-done.4 = f32[128,1,1]{2,1,0:T(1,128)S(1)} async-done(((f32[128,1,1]{2,1,0:T(1,128)}), f32[128,1,1]{2,1,0:T(1,128)S(1)}, u32[]{:S(2)}, u32[]{:S(2)}) %all-to-all-start.4) | async-done | bytes 544 | tf_op jit(solution)/shard_map/all_to_all | solution.py:197
  239.7 2.1 mul.126
  (85 shorter events, 6.8 us)
Async XLA Ops:
  0.6 8.5 %copy-start.7 = (bf16[4,64,1536]{2,1,0:T(8,128)(2,1)S(1)}, bf16[4,64,1536]{2,1,0:T(8,128)(2,1)}, u32[]{:S(2)}) copy-start(bf16[4,64,1536]{2,1,0:T(8,128)(2,1)} %param.7) | copy-start | bytes 2359300
  0.6 8.4 %copy-start.15 = (s32[1,20]{1,0:T(1,128)S(1)}, s32[1,20]{1,0:T(1,128)}, u32[]{:S(2)}) copy-start(s32[1,20]{1,0:T(1,128)} %param.12) | copy-start | bytes 244
  4.6 8.5 %copy-start.9 = (bf16[4,64,1536]{2,1,0:T(8,128)(2,1)}, bf16[4,64,1536]{2,1,0:T(8,128)(2,1)S(1)}, u32[]{:S(2)}) copy-start(bf16[4,64,1536]{2,1,0:T(8,128)(2,1)S(1)} %fusion.12) | copy-start | bytes 2359300
  4.7 4.6 %copy-start.16 = (s32[4]{0:T(128)S(1)}, s32[4]{0:T(128)}, u32[]{:S(2)}) copy-start(s32[4]{0:T(128)} %param.13) | copy-start | bytes 52
  4.7 7.0 %collective-permute-start.1 = (bf16[4,16,1536]{2,1,0:T(8,128)(2,1)S(1)}, bf16[4,16,1536]{2,1,0:T(8,128)(2,1)S(1)}, u32[]{:S(2)}, u32[]{:S(2)}) collective-permute-start(bf16[4,16,1536]{2,1,0:T(8,128)(2,1)S(1)} %get-tuple-element.14), channel_id=1, source_target_pairs={{8,0},{16,8},{24,16},{32,24},{40,32},{48,40},{56,48},{9,1},{17,9},... | collective-permute-start | bytes 589832 | tf_op jit(solution)/shard_map/ppermute | solution.py:27
  6.0 7.1 %collective-permute-start = (bf16[4,16,1536]{2,1,0:T(8,128)(2,1)S(1)}, bf16[4,16,1536]{2,1,0:T(8,128)(2,1)S(1)}, u32[]{:S(2)}, u32[]{:S(2)}) collective-permute-start(bf16[4,16,1536]{2,1,0:T(8,128)(2,1)S(1)} %get-tuple-element.13), channel_id=1, source_target_pairs={{0,8},{8,16},{16,24},{24,32},{32,40},{40,48},{48,56},{1,9},{9,17},... | collective-permute-start | bytes 589832 | tf_op jit(solution)/shard_map/ppermute | solution.py:25
  15.7 22.6 %all-to-all-start.1 = ((bf16[1,4,64,8,192]{4,2,1,0,3:T(8,128)(2,1)}), bf16[1,4,64,8,192]{4,2,1,0,3:T(8,128)(2,1)}, u32[]{:S(2)}, u32[]{:S(2)}) async-start(bf16[1,4,64,8,192]{4,2,1,0,3:T(8,128)(2,1)} %broadcast_in_dim_broadcast_in_dim.2), calls=%async_computation.1 | async-start | bytes 2097152 | tf_op jit(solution)/shard_map/all_to_all | solution.py:123
  43.8 20.5 %slice-start = ((s8[7864320]{0:T(1024)(128)(4,1)}), s8[4194304]{0:T(1024)(128)(4,1)S(1)}, s32[]{:S(2)}) async-start(s8[7864320]{0:T(1024)(128)(4,1)} %bitcast.137), calls=%async_computation.5 | async-start | bytes 8388608
  52.4 12.0 %slice-start.1 = ((s8[7864320]{0:T(1024)(128)(4,1)}), s8[3670016]{0:T(1024)(128)(4,1)S(1)}, s32[]{:S(2)}) async-start(s8[7864320]{0:T(1024)(128)(4,1)} %bitcast.137), calls=%async_computation.6 | async-start | bytes 7340032
  56.3 8.0 %copy-start = (f32[1536,2560]{1,0:T(8,128)}, f32[1536,2560]{1,0:T(8,128)S(1)}, u32[]{:S(2)}) copy-start(f32[1536,2560]{1,0:T(8,128)S(1)} %fusion.40) | copy-start | bytes 47185924
  56.4 8.0 %copy-start.8 = (bf16[256,2560]{1,0:T(8,128)(2,1)S(1)}, bf16[256,2560]{1,0:T(8,128)(2,1)}, u32[]{:S(2)}) copy-start(bf16[256,2560]{1,0:T(8,128)(2,1)} %fusion.4) | copy-start | bytes 3932164
  64.4 36.2 %collective-permute-start.2 = (f32[2,4,96,2560]{3,2,1,0:T(8,128)}, f32[2,4,96,2560]{3,2,1,0:T(8,128)}, u32[]{:S(2)}, u32[]{:S(2)}) collective-permute-start(f32[2,4,96,2560]{3,2,1,0:T(8,128)} %dynamic-slice_bitcast_fusion), channel_id=1, source_target_pairs={{0,8},{8,0},{16,24},{24,16},{32,40},{40,32},{48,56},{56,48},{1,9},... | collective-permute-start | bytes 23592968 | tf_op jit(solution)/shard_map/ppermute | solution.py:52
  68.3 4.4 %copy-start.10 = (bf16[4,64,1536]{2,1,0:T(8,128)(2,1)S(1)}, bf16[4,64,1536]{2,1,0:T(8,128)(2,1)}, u32[]{:S(2)}) copy-start(bf16[4,64,1536]{2,1,0:T(8,128)(2,1)} %copy-done.9) | copy-start | bytes 2359300
  68.3 25.0 %all-to-all-start.2 = ((f32[8,192,256]{2,1,0:T(8,128)}), f32[8,192,256]{2,1,0:T(8,128)S(1)}, u32[]{:S(2)}, u32[]{:S(2)}) async-start(f32[8,192,256]{2,1,0:T(8,128)} %bitcast.21), calls=%async_computation.2 | async-start | bytes 3145728 | tf_op jit(solution)/shard_map/all_to_all | solution.py:163
  93.3 30.7 %all-to-all-start = ((bf16[1,4,96,16,96]{4,2,1,0,3:T(8,128)(2,1)}), bf16[1,4,96,16,96]{4,2,1,0,3:T(8,128)(2,1)S(1)}, u32[]{:S(2)}, u32[]{:S(2)}) async-start(bf16[1,4,96,16,96]{4,2,1,0,3:T(8,128)(2,1)} %copy.43), calls=%async_computation | async-start | bytes 3145728 | tf_op jit(solution)/shard_map/all_to_all | solution.py:169
  125.3 40.3 %all-to-all-start.3 = ((bf16[16,192,256]{2,1,0:T(8,128)(2,1)}), bf16[16,192,256]{2,1,0:T(8,128)(2,1)S(1)}, u32[]{:S(2)}, u32[]{:S(2)}) async-start(bf16[16,192,256]{2,1,0:T(8,128)(2,1)} %broadcast_in_dim.17), calls=%async_computation.3 | async-start | bytes 3145728 | tf_op jit(solution)/shard_map/all_to_all | solution.py:176
  131.5 29.2 %copy-start.5 = (f32[2,4,96,640]{3,2,1,0:T(8,128)}, f32[2,4,96,640]{3,2,1,0:T(8,128)S(1)}, u32[]{:S(2)}) copy-start(f32[2,4,96,640]{3,2,1,0:T(8,128)S(1)} %get-tuple-element.7) | copy-start | bytes 5898244
  131.5 31.5 %copy-start.3 = (f32[2,4,96,640]{3,2,1,0:T(8,128)}, f32[2,4,96,640]{3,2,1,0:T(8,128)S(1)}, u32[]{:S(2)}) copy-start(f32[2,4,96,640]{3,2,1,0:T(8,128)S(1)} %get-tuple-element.6) | copy-start | bytes 5898244
  131.6 29.1 %collective-permute-start.3 = (f32[2,96,640]{2,1,0:T(8,128)S(1)}, f32[2,96,640]{2,1,0:T(8,128)S(1)}, u32[]{:S(2)}, u32[]{:S(2)}) collective-permute-start(f32[2,96,640]{2,1,0:T(8,128)S(1)} %dynamic-slice_bitcast_fusion.3), channel_id=1, source_target_pairs={{0,16},{8,24},{16,32},{24,40},{32,48},{40,56},{48,0},{56,8},{1,17}... | collective-permute-start | bytes 1474568 | tf_op jit(solution)/shard_map/ppermute | solution.py:63
  137.7 3.4 %copy-start.1 = (f32[2,4,96,1280]{3,2,1,0:T(8,128)}, f32[2,4,96,1280]{3,2,1,0:T(8,128)S(1)}, u32[]{:S(2)}) copy-start(f32[2,4,96,1280]{3,2,1,0:T(8,128)S(1)} %slice.72) | copy-start | bytes 11796484
  137.7 25.3 %collective-permute-start.6 = (f32[2,96,640]{2,1,0:T(8,128)S(1)}, f32[2,96,640]{2,1,0:T(8,128)S(1)}, u32[]{:S(2)}, u32[]{:S(2)}) collective-permute-start(f32[2,96,640]{2,1,0:T(8,128)S(1)} %dynamic-slice_bitcast_fusion.2), channel_id=1, source_target_pairs={{0,48},{8,56},{16,0},{24,8},{32,16},{40,24},{48,32},{56,40},{1,49}... | collective-permute-start | bytes 1474568 | tf_op jit(solution)/shard_map/ppermute | solution.py:64
  141.1 52.0 %collective-permute-start.10 = (f32[4,96,1280]{2,1,0:T(8,128)}, f32[4,96,1280]{2,1,0:T(8,128)}, u32[]{:S(2)}, u32[]{:S(2)}) collective-permute-start(f32[4,96,1280]{2,1,0:T(8,128)} %dynamic-slice_bitcast_fusion.1), channel_id=1, source_target_pairs={{0,64},{64,0},{1,65},{65,1},{2,66},{66,2},{3,67},{67,3},{4,68},{68... | collective-permute-start | bytes 5898248 | tf_op jit(solution)/shard_map/ppermute | solution.py:77
  161.5 14.5 %copy-start.6 = (f32[2,4,96,640]{3,2,1,0:T(8,128)S(1)}, f32[2,4,96,640]{3,2,1,0:T(8,128)}, u32[]{:S(2)}) copy-start(f32[2,4,96,640]{3,2,1,0:T(8,128)} %copy-done.5) | copy-start | bytes 5898244
  161.5 14.5 %collective-permute-start.4 = (f32[2,96,640]{2,1,0:T(8,128)}, f32[2,96,640]{2,1,0:T(8,128)}, u32[]{:S(2)}, u32[]{:S(2)}) collective-permute-start(f32[2,96,640]{2,1,0:T(8,128)} %bitcast_add_fusion.7), channel_id=1, source_target_pairs={{0,16},{8,24},{16,32},{24,40},{32,48},{40,56},{48,0},{56,8},{1,17}... | collective-permute-start | bytes 1474568 | tf_op jit(solution)/shard_map/ppermute | solution.py:63
  163.9 13.6 %collective-permute-start.7 = (f32[2,96,640]{2,1,0:T(8,128)}, f32[2,96,640]{2,1,0:T(8,128)}, u32[]{:S(2)}, u32[]{:S(2)}) collective-permute-start(f32[2,96,640]{2,1,0:T(8,128)} %bitcast_add_fusion.4), channel_id=1, source_target_pairs={{0,48},{8,56},{16,0},{24,8},{32,16},{40,24},{48,32},{56,40},{1,49}... | collective-permute-start | bytes 1474568 | tf_op jit(solution)/shard_map/ppermute | solution.py:64
  165.6 11.9 %copy-start.4 = (f32[2,4,96,640]{3,2,1,0:T(8,128)S(1)}, f32[2,4,96,640]{3,2,1,0:T(8,128)}, u32[]{:S(2)}) copy-start(f32[2,4,96,640]{3,2,1,0:T(8,128)} %copy-done.3) | copy-start | bytes 5898244
  168.2 13.3 %copy-start.12 = (bf16[16,4,64,96]{3,2,1,0:T(8,128)(2,1)S(1)}, bf16[16,4,64,96]{3,2,1,0:T(8,128)(2,1)}, u32[]{:S(2)}) copy-start(bf16[16,4,64,96]{3,2,1,0:T(8,128)(2,1)} %get-tuple-element.12) | copy-start | bytes 2359300
  177.1 13.4 %collective-permute-start.5 = (f32[2,96,640]{2,1,0:T(8,128)S(1)}, f32[2,96,640]{2,1,0:T(8,128)S(1)}, u32[]{:S(2)}, u32[]{:S(2)}) collective-permute-start(f32[2,96,640]{2,1,0:T(8,128)S(1)} %bitcast_add_fusion.6), channel_id=1, source_target_pairs={{0,16},{8,24},{16,32},{24,40},{32,48},{40,56},{48,0},{56,8},{1,17}... | collective-permute-start | bytes 1474568 | tf_op jit(solution)/shard_map/ppermute | solution.py:63
  178.7 12.2 %collective-permute-start.8 = (f32[2,96,640]{2,1,0:T(8,128)S(1)}, f32[2,96,640]{2,1,0:T(8,128)S(1)}, u32[]{:S(2)}, u32[]{:S(2)}) collective-permute-start(f32[2,96,640]{2,1,0:T(8,128)S(1)} %bitcast_add_fusion.3), channel_id=1, source_target_pairs={{0,48},{8,56},{16,0},{24,8},{32,16},{40,24},{48,32},{56,40},{1,49}... | collective-permute-start | bytes 1474568 | tf_op jit(solution)/shard_map/ppermute | solution.py:64
  181.6 11.5 %copy-start.2 = (f32[2,4,96,1280]{3,2,1,0:T(8,128)S(1)}, f32[2,4,96,1280]{3,2,1,0:T(8,128)}, u32[]{:S(2)}) copy-start(f32[2,4,96,1280]{3,2,1,0:T(8,128)} %copy-done.1) | copy-start | bytes 11796484
  195.1 11.4 %copy-start.11 = (bf16[16,4,64,96]{3,2,1,0:T(8,128)(2,1)S(1)}, bf16[16,4,64,96]{3,2,1,0:T(8,128)(2,1)}, u32[]{:S(2)}) copy-start(bf16[16,4,64,96]{3,2,1,0:T(8,128)(2,1)} %get-tuple-element.10) | copy-start | bytes 2359300
  195.2 7.9 %collective-permute-start.14 = (f32[96,640]{1,0:T(8,128)S(1)}, f32[96,640]{1,0:T(8,128)S(1)}, u32[]{:S(2)}, u32[]{:S(2)}) collective-permute-start(f32[96,640]{1,0:T(8,128)S(1)} %dynamic-slice_bitcast_fusion.4), channel_id=1, source_target_pairs={{0,48},{8,56},{16,0},{24,8},{32,16},{40,24},{48,32},{56,40},{1,49}... | collective-permute-start | bytes 737288 | tf_op jit(solution)/shard_map/ppermute | solution.py:64
  197.6 8.8 %collective-permute-start.11 = (f32[96,640]{1,0:T(8,128)S(1)}, f32[96,640]{1,0:T(8,128)S(1)}, u32[]{:S(2)}, u32[]{:S(2)}) collective-permute-start(f32[96,640]{1,0:T(8,128)S(1)} %dynamic-slice_bitcast_fusion.5), channel_id=1, source_target_pairs={{0,16},{8,24},{16,32},{24,40},{32,48},{40,56},{48,0},{56,8},{1,17}... | collective-permute-start | bytes 737288 | tf_op jit(solution)/shard_map/ppermute | solution.py:63
  197.7 16.8 %collective-permute-start.9 = (f32[96,1280]{1,0:T(8,128)S(1)}, f32[96,1280]{1,0:T(8,128)S(1)}, u32[]{:S(2)}, u32[]{:S(2)}) collective-permute-start(f32[96,1280]{1,0:T(8,128)S(1)} %fusion.28), channel_id=1, source_target_pairs={{0,64},{64,0},{1,65},{65,1},{2,66},{66,2},{3,67},{67,3},{4,68},{68... | collective-permute-start | bytes 1474568 | tf_op jit(solution)/shard_map/ppermute | solution.py:77
  203.1 7.4 %collective-permute-start.15 = (f32[96,640]{1,0:T(8,128)S(1)}, f32[96,640]{1,0:T(8,128)S(1)}, u32[]{:S(2)}, u32[]{:S(2)}) collective-permute-start(f32[96,640]{1,0:T(8,128)S(1)} %bitcast_add_fusion.10), channel_id=1, source_target_pairs={{0,48},{8,56},{16,0},{24,8},{32,16},{40,24},{48,32},{56,40},{1,49}... | collective-permute-start | bytes 737288 | tf_op jit(solution)/shard_map/ppermute | solution.py:64
  206.4 7.9 %collective-permute-start.12 = (f32[96,640]{1,0:T(8,128)S(1)}, f32[96,640]{1,0:T(8,128)S(1)}, u32[]{:S(2)}, u32[]{:S(2)}) collective-permute-start(f32[96,640]{1,0:T(8,128)S(1)} %bitcast_add_fusion.13), channel_id=1, source_target_pairs={{0,16},{8,24},{16,32},{24,40},{32,48},{40,56},{48,0},{56,8},{1,17}... | collective-permute-start | bytes 737288 | tf_op jit(solution)/shard_map/ppermute | solution.py:63
  210.6 7.5 %collective-permute-start.16 = (f32[96,640]{1,0:T(8,128)S(1)}, f32[96,640]{1,0:T(8,128)S(1)}, u32[]{:S(2)}, u32[]{:S(2)}) collective-permute-start(f32[96,640]{1,0:T(8,128)S(1)} %bitcast_add_fusion.9), channel_id=1, source_target_pairs={{0,48},{8,56},{16,0},{24,8},{32,16},{40,24},{48,32},{56,40},{1,49}... | collective-permute-start | bytes 737288 | tf_op jit(solution)/shard_map/ppermute | solution.py:64
  214.4 14.3 %copy-start.13 = (f32[96,1,192]{2,0,1:T(8,128)S(1)}, f32[96,1,192]{2,0,1:T(8,128)}, u32[]{:S(2)}) copy-start(f32[96,1,192]{2,0,1:T(8,128)} %convolution_bitcast_fusion.1) | copy-start | bytes 221188
  214.4 14.3 %copy-start.14 = (f32[96,1,192]{2,0,1:T(8,128)S(1)}, f32[96,1,192]{2,0,1:T(8,128)}, u32[]{:S(2)}) copy-start(f32[96,1,192]{2,0,1:T(8,128)} %convolution_bitcast_fusion.2) | copy-start | bytes 221188
  214.4 7.5 %collective-permute-start.13 = (f32[96,640]{1,0:T(8,128)S(1)}, f32[96,640]{1,0:T(8,128)S(1)}, u32[]{:S(2)}, u32[]{:S(2)}) collective-permute-start(f32[96,640]{1,0:T(8,128)S(1)} %bitcast_add_fusion.12), channel_id=1, source_target_pairs={{0,16},{8,24},{16,32},{24,40},{32,48},{40,56},{48,0},{56,8},{1,17}... | collective-permute-start | bytes 737288 | tf_op jit(solution)/shard_map/ppermute | solution.py:63
  224.1 14.1 %all-to-all-start.4 = ((f32[128,1,1]{2,1,0:T(1,128)}), f32[128,1,1]{2,1,0:T(1,128)S(1)}, u32[]{:S(2)}, u32[]{:S(2)}) async-start(f32[128,1,1]{2,1,0:T(1,128)} %broadcast_in_dim.18), calls=%async_computation.4 | async-start | bytes 131072 | tf_op jit(solution)/shard_map/all_to_all | solution.py:197
